TPU v7x, 32 devices: a whole 2x2x4 slice. The times are simulated.
32 devices in a mesh: groups: 2 (over x), slot: 16 (over z, y, core).
Axes of the slice: x: 2, y: 2, z: 4, core: 2. Of those that a mesh axis runs over, the one named last changes fastest.
Arguments:
- timesteps: int32 [32], P(('groups', 'slot')), parts along dimension 0, may hold values from 50 to 799
- prompt_ids: int32 [154], P('groups'), parts along dimension 0, may hold values from 0 to 49407
- start_latent: float32 [8, 4, 2, 128], P('groups'), parts along dimension 0, may hold values from -6 to 6
- iterate: float32 [32, 4, 4, 2, 128], P(('groups', 'slot')), parts along dimension 0, may hold values from -6 to 6
- fresh_noise: float32 [32, 4, 4, 2, 128], P(('groups', 'slot')), parts along dimension 0, may hold values from -6 to 6
- token_table: bfloat16 [49408, 1024], P('slot'), may hold values from -6 to 6
- empty_text: float32 [1024], replicated, may hold values from -6 to 6
- time_in: bfloat16 [320, 1280], replicated, may hold values from -0.3125 to 0.3125
- time_out: bfloat16 [1280, 320], replicated, may hold values from -0.15625 to 0.15625
- text_proj: bfloat16 [1024, 320], replicated, may hold values from -0.1875 to 0.1875
- conv_first: bfloat16 [9, 320, 4], replicated, may hold values from -1 to 1
- spatial_weights: bfloat16 [2, 9, 320, 320], replicated, may hold values from -0.109375 to 0.109375
- temporal_weights: bfloat16 [2, 3, 320, 320], replicated, may hold values from -0.1875 to 0.1875
- conv_last: bfloat16 [9, 4, 320], replicated, may hold values from -0.109375 to 0.109375
Outputs:
- new_iterate: float32 [32, 4, 4, 2, 128], P(('groups', 'slot')), parts along dimension 0
- final_latent: float32 [8, 4, 2, 128], P('groups'), parts along dimension 0
There are 2 independent parts, one for each index of `groups`. A program takes and returns all parts, laid end to end along the dimension named above; an argument that names none is the same for every part. Nothing has to cross between parts.
All inputs are finite; a program needn't handle non-finite values.
Results may differ from a plain program's by a relative error of at most 0.012.
Values sent between devices are 32-bit elements; how exact they have to be, the bound alone decides.
No kernel may reach another device: no remote copies, remote signals or barrier semaphores. Data moves between devices by JAX's collectives and lax.ppermute only.
A program may use at most 64 MiB of HBM per device.

v0:
```python
import jax
import jax.numpy as jnp
from jax import lax
from jax.sharding import PartitionSpec as P
from jax.experimental import pallas as pl
from jax.experimental.pallas import tpu as pltpu

GROUPS = 32
DT = 50


NORM_EPS = 1e-05
GUIDANCE_SCALE = 5.0


def alpha_bar(step_value):
    phase_angle = (step_value / 1000.0 + 0.008) / 1.008 * (jnp.pi / 2.0)
    cosine = jnp.cos(phase_angle)
    return cosine * cosine


def layer_norm(values):
    average = jnp.mean(values)
    spread = jnp.mean((values - average) ** 2)
    return (values - average) * lax.rsqrt(spread + NORM_EPS)


def group_norm(values, axes):
    batch, channels = (values.shape[0], values.shape[1])
    shaped = values.reshape((batch, GROUPS, channels // GROUPS) + values.shape[2:])
    average = jnp.mean(shaped, axis=axes, keepdims=True)
    spread = jnp.mean((shaped - average) ** 2, axis=axes, keepdims=True)
    return ((shaped - average) * lax.rsqrt(spread + NORM_EPS)).reshape(values.shape)


def shift_columns(inputs, offset):
    if offset == 0:
        return inputs
    blank = jnp.zeros(inputs.shape[:-1] + (1,), inputs.dtype)
    if offset == 1:
        return jnp.concatenate([inputs[..., 1:], blank], axis=-1)
    return jnp.concatenate([blank, inputs[..., :-1]], axis=-1)


def conv_space(inputs, weight):
    row_count = inputs.shape[3]
    result = None
    for col_step in range(3):
        moved = shift_columns(inputs, col_step - 1)
        padded = jnp.pad(moved, ((0, 0), (0, 0), (0, 0), (1, 1), (0, 0)))
        for row_step in range(3):
            window = padded[:, :, :, row_step : row_step + row_count]
            term = jnp.einsum(
                "oc,bcfrw->bofrw",
                weight[row_step * 3 + col_step],
                window,
                preferred_element_type=jnp.float32,
            )
            result = term if result is None else result + term
    return result


def conv_time(inputs, weight):
    padded = jnp.pad(inputs, ((0, 0), (0, 0), (1, 1), (0, 0), (0, 0)))
    frame_count = inputs.shape[2]
    result = None
    for tap_index in range(3):
        window = padded[:, :, tap_index : tap_index + frame_count]
        term = jnp.einsum(
            "oc,bcfrw->bofrw", weight[tap_index], window, preferred_element_type=jnp.float32
        )
        result = term if result is None else result + term
    return result


def unet_body(state_ref, wsp_ref, wt_ref, same_ref, batch_ref, out_ref):
    rows, blocks, cols, chans = state_ref.shape
    frames = blocks // 2
    same = same_ref[...]
    batch_mix = batch_ref[...]
    hi = lax.Precision.HIGHEST

    def group_stats(sums, count, mix):
        if mix is not None:
            sums = jnp.dot(mix, sums, precision=hi, preferred_element_type=jnp.float32)
        return jnp.dot(sums, same, precision=hi, preferred_element_type=jnp.float32) / count

    def norm_silu(x, mix, count):
        colsum = jnp.sum(x[0], axis=1) + jnp.sum(x[1], axis=1)
        mean = group_stats(colsum, count, mix)
        d = x - mean[None, :, None, :]
        sq = d * d
        var = group_stats(jnp.sum(sq[0], axis=1) + jnp.sum(sq[1], axis=1), count, mix)
        v = d * lax.rsqrt(var + NORM_EPS)[None, :, None, :]
        return (v / (1.0 + jnp.exp(-v))).astype(jnp.bfloat16)

    def mm(a, w):
        return lax.dot_general(a, w, (((1,), (1,)), ((), ())), preferred_element_type=jnp.float32)

    col = lax.broadcasted_iota(jnp.int32, (blocks, cols, chans), 1)

    def conv_sp(n, section):
        x0 = n[0].reshape(blocks * cols, chans)
        x1 = n[1].reshape(blocks * cols, chans)
        outs = []
        for row in range(rows):
            own, other = (x0, x1) if row == 0 else (x1, x0)
            other_dr = 1 if row == 0 else -1
            acc = None
            for dc in (-1, 0, 1):
                y = mm(own, wsp_ref[section, 3 + dc + 1]) + mm(other, wsp_ref[section, (other_dr + 1) * 3 + dc + 1])
                y = y.reshape(blocks, cols, chans)
                if dc == -1:
                    y = jnp.where(col == 0, 0.0, pltpu.roll(y, 1, 1))
                elif dc == 1:
                    y = jnp.where(col == cols - 1, 0.0, pltpu.roll(y, cols - 1, 1))
                acc = y if acc is None else acc + y
            outs.append(acc)
        return jnp.stack(outs)

    def conv_tm(n, section):
        n5 = n.reshape(rows, 2, frames, cols, chans)
        blank = jnp.zeros((rows, 2, 1, cols, chans), n.dtype)
        before = jnp.concatenate([blank, n5[:, :, :-1]], axis=2)
        after = jnp.concatenate([n5[:, :, 1:], blank], axis=2)
        flat = rows * blocks * cols
        acc = mm(before.reshape(flat, chans), wt_ref[section, 0])
        acc = acc + mm(n.reshape(flat, chans), wt_ref[section, 1])
        acc = acc + mm(after.reshape(flat, chans), wt_ref[section, 2])
        return acc.reshape(rows, blocks, cols, chans)

    per_frame = float(chans // GROUPS * rows * cols)
    per_sample = per_frame * frames
    state = state_ref[...]
    for section in range(wsp_ref.shape[0]):
        x = state.astype(jnp.float32)
        normed = norm_silu(x, None, per_frame)
        state = (x + conv_sp(normed, section)).astype(jnp.bfloat16)
        x = state.astype(jnp.float32)
        normed = norm_silu(x, batch_mix, per_sample)
        state = (x + conv_tm(normed, section)).astype(jnp.bfloat16)
    out_ref[...] = norm_silu(state.astype(jnp.float32), None, per_frame)


def unet_sections(state, spatial_weights, temporal_weights):
    rows, blocks, cols, chans = state.shape
    group = jnp.arange(chans) // (chans // GROUPS)
    same = (group[:, None] == group[None, :]).astype(jnp.float32)
    block_of = jnp.arange(blocks) // (blocks // 2)
    batch_mix = (block_of[:, None] == block_of[None, :]).astype(jnp.float32)
    return pl.pallas_call(
        unet_body,
        out_shape=jax.ShapeDtypeStruct(state.shape, jnp.bfloat16),
        compiler_params=pltpu.CompilerParams(vmem_limit_bytes=100 * 1024 * 1024 // 2),
    )(state, spatial_weights, temporal_weights, same, batch_mix)


def butterfly_sum(x, axis):
    peers = lax.axis_size(axis)
    if peers & (peers - 1):
        return jnp.sum(lax.all_gather(x, axis), axis=0)
    k = 1
    while k < peers:
        x = x + lax.ppermute(x, axis, [(i, i ^ k) for i in range(peers)])
        k *= 2
    return x


def butterfly_scan(x, axis):
    peers, me = lax.axis_size(axis), lax.axis_index(axis)
    if peers & (peers - 1):
        everything = lax.all_gather(x, axis)
        lower = (jnp.arange(peers) < me).reshape((peers,) + (1,) * x.ndim)
        return jnp.sum(jnp.where(lower, everything, 0.0), axis=0), jnp.sum(everything, axis=0)
    total, before = x, jnp.zeros_like(x)
    k = 1
    while k < peers:
        got = lax.ppermute(total, axis, [(i, i ^ k) for i in range(peers)])
        before = jnp.where((me & k) != 0, before + got, before)
        total = total + got
        k *= 2
    return before, total


def local(
    timesteps,
    prompt_ids,
    start_latent,
    iterate,
    fresh_noise,
    token_table,
    empty_text,
    time_in,
    time_out,
    text_proj,
    conv_first,
    spatial_weights,
    temporal_weights,
    conv_last,
):
    shard_rows = token_table.shape[0]
    first_row = lax.axis_index("slot") * shard_rows
    local_ids = prompt_ids - first_row
    held = (local_ids >= 0) & (local_ids < shard_rows)
    rows = token_table[jnp.clip(local_ids, 0, shard_rows - 1)].astype(jnp.float32)
    partial = jnp.sum(jnp.where(held[:, None], rows, 0.0), axis=0)
    pooled = butterfly_sum(partial, "slot") / prompt_ids.shape[0]
    text_pair = jnp.stack([layer_norm(pooled), layer_norm(empty_text)]).astype(jnp.bfloat16)
    text_vector = jnp.dot(text_pair, text_proj, preferred_element_type=jnp.float32)
    half_width = time_in.shape[0] // 2
    frequency = jnp.exp(-jnp.log(10000.0) * jnp.arange(half_width, dtype=jnp.float32) / half_width)
    step_value = timesteps[0].astype(jnp.float32)
    angles = step_value * frequency
    feature = jnp.concatenate([jnp.cos(angles), jnp.sin(angles)]).astype(jnp.bfloat16)[None, :]
    hidden = jax.nn.silu(jnp.dot(feature, time_in, preferred_element_type=jnp.float32)).astype(
        jnp.bfloat16
    )
    time_vector = jnp.dot(hidden, time_out, preferred_element_type=jnp.float32)
    embedding = text_vector + time_vector
    latent = iterate[0]
    state = (
        conv_space(latent.astype(jnp.bfloat16)[None], conv_first)
        + embedding[:, :, None, None, None]
    ).astype(jnp.bfloat16)
    batch, chans, frames, rows, cols = state.shape
    laid = state.transpose(3, 0, 2, 4, 1).reshape(rows, batch * frames, cols, chans)
    normed = unet_sections(laid, spatial_weights, temporal_weights)
    normed = normed.reshape(rows, batch, frames, cols, chans).transpose(1, 4, 2, 0, 3)
    predicted = conv_space(normed, conv_last)
    guided = predicted[1] + GUIDANCE_SCALE * (predicted[0] - predicted[1])
    alpha_now = alpha_bar(step_value)
    alpha_prev = alpha_bar(step_value - DT)
    scale_ratio = jnp.sqrt(alpha_prev / alpha_now)
    noise_square = (1.0 - alpha_prev) * (1.0 - alpha_now / alpha_prev) / (1.0 - alpha_now)
    kept_square = (1.0 - alpha_prev) * (alpha_now / alpha_prev - alpha_now) / (1.0 - alpha_now)
    eps_factor = jnp.sqrt(kept_square) - scale_ratio * jnp.sqrt(1.0 - alpha_now)
    drift_term = (
        (scale_ratio - 1.0) * latent + eps_factor * guided + jnp.sqrt(noise_square) * fresh_noise[0]
    )[None]
    earlier, total_drift = butterfly_scan(drift_term[0], "slot")
    new_iterate = start_latent[None] + earlier[None]
    final_latent = start_latent + total_drift
    return (new_iterate, final_latent)


def solution(mesh):
    placed = (
        P(("groups", "slot")),
        P("groups"),
        P("groups", None, None, None),
        P(("groups", "slot"), None, None, None, None),
        P(("groups", "slot"), None, None, None, None),
        P("slot", None),
        P(),
        P(),
        P(),
        P(),
        P(),
        P(),
        P(),
        P(),
    )
    return jax.shard_map(
        local,
        mesh=mesh,
        in_specs=placed,
        out_specs=(P(("groups", "slot"), None, None, None, None), P("groups", None, None, None)),
        check_vma=False,
    )
```

profile of v0, /device:TPU:0, one launch (start us, length us, event | category | flops | bytes accessed | tf_op | source)
XLA Modules:
  0.0 88.3 jit_solution(2382317831484278849)
XLA Ops:
  0.7 0.7 compare_select_fusion
  1.4 0.7 compare_and_fusion
  2.1 4.5 %gather_fusion = bf16[77,1024]{1,0:T(8,128)(2,1)S(1)} fusion(bf16[3088,1024]{1,0:T(8,128)(2,1)} %param.19, s32[1024]{0:T(1024)S(1)} %pad_clamp_fusion), kind=kCustom, calls=%fused_computation | custom fusion | bytes 315700 | tf_op jit(solution)/shard_map/gather | solution.py:205
  6.7 0.5 collective-permute-start
  8.2 0.6 reduce_sum.48
  9.5 0.6 multiply_reduce_fusion
  13.9 1.4 %fusion = f32[2,4,128,320]{2,3,0,1:T(8,128)} fusion(f32[4,2,128,320]{2,3,1,0:T(8,128)S(1)} %convolution_add_fusion.1, bf16[1,4,4,2,128]{4,1,3,2,0:T(4,128)(2,1)S(1)} %concatenate.18, bf16[9,320,4]{1,2,0:T(4,128)(2,1)S(1)} %copy-done.9), kind=kOutput, calls=%fused_computation.3 | convolution fusion | flops 2949120 | bytes 2632704 | tf_op jit(solution)/shard_map/oc,bcfrw->bofrw/dot_general | solution.py:53
  15.4 2.6 %collective-permute-start.1 = (f32[1024]{0:T(1024)S(1)}, f32[1024]{0:T(1024)S(1)}, u32[]{:S(2)}, u32[]{:S(2)}) collective-permute-start(f32[1024]{0:T(1024)S(1)} %add.234), channel_id=1, source_target_pairs={{0,2},{1,3},{2,0},{3,1},{4,6},{5,7},{6,4},{7,5},{8,10},{9,11},{10,... | collective-permute-start | bytes 12296 | tf_op jit(solution)/shard_map/ppermute | solution.py:164
  18.0 1.6 %collective-permute-done.1 = f32[1024]{0:T(1024)S(1)} collective-permute-done((f32[1024]{0:T(1024)S(1)}, f32[1024]{0:T(1024)S(1)}, u32[]{:S(2)}, u32[]{:S(2)}) %collective-permute-start.1) | collective-permute-done | bytes 4128 | tf_op jit(solution)/shard_map/ppermute | solution.py:164
  19.6 2.1 %collective-permute-start.2 = (f32[1024]{0:T(1024)S(1)}, f32[1024]{0:T(1024)S(1)}, u32[]{:S(2)}, u32[]{:S(2)}) collective-permute-start(f32[1024]{0:T(1024)S(1)} %add.235), channel_id=1, source_target_pairs={{0,4},{1,5},{2,6},{3,7},{4,0},{5,1},{6,2},{7,3},{8,12},{9,13},{10,... | collective-permute-start | bytes 12296 | tf_op jit(solution)/shard_map/ppermute | solution.py:164
  21.8 1.5 %collective-permute-done.2 = f32[1024]{0:T(1024)S(1)} collective-permute-done((f32[1024]{0:T(1024)S(1)}, f32[1024]{0:T(1024)S(1)}, u32[]{:S(2)}, u32[]{:S(2)}) %collective-permute-start.2) | collective-permute-done | bytes 4128 | tf_op jit(solution)/shard_map/ppermute | solution.py:164
  23.3 3.0 %collective-permute-start.3 = (f32[1024]{0:T(1024)S(1)}, f32[1024]{0:T(1024)S(1)}, u32[]{:S(2)}, u32[]{:S(2)}) collective-permute-start(f32[1024]{0:T(1024)S(1)} %add.236), channel_id=1, source_target_pairs={{0,8},{1,9},{2,10},{3,11},{4,12},{5,13},{6,14},{7,15},{8,0},{9,1},... | collective-permute-start | bytes 12296 | tf_op jit(solution)/shard_map/ppermute | solution.py:164
  26.3 0.9 %convolution_reduce_fusion.1 = f32[320]{0:T(512)} fusion(bf16[1280,1]{0,1:T(2,128)(2,1)S(1)} %reshape.159, bf16[1280,320]{0,1:T(8,128)(2,1)S(1)} %copy-done.3), kind=kOutput, calls=%fused_computation.22 | convolution fusion | flops 819200 | bytes 823040 | tf_op jit(solution)/shard_map/dot_general | solution.py:218
  27.5 1.8 %copy.18 = f32[2,4,128,320]{3,2,1,0:T(8,128)S(1)} copy(f32[2,4,128,320]{2,3,0,1:T(8,128)} %fusion) | data formatting | bytes 2621440 | tf_op jit(solution)/shard_map/add | solution.py:222
  29.7 0.6 fusion.95
  30.9 0.6 multiply_reduce_fusion.1
  32.3 1.0 %convolution_add_fusion.14 = f32[2,320]{1,0:T(2,128)S(1)} fusion(bf16[1024,320]{0,1:T(8,128)(2,1)S(1)} %copy-done.4, bf16[1,1024]{1,0:T(2,128)(2,1)S(1)} %stack.13, bf16[1,1024]{1,0:T(2,128)(2,1)S(1)} %stack.12, f32[320]{0:T(512)} %convolution_reduce_fusion.1), kind=kOutput, calls=%fused_computation.21 | convolution fusion | flops 1319552 | bytes 663296 | tf_op jit(solution)/shard_map/dot_general | solution.py:209
  33.6 1.5 %add_convert_fusion.state_ref = bf16[2,8,128,320]{3,2,1,0:T(8,128)(2,1)} fusion(f32[2,8,128,320]{3,2,1,0:T(8,128)S(1)} %bitcast.204, f32[8,320]{1,0:T(8,128)S(1)} %add.244), kind=kLoop, calls=%fused_computation.1 | loop fusion | flops 1310720 | bytes 3942400 | tf_op jit(solution)/shard_map/convert_element_type | solution.py:224
  35.1 31.3 %shard_map.149 = bf16[2,8,128,320]{3,2,1,0:T(8,128)(2,1)S(1)} custom-call(bf16[2,8,128,320]{3,2,1,0:T(8,128)(2,1)} %add_convert_fusion.state_ref, bf16[2,9,320,320]{3,2,1,0:T(8,128)(2,1)} %wsp_ref.1, bf16[2,3,320,320]{3,2,1,0:T(8,128)(2,1)S(1)} %copy-done.1, f32[320,320]{1,0:T(8,128)S(1)} %compare_convert_fusion.same_ref, ...), custom_call_target="tpu_custom_call" | custom-call | tf_op jit(solution)/shard_map/pallas_call | solution.py:151
  66.4 1.6 %copy.19 = bf16[2,2,4,128,320]{3,4,0,2,1:T(8,128)(2,1)} copy(bf16[2,2,4,128,320]{4,3,2,1,0:T(8,128)(2,1)S(1)} %bitcast.202) | data formatting | bytes 2621440 | tf_op jit(solution)/shard_map/reshape | solution.py:228
  68.0 2.4 %fusion.98 = (bf16[2,320,4,2,127]{4,1,3,2,0:T(8,128)(2,1)S(1)}, bf16[2,320,4,2,127]{4,1,3,2,0:T(8,128)(2,1)S(1)}) fusion(bf16[2,320,4,2,128]{4,1,3,2,0:T(8,128)(2,1)} %bitcast.203), kind=kLoop, calls=%fused_computation.149 | loop fusion | bytes 5201920 | tf_op jit(solution)/shard_map/slice | solution.py:42
  70.7 0.6 fusion.9
  71.3 0.4 convolution_add_fusion.13
  73.7 1.2 %collective-permute-done.4 = f32[4,4,2,128]{3,0,2,1:T(4,128)S(1)} collective-permute-done((f32[4,4,2,128]{3,0,2,1:T(4,128)S(1)}, f32[4,4,2,128]{3,0,2,1:T(4,128)S(1)}, u32[]{:S(2)}, u32[]{:S(2)}) %collective-permute-start.4) | collective-permute-done | bytes 16416 | tf_op jit(solution)/shard_map/ppermute | solution.py:178
  74.9 1.5 %collective-permute-start.5 = (f32[4,4,2,128]{3,0,2,1:T(4,128)S(1)}, f32[4,4,2,128]{3,0,2,1:T(4,128)S(1)}, u32[]{:S(2)}, u32[]{:S(2)}) collective-permute-start(f32[4,4,2,128]{3,0,2,1:T(4,128)S(1)} %add.259), channel_id=1, source_target_pairs={{0,2},{1,3},{2,0},{3,1},{4,6},{5,7},{6,4},{7,5},{8,10},{9,11},{10,... | collective-permute-start | bytes 49160 | tf_op jit(solution)/shard_map/ppermute | solution.py:178
  76.4 2.2 %collective-permute-done.5 = f32[4,4,2,128]{3,0,2,1:T(4,128)S(1)} collective-permute-done((f32[4,4,2,128]{3,0,2,1:T(4,128)S(1)}, f32[4,4,2,128]{3,0,2,1:T(4,128)S(1)}, u32[]{:S(2)}, u32[]{:S(2)}) %collective-permute-start.5) | collective-permute-done | bytes 16416 | tf_op jit(solution)/shard_map/ppermute | solution.py:178
  78.6 1.6 %collective-permute-start.6 = (f32[4,4,2,128]{3,0,2,1:T(4,128)S(1)}, f32[4,4,2,128]{3,0,2,1:T(4,128)S(1)}, u32[]{:S(2)}, u32[]{:S(2)}) collective-permute-start(f32[4,4,2,128]{3,0,2,1:T(4,128)S(1)} %add.261), channel_id=1, source_target_pairs={{0,4},{1,5},{2,6},{3,7},{4,0},{5,1},{6,2},{7,3},{8,12},{9,13},{10,... | collective-permute-start | bytes 49160 | tf_op jit(solution)/shard_map/ppermute | solution.py:178
  80.2 2.2 %collective-permute-done.6 = f32[4,4,2,128]{3,0,2,1:T(4,128)S(1)} collective-permute-done((f32[4,4,2,128]{3,0,2,1:T(4,128)S(1)}, f32[4,4,2,128]{3,0,2,1:T(4,128)S(1)}, u32[]{:S(2)}, u32[]{:S(2)}) %collective-permute-start.6) | collective-permute-done | bytes 16416 | tf_op jit(solution)/shard_map/ppermute | solution.py:178
  82.4 1.2 %collective-permute-start.7 = (f32[4,4,2,128]{3,0,2,1:T(4,128)S(1)}, f32[4,4,2,128]{3,0,2,1:T(4,128)S(1)}, u32[]{:S(2)}, u32[]{:S(2)}) collective-permute-start(f32[4,4,2,128]{3,0,2,1:T(4,128)S(1)} %add.263), channel_id=1, source_target_pairs={{0,8},{1,9},{2,10},{3,11},{4,12},{5,13},{6,14},{7,15},{8,0},{9,1},... | collective-permute-start | bytes 49160 | tf_op jit(solution)/shard_map/ppermute | solution.py:178
  83.6 3.5 %collective-permute-done.7 = f32[4,4,2,128]{3,0,2,1:T(4,128)S(1)} collective-permute-done((f32[4,4,2,128]{3,0,2,1:T(4,128)S(1)}, f32[4,4,2,128]{3,0,2,1:T(4,128)S(1)}, u32[]{:S(2)}, u32[]{:S(2)}) %collective-permute-start.7) | collective-permute-done | bytes 16416 | tf_op jit(solution)/shard_map/ppermute | solution.py:178
  87.0 0.6 copy.23
  87.7 0.6 copy.24
  (73 shorter events, 6.5 us)
Async XLA Ops:
  0.6 7.3 %copy-start = (bf16[320,1280]{1,0:T(8,128)(2,1)S(1)}, bf16[320,1280]{1,0:T(8,128)(2,1)}, u32[]{:S(2)}) copy-start(bf16[320,1280]{1,0:T(8,128)(2,1)} %param.21) | copy-start | bytes 2457604
  0.6 7.6 %copy-start.7 = (f32[1024]{0:T(1024)S(1)}, f32[1024]{0:T(1024)}, u32[]{:S(2)}) copy-start(f32[1024]{0:T(1024)} %param.20) | copy-start | bytes 12292
  0.7 10.1 %copy-start.5 = (f32[1,4,4,2,128]{4,3,2,1,0:T(2,128)S(1)}, f32[1,4,4,2,128]{4,3,2,1,0:T(2,128)}, u32[]{:S(2)}) copy-start(f32[1,4,4,2,128]{4,3,2,1,0:T(2,128)} %param.17) | copy-start | bytes 49156
  0.7 10.3 %copy-start.9 = (bf16[9,320,4]{1,2,0:T(4,128)(2,1)S(1)}, bf16[9,320,4]{1,2,0:T(4,128)(2,1)}, u32[]{:S(2)}) copy-start(bf16[9,320,4]{1,2,0:T(4,128)(2,1)} %param.24) | copy-start | bytes 69124
  6.7 8.8 %collective-permute-start = (f32[1024]{0:T(1024)S(1)}, f32[1024]{0:T(1024)S(1)}, u32[]{:S(2)}, u32[]{:S(2)}) collective-permute-start(f32[1024]{0:T(1024)S(1)} %select_reduce_fusion), channel_id=1, source_target_pairs={{0,1},{1,0},{2,3},{3,2},{4,5},{5,4},{6,7},{7,6},{8,9},{9,8},{10,11... | collective-permute-start | bytes 12296 | tf_op jit(solution)/shard_map/ppermute | solution.py:164
  13.9 12.4 %copy-start.3 = (bf16[1280,320]{0,1:T(8,128)(2,1)S(1)}, bf16[1280,320]{0,1:T(8,128)(2,1)}, u32[]{:S(2)}) copy-start(bf16[1280,320]{0,1:T(8,128)(2,1)} %param.22) | copy-start | bytes 2457604
  15.4 4.2 %collective-permute-start.1 = (f32[1024]{0:T(1024)S(1)}, f32[1024]{0:T(1024)S(1)}, u32[]{:S(2)}, u32[]{:S(2)}) collective-permute-start(f32[1024]{0:T(1024)S(1)} %add.234), channel_id=1, source_target_pairs={{0,2},{1,3},{2,0},{3,1},{4,6},{5,7},{6,4},{7,5},{8,10},{9,11},{10,... | collective-permute-start | bytes 12296 | tf_op jit(solution)/shard_map/ppermute | solution.py:164
  19.6 3.7 %collective-permute-start.2 = (f32[1024]{0:T(1024)S(1)}, f32[1024]{0:T(1024)S(1)}, u32[]{:S(2)}, u32[]{:S(2)}) collective-permute-start(f32[1024]{0:T(1024)S(1)} %add.235), channel_id=1, source_target_pairs={{0,4},{1,5},{2,6},{3,7},{4,0},{5,1},{6,2},{7,3},{8,12},{9,13},{10,... | collective-permute-start | bytes 12296 | tf_op jit(solution)/shard_map/ppermute | solution.py:164
  23.3 6.4 %collective-permute-start.3 = (f32[1024]{0:T(1024)S(1)}, f32[1024]{0:T(1024)S(1)}, u32[]{:S(2)}, u32[]{:S(2)}) collective-permute-start(f32[1024]{0:T(1024)S(1)} %add.236), channel_id=1, source_target_pairs={{0,8},{1,9},{2,10},{3,11},{4,12},{5,13},{6,14},{7,15},{8,0},{9,1},... | collective-permute-start | bytes 12296 | tf_op jit(solution)/shard_map/ppermute | solution.py:164
  27.5 4.7 %copy-start.4 = (bf16[1024,320]{0,1:T(8,128)(2,1)S(1)}, bf16[1024,320]{0,1:T(8,128)(2,1)}, u32[]{:S(2)}) copy-start(bf16[1024,320]{0,1:T(8,128)(2,1)} %param.23) | copy-start | bytes 1966084
  33.6 1.5 %copy-start.1 = (bf16[2,3,320,320]{3,2,1,0:T(8,128)(2,1)S(1)}, bf16[2,3,320,320]{3,2,1,0:T(8,128)(2,1)}, u32[]{:S(2)}) copy-start(bf16[2,3,320,320]{3,2,1,0:T(8,128)(2,1)} %wt_ref.1) | copy-start | bytes 3686404
  68.0 2.5 %copy-start.2 = (bf16[2,2,4,128,320]{3,4,0,2,1:T(8,128)(2,1)S(1)}, bf16[2,2,4,128,320]{3,4,0,2,1:T(8,128)(2,1)}, u32[]{:S(2)}) copy-start(bf16[2,2,4,128,320]{3,4,0,2,1:T(8,128)(2,1)} %copy.19) | copy-start | bytes 3932164
  68.0 2.5 %copy-start.8 = (bf16[9,4,320]{2,1,0:T(4,128)(2,1)S(1)}, bf16[9,4,320]{2,1,0:T(4,128)(2,1)}, u32[]{:S(2)}) copy-start(bf16[9,4,320]{2,1,0:T(4,128)(2,1)} %param.27) | copy-start | bytes 69124
  72.9 0.7 copy-start.6
  72.9 0.7 copy-start.10
  72.9 14.1 %copy-start.11 = (f32[4,4,2,128]{3,2,1,0:T(2,128)S(1)}, f32[4,4,2,128]{3,2,1,0:T(2,128)}, u32[]{:S(2)}) copy-start(f32[4,4,2,128]{3,2,1,0:T(2,128)} %param.16) | copy-start | bytes 49156
  73.6 1.2 %collective-permute-start.4 = (f32[4,4,2,128]{3,0,2,1:T(4,128)S(1)}, f32[4,4,2,128]{3,0,2,1:T(4,128)S(1)}, u32[]{:S(2)}, u32[]{:S(2)}) collective-permute-start(f32[4,4,2,128]{3,0,2,1:T(4,128)S(1)} %fusion.19), channel_id=1, source_target_pairs={{0,1},{1,0},{2,3},{3,2},{4,5},{5,4},{6,7},{7,6},{8,9},{9,8},{10,11... | collective-permute-start | bytes 49160 | tf_op jit(solution)/shard_map/ppermute | solution.py:178
  74.9 3.7 %collective-permute-start.5 = (f32[4,4,2,128]{3,0,2,1:T(4,128)S(1)}, f32[4,4,2,128]{3,0,2,1:T(4,128)S(1)}, u32[]{:S(2)}, u32[]{:S(2)}) collective-permute-start(f32[4,4,2,128]{3,0,2,1:T(4,128)S(1)} %add.259), channel_id=1, source_target_pairs={{0,2},{1,3},{2,0},{3,1},{4,6},{5,7},{6,4},{7,5},{8,10},{9,11},{10,... | collective-permute-start | bytes 49160 | tf_op jit(solution)/shard_map/ppermute | solution.py:178
  78.6 3.7 %collective-permute-start.6 = (f32[4,4,2,128]{3,0,2,1:T(4,128)S(1)}, f32[4,4,2,128]{3,0,2,1:T(4,128)S(1)}, u32[]{:S(2)}, u32[]{:S(2)}) collective-permute-start(f32[4,4,2,128]{3,0,2,1:T(4,128)S(1)} %add.261), channel_id=1, source_target_pairs={{0,4},{1,5},{2,6},{3,7},{4,0},{5,1},{6,2},{7,3},{8,12},{9,13},{10,... | collective-permute-start | bytes 49160 | tf_op jit(solution)/shard_map/ppermute | solution.py:178
  82.4 4.6 %collective-permute-start.7 = (f32[4,4,2,128]{3,0,2,1:T(4,128)S(1)}, f32[4,4,2,128]{3,0,2,1:T(4,128)S(1)}, u32[]{:S(2)}, u32[]{:S(2)}) collective-permute-start(f32[4,4,2,128]{3,0,2,1:T(4,128)S(1)} %add.263), channel_id=1, source_target_pairs={{0,8},{1,9},{2,10},{3,11},{4,12},{5,13},{6,14},{7,15},{8,0},{9,1},... | collective-permute-start | bytes 49160 | tf_op jit(solution)/shard_map/ppermute | solution.py:178
where the time goes:
time: 88.6 us; the launch traced here: 88.3 us
  Pallas kernels  31.3 us (35%)
  starting transfers between devices  12.6 us (14%)
  local copies, waits for them, and re-layouts  12.4 us (14%)
  waiting for transfers between devices  12.1 us (14%)
  matrix products  9.25 us (10%)
  other arithmetic  5.85 us (7%)
  between operations  4.85 us (5%)
    pallas_call x1, Pallas kernels, unet_sections(): pl.pallas_call(unet_body, out_shape=jax.ShapeDtypeStruct(state.shape, jnp...  31.3 us
    ppermute x4, waiting for transfers between devices, butterfly_scan(): got = lax.ppermute(total, axis, [(i, i ^ k) for i in range(peers)])  9.03 us
    ppermute x4, starting transfers between devices, butterfly_sum(): x = x + lax.ppermute(x, axis, [(i, i ^ k) for i in range(peers)])  8.23 us
    dot_general x18, matrix products, conv_space(): jnp.einsum('oc,bcfrw->bofrw', weight[row_step * 3 + col_step], window, pr...  7.12 us
    gather x1, local copies, waits for them, and re-layouts, local(): token_table[jnp.clip(local_ids, 0, shard_rows - 1)].astype(jnp.float32)  4.45 us
    ppermute x4, starting transfers between devices, butterfly_scan(): got = lax.ppermute(total, axis, [(i, i ^ k) for i in range(peers)])  4.33 us
    ppermute x4, waiting for transfers between devices, butterfly_sum(): x = x + lax.ppermute(x, axis, [(i, i ^ k) for i in range(peers)])  3.1 us
    slice x1, local copies, waits for them, and re-layouts, shift_columns(): return jnp.concatenate([blank, inputs[..., :-1]], axis=-1)  2.44 us
  transfers between devices with their start and end apart: 8, of which 6 were waited for; matrix products, arithmetic and copies ran while one was open for 10% of the time, Pallas kernels for 0%

commit v1 on v0

--- a/solution.py
+++ b/solution.py
@@ -92,7 +92,7 @@
         sq = d * d
         var = group_stats(jnp.sum(sq[0], axis=1) + jnp.sum(sq[1], axis=1), count, mix)
         v = d * lax.rsqrt(var + NORM_EPS)[None, :, None, :]
-        return (v / (1.0 + jnp.exp(-v))).astype(jnp.bfloat16)
+        return (v * (0.5 + 0.5 * jnp.tanh(0.5 * v))).astype(jnp.bfloat16)
 
     def mm(a, w):
         return lax.dot_general(a, w, (((1,), (1,)), ((), ())), preferred_element_type=jnp.float32)
@@ -201,9 +201,9 @@
     shard_rows = token_table.shape[0]
     first_row = lax.axis_index("slot") * shard_rows
     local_ids = prompt_ids - first_row
-    held = (local_ids >= 0) & (local_ids < shard_rows)
-    rows = token_table[jnp.clip(local_ids, 0, shard_rows - 1)].astype(jnp.float32)
-    partial = jnp.sum(jnp.where(held[:, None], rows, 0.0), axis=0)
+    hits = local_ids[:, None] == jnp.arange(shard_rows, dtype=jnp.int32)[None, :]
+    counts = jnp.sum(hits.astype(jnp.float32), axis=0).astype(jnp.bfloat16)[None]
+    partial = jnp.dot(counts, token_table, preferred_element_type=jnp.float32)[0]
     pooled = butterfly_sum(partial, "slot") / prompt_ids.shape[0]
     text_pair = jnp.stack([layer_norm(pooled), layer_norm(empty_text)]).astype(jnp.bfloat16)
     text_vector = jnp.dot(text_pair, text_proj, preferred_element_type=jnp.float32)

time: 88.6 us -> 87.3 us (0.985)
  local copies, waits for them, and re-layouts: 12.4 us -> 7.94 us
  matrix products: 9.25 us -> 13 us
    gather x1 -> x0, local copies, waits for them, and re-layouts: 4.45 us -> none  [local(): token_table[jnp.clip(local_ids, 0, shard_rows - 1)].astype(jnp.float32)]
    dot_general x0 -> x1, matrix products: none -> 3.73 us  [local(): jnp.dot(counts, token_table, preferred_element_type=jnp.float32)[0]]
where the time goes in v1:
time: 87.3 us; the launch traced here: 87 us
  Pallas kernels  31.3 us (36%)
  matrix products  13 us (15%)
  starting transfers between devices  12.5 us (14%)
  waiting for transfers between devices  12.1 us (14%)
  local copies, waits for them, and re-layouts  7.94 us (9%)
  other arithmetic  5.28 us (6%)
  between operations  4.85 us (6%)
    pallas_call x1, Pallas kernels, unet_sections(): pl.pallas_call(unet_body, out_shape=jax.ShapeDtypeStruct(state.shape, jnp...  31.3 us
    ppermute x4, waiting for transfers between devices, butterfly_scan(): got = lax.ppermute(total, axis, [(i, i ^ k) for i in range(peers)])  9.03 us
    ppermute x4, starting transfers between devices, butterfly_sum(): x = x + lax.ppermute(x, axis, [(i, i ^ k) for i in range(peers)])  8.16 us
    dot_general x18, matrix products, conv_space(): jnp.einsum('oc,bcfrw->bofrw', weight[row_step * 3 + col_step], window, pr...  7.11 us
    ppermute x4, starting transfers between devices, butterfly_scan(): got = lax.ppermute(total, axis, [(i, i ^ k) for i in range(peers)])  4.33 us
    dot_general x1, matrix products, local(): jnp.dot(counts, token_table, preferred_element_type=jnp.float32)[0]  3.73 us
    ppermute x4, waiting for transfers between devices, butterfly_sum(): x = x + lax.ppermute(x, axis, [(i, i ^ k) for i in range(peers)])  3.1 us
    slice x1, local copies, waits for them, and re-layouts, shift_columns(): return jnp.concatenate([blank, inputs[..., :-1]], axis=-1)  2.44 us
  transfers between devices with their start and end apart: 8, of which 6 were waited for; matrix products, arithmetic and copies ran while one was open for 10% of the time, Pallas kernels for 0%

profile of v1, /device:TPU:0, one launch (start us, length us, event | category | flops | bytes accessed | tf_op | source)
XLA Modules:
  0.0 87.0 jit_solution(9373102002755641052)
XLA Ops:
  0.6 0.7 broadcast_subtract_fusion
  1.6 3.7 %fusion.102 = f32[1,1024]{1,0:T(1,128)S(1)} fusion(bf16[3088,1]{0,1:T(2,128)(2,1)S(1)} %reshape.153, bf16[3088,1024]{1,0:T(8,128)(2,1)} %param.19), kind=kOutput, calls=%fused_computation.151 | convolution fusion | flops 6324224 | bytes 6334496 | tf_op jit(solution)/shard_map/dot_general | solution.py:206
  5.4 0.5 collective-permute-start
  6.9 0.6 reduce_sum.48
  8.2 0.6 multiply_reduce_fusion
  11.8 0.4 convolution_add_fusion.2
  12.6 1.4 %fusion = f32[2,4,128,320]{2,3,0,1:T(8,128)} fusion(f32[4,2,128,320]{2,3,1,0:T(8,128)S(1)} %convolution_add_fusion.1, bf16[1,4,4,2,128]{4,1,3,2,0:T(4,128)(2,1)S(1)} %concatenate.18, bf16[9,320,4]{1,2,0:T(4,128)(2,1)S(1)} %copy-done.9), kind=kOutput, calls=%fused_computation.2 | convolution fusion | flops 2949120 | bytes 2632704 | tf_op jit(solution)/shard_map/oc,bcfrw->bofrw/dot_general | solution.py:53
  14.1 2.6 %collective-permute-start.1 = (f32[1024]{0:T(1024)S(1)}, f32[1024]{0:T(1024)S(1)}, u32[]{:S(2)}, u32[]{:S(2)}) collective-permute-start(f32[1024]{0:T(1024)S(1)} %add.230), channel_id=1, source_target_pairs={{0,2},{1,3},{2,0},{3,1},{4,6},{5,7},{6,4},{7,5},{8,10},{9,11},{10,... | collective-permute-start | bytes 12296 | tf_op jit(solution)/shard_map/ppermute | solution.py:164
  16.7 1.6 %collective-permute-done.1 = f32[1024]{0:T(1024)S(1)} collective-permute-done((f32[1024]{0:T(1024)S(1)}, f32[1024]{0:T(1024)S(1)}, u32[]{:S(2)}, u32[]{:S(2)}) %collective-permute-start.1) | collective-permute-done | bytes 4128 | tf_op jit(solution)/shard_map/ppermute | solution.py:164
  18.3 2.1 %collective-permute-start.2 = (f32[1024]{0:T(1024)S(1)}, f32[1024]{0:T(1024)S(1)}, u32[]{:S(2)}, u32[]{:S(2)}) collective-permute-start(f32[1024]{0:T(1024)S(1)} %add.231), channel_id=1, source_target_pairs={{0,4},{1,5},{2,6},{3,7},{4,0},{5,1},{6,2},{7,3},{8,12},{9,13},{10,... | collective-permute-start | bytes 12296 | tf_op jit(solution)/shard_map/ppermute | solution.py:164
  20.4 1.5 %collective-permute-done.2 = f32[1024]{0:T(1024)S(1)} collective-permute-done((f32[1024]{0:T(1024)S(1)}, f32[1024]{0:T(1024)S(1)}, u32[]{:S(2)}, u32[]{:S(2)}) %collective-permute-start.2) | collective-permute-done | bytes 4128 | tf_op jit(solution)/shard_map/ppermute | solution.py:164
  21.9 3.0 %collective-permute-start.3 = (f32[1024]{0:T(1024)S(1)}, f32[1024]{0:T(1024)S(1)}, u32[]{:S(2)}, u32[]{:S(2)}) collective-permute-start(f32[1024]{0:T(1024)S(1)} %add.232), channel_id=1, source_target_pairs={{0,8},{1,9},{2,10},{3,11},{4,12},{5,13},{6,14},{7,15},{8,0},{9,1},... | collective-permute-start | bytes 12296 | tf_op jit(solution)/shard_map/ppermute | solution.py:164
  25.0 0.9 %convolution_reduce_fusion.1 = f32[320]{0:T(512)} fusion(bf16[1280,1]{0,1:T(2,128)(2,1)S(1)} %reshape.157, bf16[1280,320]{0,1:T(8,128)(2,1)S(1)} %copy-done.3), kind=kOutput, calls=%fused_computation.21 | convolution fusion | flops 819200 | bytes 823040 | tf_op jit(solution)/shard_map/dot_general | solution.py:218
  26.2 1.8 %copy.27 = f32[2,4,128,320]{3,2,1,0:T(8,128)S(1)} copy(f32[2,4,128,320]{2,3,0,1:T(8,128)} %fusion) | data formatting | bytes 2621440 | tf_op jit(solution)/shard_map/add | solution.py:222
  28.3 0.6 fusion.95
  29.6 0.6 multiply_reduce_fusion.1
  30.9 1.0 %convolution_add_fusion.14 = f32[2,320]{1,0:T(2,128)S(1)} fusion(bf16[1024,320]{0,1:T(8,128)(2,1)S(1)} %copy-done.4, bf16[1,1024]{1,0:T(2,128)(2,1)S(1)} %stack.13, bf16[1,1024]{1,0:T(2,128)(2,1)S(1)} %stack.12, f32[320]{0:T(512)} %convolution_reduce_fusion.1), kind=kOutput, calls=%fused_computation.20 | convolution fusion | flops 1319552 | bytes 663296 | tf_op jit(solution)/shard_map/dot_general | solution.py:209
  32.3 1.5 %add_convert_fusion.state_ref = bf16[2,8,128,320]{3,2,1,0:T(8,128)(2,1)} fusion(f32[2,8,128,320]{3,2,1,0:T(8,128)S(1)} %bitcast.207, f32[8,320]{1,0:T(8,128)S(1)} %add.240), kind=kLoop, calls=%fused_computation | loop fusion | flops 1310720 | bytes 3942400 | tf_op jit(solution)/shard_map/convert_element_type | solution.py:224
  33.8 31.3 %shard_map.149 = bf16[2,8,128,320]{3,2,1,0:T(8,128)(2,1)S(1)} custom-call(bf16[2,8,128,320]{3,2,1,0:T(8,128)(2,1)} %add_convert_fusion.state_ref, bf16[2,9,320,320]{3,2,1,0:T(8,128)(2,1)} %wsp_ref.1, bf16[2,3,320,320]{3,2,1,0:T(8,128)(2,1)S(1)} %copy-done.1, f32[320,320]{1,0:T(8,128)S(1)} %compare_convert_fusion.same_ref, ...), custom_call_target="tpu_custom_call" | custom-call | tf_op jit(solution)/shard_map/pallas_call | solution.py:151
  65.1 1.6 %copy.28 = bf16[2,2,4,128,320]{3,4,0,2,1:T(8,128)(2,1)} copy(bf16[2,2,4,128,320]{4,3,2,1,0:T(8,128)(2,1)S(1)} %bitcast.205) | data formatting | bytes 2621440 | tf_op jit(solution)/shard_map/reshape | solution.py:228
  66.7 2.4 %fusion.98 = (bf16[2,320,4,2,127]{4,1,3,2,0:T(8,128)(2,1)S(1)}, bf16[2,320,4,2,127]{4,1,3,2,0:T(8,128)(2,1)S(1)}) fusion(bf16[2,320,4,2,128]{4,1,3,2,0:T(8,128)(2,1)} %bitcast.206), kind=kLoop, calls=%fused_computation.147 | loop fusion | bytes 5201920 | tf_op jit(solution)/shard_map/slice | solution.py:42
  69.4 0.6 fusion.9
  70.0 0.4 convolution_add_fusion.13
  72.4 1.2 %collective-permute-done.4 = f32[4,4,2,128]{3,0,2,1:T(4,128)S(1)} collective-permute-done((f32[4,4,2,128]{3,0,2,1:T(4,128)S(1)}, f32[4,4,2,128]{3,0,2,1:T(4,128)S(1)}, u32[]{:S(2)}, u32[]{:S(2)}) %collective-permute-start.4) | collective-permute-done | bytes 16416 | tf_op jit(solution)/shard_map/ppermute | solution.py:178
  73.6 1.5 %collective-permute-start.5 = (f32[4,4,2,128]{3,0,2,1:T(4,128)S(1)}, f32[4,4,2,128]{3,0,2,1:T(4,128)S(1)}, u32[]{:S(2)}, u32[]{:S(2)}) collective-permute-start(f32[4,4,2,128]{3,0,2,1:T(4,128)S(1)} %add.255), channel_id=1, source_target_pairs={{0,2},{1,3},{2,0},{3,1},{4,6},{5,7},{6,4},{7,5},{8,10},{9,11},{10,... | collective-permute-start | bytes 49160 | tf_op jit(solution)/shard_map/ppermute | solution.py:178
  75.1 2.2 %collective-permute-done.5 = f32[4,4,2,128]{3,0,2,1:T(4,128)S(1)} collective-permute-done((f32[4,4,2,128]{3,0,2,1:T(4,128)S(1)}, f32[4,4,2,128]{3,0,2,1:T(4,128)S(1)}, u32[]{:S(2)}, u32[]{:S(2)}) %collective-permute-start.5) | collective-permute-done | bytes 16416 | tf_op jit(solution)/shard_map/ppermute | solution.py:178
  77.3 1.6 %collective-permute-start.6 = (f32[4,4,2,128]{3,0,2,1:T(4,128)S(1)}, f32[4,4,2,128]{3,0,2,1:T(4,128)S(1)}, u32[]{:S(2)}, u32[]{:S(2)}) collective-permute-start(f32[4,4,2,128]{3,0,2,1:T(4,128)S(1)} %add.257), channel_id=1, source_target_pairs={{0,4},{1,5},{2,6},{3,7},{4,0},{5,1},{6,2},{7,3},{8,12},{9,13},{10,... | collective-permute-start | bytes 49160 | tf_op jit(solution)/shard_map/ppermute | solution.py:178
  78.9 2.2 %collective-permute-done.6 = f32[4,4,2,128]{3,0,2,1:T(4,128)S(1)} collective-permute-done((f32[4,4,2,128]{3,0,2,1:T(4,128)S(1)}, f32[4,4,2,128]{3,0,2,1:T(4,128)S(1)}, u32[]{:S(2)}, u32[]{:S(2)}) %collective-permute-start.6) | collective-permute-done | bytes 16416 | tf_op jit(solution)/shard_map/ppermute | solution.py:178
  81.1 1.2 %collective-permute-start.7 = (f32[4,4,2,128]{3,0,2,1:T(4,128)S(1)}, f32[4,4,2,128]{3,0,2,1:T(4,128)S(1)}, u32[]{:S(2)}, u32[]{:S(2)}) collective-permute-start(f32[4,4,2,128]{3,0,2,1:T(4,128)S(1)} %add.259), channel_id=1, source_target_pairs={{0,8},{1,9},{2,10},{3,11},{4,12},{5,13},{6,14},{7,15},{8,0},{9,1},... | collective-permute-start | bytes 49160 | tf_op jit(solution)/shard_map/ppermute | solution.py:178
  82.3 3.5 %collective-permute-done.7 = f32[4,4,2,128]{3,0,2,1:T(4,128)S(1)} collective-permute-done((f32[4,4,2,128]{3,0,2,1:T(4,128)S(1)}, f32[4,4,2,128]{3,0,2,1:T(4,128)S(1)}, u32[]{:S(2)}, u32[]{:S(2)}) %collective-permute-start.7) | collective-permute-done | bytes 16416 | tf_op jit(solution)/shard_map/ppermute | solution.py:178
  85.7 0.6 copy.32
  86.4 0.6 copy.33
  (72 shorter events, 6.2 us)
Async XLA Ops:
  0.6 6.0 %copy-start = (bf16[320,1280]{1,0:T(8,128)(2,1)S(1)}, bf16[320,1280]{1,0:T(8,128)(2,1)}, u32[]{:S(2)}) copy-start(bf16[320,1280]{1,0:T(8,128)(2,1)} %param.21) | copy-start | bytes 2457604
  1.6 5.3 %copy-start.7 = (f32[1024]{0:T(1024)S(1)}, f32[1024]{0:T(1024)}, u32[]{:S(2)}) copy-start(f32[1024]{0:T(1024)} %param.20) | copy-start | bytes 12292
  1.6 7.8 %copy-start.5 = (f32[1,4,4,2,128]{4,3,2,1,0:T(2,128)S(1)}, f32[1,4,4,2,128]{4,3,2,1,0:T(2,128)}, u32[]{:S(2)}) copy-start(f32[1,4,4,2,128]{4,3,2,1,0:T(2,128)} %param.17) | copy-start | bytes 49156
  1.6 8.0 %copy-start.9 = (bf16[9,320,4]{1,2,0:T(4,128)(2,1)S(1)}, bf16[9,320,4]{1,2,0:T(4,128)(2,1)}, u32[]{:S(2)}) copy-start(bf16[9,320,4]{1,2,0:T(4,128)(2,1)} %param.24) | copy-start | bytes 69124
  5.4 8.7 %collective-permute-start = (f32[1024]{0:T(1024)S(1)}, f32[1024]{0:T(1024)S(1)}, u32[]{:S(2)}, u32[]{:S(2)}) collective-permute-start(f32[1024]{0:T(1024)S(1)} %bitcast.208), channel_id=1, source_target_pairs={{0,1},{1,0},{2,3},{3,2},{4,5},{5,4},{6,7},{7,6},{8,9},{9,8},{10,11... | collective-permute-start | bytes 12296 | tf_op jit(solution)/shard_map/ppermute | solution.py:164
  12.6 12.4 %copy-start.3 = (bf16[1280,320]{0,1:T(8,128)(2,1)S(1)}, bf16[1280,320]{0,1:T(8,128)(2,1)}, u32[]{:S(2)}) copy-start(bf16[1280,320]{0,1:T(8,128)(2,1)} %param.22) | copy-start | bytes 2457604
  14.1 4.2 %collective-permute-start.1 = (f32[1024]{0:T(1024)S(1)}, f32[1024]{0:T(1024)S(1)}, u32[]{:S(2)}, u32[]{:S(2)}) collective-permute-start(f32[1024]{0:T(1024)S(1)} %add.230), channel_id=1, source_target_pairs={{0,2},{1,3},{2,0},{3,1},{4,6},{5,7},{6,4},{7,5},{8,10},{9,11},{10,... | collective-permute-start | bytes 12296 | tf_op jit(solution)/shard_map/ppermute | solution.py:164
  18.3 3.7 %collective-permute-start.2 = (f32[1024]{0:T(1024)S(1)}, f32[1024]{0:T(1024)S(1)}, u32[]{:S(2)}, u32[]{:S(2)}) collective-permute-start(f32[1024]{0:T(1024)S(1)} %add.231), channel_id=1, source_target_pairs={{0,4},{1,5},{2,6},{3,7},{4,0},{5,1},{6,2},{7,3},{8,12},{9,13},{10,... | collective-permute-start | bytes 12296 | tf_op jit(solution)/shard_map/ppermute | solution.py:164
  21.9 6.4 %collective-permute-start.3 = (f32[1024]{0:T(1024)S(1)}, f32[1024]{0:T(1024)S(1)}, u32[]{:S(2)}, u32[]{:S(2)}) collective-permute-start(f32[1024]{0:T(1024)S(1)} %add.232), channel_id=1, source_target_pairs={{0,8},{1,9},{2,10},{3,11},{4,12},{5,13},{6,14},{7,15},{8,0},{9,1},... | collective-permute-start | bytes 12296 | tf_op jit(solution)/shard_map/ppermute | solution.py:164
  26.2 4.7 %copy-start.4 = (bf16[1024,320]{0,1:T(8,128)(2,1)S(1)}, bf16[1024,320]{0,1:T(8,128)(2,1)}, u32[]{:S(2)}) copy-start(bf16[1024,320]{0,1:T(8,128)(2,1)} %param.23) | copy-start | bytes 1966084
  32.3 1.5 %copy-start.1 = (bf16[2,3,320,320]{3,2,1,0:T(8,128)(2,1)S(1)}, bf16[2,3,320,320]{3,2,1,0:T(8,128)(2,1)}, u32[]{:S(2)}) copy-start(bf16[2,3,320,320]{3,2,1,0:T(8,128)(2,1)} %wt_ref.1) | copy-start | bytes 3686404
  66.7 2.5 %copy-start.2 = (bf16[2,2,4,128,320]{3,4,0,2,1:T(8,128)(2,1)S(1)}, bf16[2,2,4,128,320]{3,4,0,2,1:T(8,128)(2,1)}, u32[]{:S(2)}) copy-start(bf16[2,2,4,128,320]{3,4,0,2,1:T(8,128)(2,1)} %copy.28) | copy-start | bytes 3932164
  66.7 2.5 %copy-start.8 = (bf16[9,4,320]{2,1,0:T(4,128)(2,1)S(1)}, bf16[9,4,320]{2,1,0:T(4,128)(2,1)}, u32[]{:S(2)}) copy-start(bf16[9,4,320]{2,1,0:T(4,128)(2,1)} %param.27) | copy-start | bytes 69124
  71.6 0.7 copy-start.6
  71.6 0.7 copy-start.10
  71.6 14.1 %copy-start.11 = (f32[4,4,2,128]{3,2,1,0:T(2,128)S(1)}, f32[4,4,2,128]{3,2,1,0:T(2,128)}, u32[]{:S(2)}) copy-start(f32[4,4,2,128]{3,2,1,0:T(2,128)} %param.16) | copy-start | bytes 49156
  72.3 1.2 %collective-permute-start.4 = (f32[4,4,2,128]{3,0,2,1:T(4,128)S(1)}, f32[4,4,2,128]{3,0,2,1:T(4,128)S(1)}, u32[]{:S(2)}, u32[]{:S(2)}) collective-permute-start(f32[4,4,2,128]{3,0,2,1:T(4,128)S(1)} %fusion.19), channel_id=1, source_target_pairs={{0,1},{1,0},{2,3},{3,2},{4,5},{5,4},{6,7},{7,6},{8,9},{9,8},{10,11... | collective-permute-start | bytes 49160 | tf_op jit(solution)/shard_map/ppermute | solution.py:178
  73.6 3.7 %collective-permute-start.5 = (f32[4,4,2,128]{3,0,2,1:T(4,128)S(1)}, f32[4,4,2,128]{3,0,2,1:T(4,128)S(1)}, u32[]{:S(2)}, u32[]{:S(2)}) collective-permute-start(f32[4,4,2,128]{3,0,2,1:T(4,128)S(1)} %add.255), channel_id=1, source_target_pairs={{0,2},{1,3},{2,0},{3,1},{4,6},{5,7},{6,4},{7,5},{8,10},{9,11},{10,... | collective-permute-start | bytes 49160 | tf_op jit(solution)/shard_map/ppermute | solution.py:178
  77.3 3.7 %collective-permute-start.6 = (f32[4,4,2,128]{3,0,2,1:T(4,128)S(1)}, f32[4,4,2,128]{3,0,2,1:T(4,128)S(1)}, u32[]{:S(2)}, u32[]{:S(2)}) collective-permute-start(f32[4,4,2,128]{3,0,2,1:T(4,128)S(1)} %add.257), channel_id=1, source_target_pairs={{0,4},{1,5},{2,6},{3,7},{4,0},{5,1},{6,2},{7,3},{8,12},{9,13},{10,... | collective-permute-start | bytes 49160 | tf_op jit(solution)/shard_map/ppermute | solution.py:178
  81.1 4.6 %collective-permute-start.7 = (f32[4,4,2,128]{3,0,2,1:T(4,128)S(1)}, f32[4,4,2,128]{3,0,2,1:T(4,128)S(1)}, u32[]{:S(2)}, u32[]{:S(2)}) collective-permute-start(f32[4,4,2,128]{3,0,2,1:T(4,128)S(1)} %add.259), channel_id=1, source_target_pairs={{0,8},{1,9},{2,10},{3,11},{4,12},{5,13},{6,14},{7,15},{8,0},{9,1},... | collective-permute-start | bytes 49160 | tf_op jit(solution)/shard_map/ppermute | solution.py:178

commit v2 on v1

--- a/solution.py
+++ b/solution.py
@@ -73,7 +73,7 @@
     return result
 
 
-def unet_body(state_ref, wsp_ref, wt_ref, same_ref, batch_ref, out_ref):
+def unet_body(state_ref, wsp_ref, wt_ref, wl_ref, same_ref, batch_ref, out_ref):
     rows, blocks, cols, chans = state_ref.shape
     frames = blocks // 2
     same = same_ref[...]
@@ -139,20 +139,42 @@
         x = state.astype(jnp.float32)
         normed = norm_silu(x, batch_mix, per_sample)
         state = (x + conv_tm(normed, section)).astype(jnp.bfloat16)
-    out_ref[...] = norm_silu(state.astype(jnp.float32), None, per_frame)
-
-
-def unet_sections(state, spatial_weights, temporal_weights):
+    last = norm_silu(state.astype(jnp.float32), None, per_frame)
+    x0 = last[0].reshape(blocks * cols, chans)
+    x1 = last[1].reshape(blocks * cols, chans)
+    lane = lax.broadcasted_iota(jnp.int32, (wl_ref.shape[1], blocks * cols), 1) % cols
+
+    def mm_t(w, a):
+        return lax.dot_general(w, a, (((1,), (1,)), ((), ())), preferred_element_type=jnp.float32)
+
+    for row in range(rows):
+        own, other = (x0, x1) if row == 0 else (x1, x0)
+        other_dr = 1 if row == 0 else -1
+        acc = None
+        for dc in (-1, 0, 1):
+            y = mm_t(wl_ref[3 + dc + 1], own) + mm_t(wl_ref[(other_dr + 1) * 3 + dc + 1], other)
+            if dc == -1:
+                y = jnp.where(lane == 0, 0.0, pltpu.roll(y, 1, 1))
+            elif dc == 1:
+                y = jnp.where(lane == cols - 1, 0.0, pltpu.roll(y, blocks * cols - 1, 1))
+            acc = y if acc is None else acc + y
+        out_ref[row] = acc
+
+
+def unet_sections(state, spatial_weights, temporal_weights, conv_last):
     rows, blocks, cols, chans = state.shape
+    taps, outs, _ = conv_last.shape
+    padded = -(-outs // 16) * 16
+    last = jnp.concatenate([conv_last, jnp.zeros((taps, padded - outs, chans), conv_last.dtype)], axis=1)
     group = jnp.arange(chans) // (chans // GROUPS)
     same = (group[:, None] == group[None, :]).astype(jnp.float32)
     block_of = jnp.arange(blocks) // (blocks // 2)
     batch_mix = (block_of[:, None] == block_of[None, :]).astype(jnp.float32)
     return pl.pallas_call(
         unet_body,
-        out_shape=jax.ShapeDtypeStruct(state.shape, jnp.bfloat16),
+        out_shape=jax.ShapeDtypeStruct((rows, padded, blocks * cols), jnp.float32),
         compiler_params=pltpu.CompilerParams(vmem_limit_bytes=100 * 1024 * 1024 // 2),
-    )(state, spatial_weights, temporal_weights, same, batch_mix)
+    )(state, spatial_weights, temporal_weights, last, same, batch_mix)[:, :outs]
 
 
 def butterfly_sum(x, axis):
@@ -224,9 +246,8 @@
     ).astype(jnp.bfloat16)
     batch, chans, frames, rows, cols = state.shape
     laid = state.transpose(3, 0, 2, 4, 1).reshape(rows, batch * frames, cols, chans)
-    normed = unet_sections(laid, spatial_weights, temporal_weights)
-    normed = normed.reshape(rows, batch, frames, cols, chans).transpose(1, 4, 2, 0, 3)
-    predicted = conv_space(normed, conv_last)
+    predicted = unet_sections(laid, spatial_weights, temporal_weights, conv_last)
+    predicted = predicted.reshape(rows, -1, batch, frames, cols).transpose(2, 1, 3, 0, 4)
     guided = predicted[1] + GUIDANCE_SCALE * (predicted[0] - predicted[1])
     alpha_now = alpha_bar(step_value)
     alpha_prev = alpha_bar(step_value - DT)

time: 87.3 us -> 80.6 us (0.923)
  local copies, waits for them, and re-layouts: 7.94 us -> 3.48 us
  matrix products: 13 us -> 9.92 us
  Pallas kernels: 31.3 us -> 32.5 us
    dot_general x18 -> x9, matrix products: 7.11 us -> 4.23 us  [conv_space(): jnp.einsum('oc,bcfrw->bofrw', weight[row_step * 3 + col_step], window, pr...]
    slice x1, local copies, waits for them, and re-layouts: 2.44 us -> 0.01 us  [unet_sections(): pl.pallas_call(unet_body, out_shape=jax.ShapeDtypeStruct((rows, padded, b...]
    reshape x1 -> x2, local copies, waits for them, and re-layouts: 1.58 us -> 0.05 us  [local(): predicted.reshape(rows, -1, batch, frames, cols).transpose(2, 1, 3, 0, 4)]
    convert_element_type x1, other arithmetic: 1.52 us -> 0.34 us  [local(): state = (conv_space(latent.astype(jnp.bfloat16)[None], conv_first) + embe...]
    pallas_call x1, Pallas kernels: 31.3 us -> 32.5 us  [unet_sections(): pl.pallas_call(unet_body, out_shape=jax.ShapeDtypeStruct((rows, padded, b...]
where the time goes in v2:
time: 80.6 us; the launch traced here: 80.3 us
  Pallas kernels  32.5 us (40%)
  starting transfers between devices  13.3 us (17%)
  waiting for transfers between devices  11.5 us (14%)
  matrix products  9.92 us (12%)
  between operations  4.85 us (6%)
  other arithmetic  4.75 us (6%)
  local copies, waits for them, and re-layouts  3.48 us (4%)
    pallas_call x1, Pallas kernels, unet_sections(): pl.pallas_call(unet_body, out_shape=jax.ShapeDtypeStruct((rows, padded, b...  32.5 us
    ppermute x4, waiting for transfers between devices, butterfly_scan(): got = lax.ppermute(total, axis, [(i, i ^ k) for i in range(peers)])  8.39 us
    ppermute x4, starting transfers between devices, butterfly_sum(): x = x + lax.ppermute(x, axis, [(i, i ^ k) for i in range(peers)])  8.15 us
    ppermute x4, starting transfers between devices, butterfly_scan(): got = lax.ppermute(total, axis, [(i, i ^ k) for i in range(peers)])  5.16 us
    dot_general x9, matrix products, conv_space(): jnp.einsum('oc,bcfrw->bofrw', weight[row_step * 3 + col_step], window, pr...  4.23 us
    dot_general x1, matrix products, local(): jnp.dot(counts, token_table, preferred_element_type=jnp.float32)[0]  3.73 us
    ppermute x4, waiting for transfers between devices, butterfly_sum(): x = x + lax.ppermute(x, axis, [(i, i ^ k) for i in range(peers)])  3.1 us
    add x4, local copies, waits for them, and re-layouts, local(): conv_space(latent.astype(jnp.bfloat16)[None], conv_first)  2.13 us
  transfers between devices with their start and end apart: 8, of which 6 were waited for; matrix products, arithmetic and copies ran while one was open for 10% of the time, Pallas kernels for 0%

profile of v2, /device:TPU:0, one launch (start us, length us, event | category | flops | bytes accessed | tf_op | source)
XLA Modules:
  0.0 80.3 jit_solution(7606707484164554057)
XLA Ops:
  0.6 0.7 broadcast_subtract_fusion
  1.6 3.7 %fusion.62 = f32[1,1024]{1,0:T(1,128)S(1)} fusion(bf16[3088,1]{0,1:T(2,128)(2,1)S(1)} %reshape.153, bf16[3088,1024]{1,0:T(8,128)(2,1)} %param.19), kind=kOutput, calls=%fused_computation.105 | convolution fusion | flops 6324224 | bytes 6334496 | tf_op jit(solution)/shard_map/dot_general | solution.py:228
  5.4 0.5 collective-permute-start
  6.9 0.6 reduce_sum.48
  8.2 0.6 multiply_reduce_fusion
  9.6 0.4 fusion.10
  10.0 0.4 convolution_add_fusion.7
  10.7 0.4 convolution_add_fusion.5
  11.1 0.4 convolution_add_fusion.4
  11.8 0.4 convolution_add_fusion.2
  12.2 0.4 convolution_add_fusion.1
  12.6 1.4 %fusion = f32[2,4,128,320]{2,3,0,1:T(8,128)} fusion(f32[4,2,128,320]{2,3,1,0:T(8,128)S(1)} %convolution_add_fusion.1, bf16[1,4,4,2,128]{4,1,3,2,0:T(4,128)(2,1)S(1)} %concatenate.15, bf16[9,320,4]{1,2,0:T(4,128)(2,1)S(1)} %copy-done.6), kind=kOutput, calls=%fused_computation.2 | convolution fusion | flops 2949120 | bytes 2632704 | tf_op jit(solution)/shard_map/oc,bcfrw->bofrw/dot_general | solution.py:53
  14.1 2.6 %collective-permute-start.1 = (f32[1024]{0:T(1024)S(1)}, f32[1024]{0:T(1024)S(1)}, u32[]{:S(2)}, u32[]{:S(2)}) collective-permute-start(f32[1024]{0:T(1024)S(1)} %add.192), channel_id=1, source_target_pairs={{0,2},{1,3},{2,0},{3,1},{4,6},{5,7},{6,4},{7,5},{8,10},{9,11},{10,... | collective-permute-start | bytes 12296 | tf_op jit(solution)/shard_map/ppermute | solution.py:186
  16.7 1.6 %collective-permute-done.1 = f32[1024]{0:T(1024)S(1)} collective-permute-done((f32[1024]{0:T(1024)S(1)}, f32[1024]{0:T(1024)S(1)}, u32[]{:S(2)}, u32[]{:S(2)}) %collective-permute-start.1) | collective-permute-done | bytes 4128 | tf_op jit(solution)/shard_map/ppermute | solution.py:186
  18.3 2.1 %collective-permute-start.2 = (f32[1024]{0:T(1024)S(1)}, f32[1024]{0:T(1024)S(1)}, u32[]{:S(2)}, u32[]{:S(2)}) collective-permute-start(f32[1024]{0:T(1024)S(1)} %add.193), channel_id=1, source_target_pairs={{0,4},{1,5},{2,6},{3,7},{4,0},{5,1},{6,2},{7,3},{8,12},{9,13},{10,... | collective-permute-start | bytes 12296 | tf_op jit(solution)/shard_map/ppermute | solution.py:186
  20.4 1.5 %collective-permute-done.2 = f32[1024]{0:T(1024)S(1)} collective-permute-done((f32[1024]{0:T(1024)S(1)}, f32[1024]{0:T(1024)S(1)}, u32[]{:S(2)}, u32[]{:S(2)}) %collective-permute-start.2) | collective-permute-done | bytes 4128 | tf_op jit(solution)/shard_map/ppermute | solution.py:186
  22.0 3.0 %collective-permute-start.3 = (f32[1024]{0:T(1024)S(1)}, f32[1024]{0:T(1024)S(1)}, u32[]{:S(2)}, u32[]{:S(2)}) collective-permute-start(f32[1024]{0:T(1024)S(1)} %add.194), channel_id=1, source_target_pairs={{0,8},{1,9},{2,10},{3,11},{4,12},{5,13},{6,14},{7,15},{8,0},{9,1},... | collective-permute-start | bytes 12296 | tf_op jit(solution)/shard_map/ppermute | solution.py:186
  25.6 1.8 %copy.20 = f32[2,4,128,320]{3,2,1,0:T(8,128)S(1)} copy(f32[2,4,128,320]{2,3,0,1:T(8,128)} %fusion) | data formatting | bytes 2621440 | tf_op jit(solution)/shard_map/add | solution.py:244
  27.7 0.6 fusion.56
  29.0 0.6 multiply_reduce_fusion.1
  30.3 1.4 %convolution_add_fusion.8 = f32[2,320]{1,0:T(2,128)S(1)} fusion(bf16[1024,320]{0,1:T(8,128)(2,1)} %param.23, bf16[1,1024]{1,0:T(2,128)(2,1)S(1)} %stack.13, bf16[1,1024]{1,0:T(2,128)(2,1)S(1)} %stack.12, f32[320]{0:T(512)S(1)} %convolution_reduce_fusion.1), kind=kOutput, calls=%fused_computation.11 | convolution fusion | flops 1319552 | bytes 663296 | tf_op jit(solution)/shard_map/dot_general | solution.py:231
  32.1 0.3 add_convert_fusion.state_ref
  32.4 1.0 %copy-done.1 = bf16[2,3,320,320]{3,2,1,0:T(8,128)(2,1)S(1)} copy-done((bf16[2,3,320,320]{3,2,1,0:T(8,128)(2,1)S(1)}, bf16[2,3,320,320]{3,2,1,0:T(8,128)(2,1)}, u32[]{:S(2)}) %copy-start.1) | copy-done | bytes 1228824
  33.4 32.5 %shard_map.149 = f32[2,16,1024]{2,1,0:T(8,128)S(1)} custom-call(bf16[2,8,128,320]{3,2,1,0:T(8,128)(2,1)S(1)} %add_convert_fusion.state_ref, bf16[2,9,320,320]{3,2,1,0:T(8,128)(2,1)} %wsp_ref.1, bf16[2,3,320,320]{3,2,1,0:T(8,128)(2,1)S(1)} %copy-done.1, bf16[9,16,320]{2,1,0:T(8,128)(2,1)S(1)} %concatenate.17.wl_ref, ...), custom_call_target="tpu_custom_call" | custom-call | tf_op jit(solution)/shard_map/pallas_call | solution.py:173
  66.1 1.2 %collective-permute-done.4 = f32[4,4,2,128]{3,2,1,0:T(2,128)S(1)} collective-permute-done((f32[4,4,2,128]{3,2,1,0:T(2,128)S(1)}, f32[4,4,2,128]{3,2,1,0:T(2,128)S(1)}, u32[]{:S(2)}, u32[]{:S(2)}) %collective-permute-start.4) | collective-permute-done | bytes 16416 | tf_op jit(solution)/shard_map/ppermute | solution.py:200
  67.3 1.6 %collective-permute-start.5 = (f32[4,4,2,128]{3,2,1,0:T(2,128)S(1)}, f32[4,4,2,128]{3,2,1,0:T(2,128)S(1)}, u32[]{:S(2)}, u32[]{:S(2)}) collective-permute-start(f32[4,4,2,128]{3,2,1,0:T(2,128)S(1)} %add.208), channel_id=1, source_target_pairs={{0,2},{1,3},{2,0},{3,1},{4,6},{5,7},{6,4},{7,5},{8,10},{9,11},{10,... | collective-permute-start | bytes 49160 | tf_op jit(solution)/shard_map/ppermute | solution.py:200
  68.9 2.2 %collective-permute-done.5 = f32[4,4,2,128]{3,2,1,0:T(2,128)S(1)} collective-permute-done((f32[4,4,2,128]{3,2,1,0:T(2,128)S(1)}, f32[4,4,2,128]{3,2,1,0:T(2,128)S(1)}, u32[]{:S(2)}, u32[]{:S(2)}) %collective-permute-start.5) | collective-permute-done | bytes 16416 | tf_op jit(solution)/shard_map/ppermute | solution.py:200
  71.1 1.7 %collective-permute-start.6 = (f32[4,4,2,128]{3,2,1,0:T(2,128)S(1)}, f32[4,4,2,128]{3,2,1,0:T(2,128)S(1)}, u32[]{:S(2)}, u32[]{:S(2)}) collective-permute-start(f32[4,4,2,128]{3,2,1,0:T(2,128)S(1)} %add.210), channel_id=1, source_target_pairs={{0,4},{1,5},{2,6},{3,7},{4,0},{5,1},{6,2},{7,3},{8,12},{9,13},{10,... | collective-permute-start | bytes 49160 | tf_op jit(solution)/shard_map/ppermute | solution.py:200
  72.8 2.2 %collective-permute-done.6 = f32[4,4,2,128]{3,2,1,0:T(2,128)S(1)} collective-permute-done((f32[4,4,2,128]{3,2,1,0:T(2,128)S(1)}, f32[4,4,2,128]{3,2,1,0:T(2,128)S(1)}, u32[]{:S(2)}, u32[]{:S(2)}) %collective-permute-start.6) | collective-permute-done | bytes 16416 | tf_op jit(solution)/shard_map/ppermute | solution.py:200
  74.9 1.8 %collective-permute-start.7 = (f32[4,4,2,128]{3,2,1,0:T(2,128)S(1)}, f32[4,4,2,128]{3,2,1,0:T(2,128)S(1)}, u32[]{:S(2)}, u32[]{:S(2)}) collective-permute-start(f32[4,4,2,128]{3,2,1,0:T(2,128)S(1)} %add.212), channel_id=1, source_target_pairs={{0,8},{1,9},{2,10},{3,11},{4,12},{5,13},{6,14},{7,15},{8,0},{9,1},... | collective-permute-start | bytes 49160 | tf_op jit(solution)/shard_map/ppermute | solution.py:200
  76.8 2.9 %collective-permute-done.7 = f32[4,4,2,128]{3,2,1,0:T(2,128)S(1)} collective-permute-done((f32[4,4,2,128]{3,2,1,0:T(2,128)S(1)}, f32[4,4,2,128]{3,2,1,0:T(2,128)S(1)}, u32[]{:S(2)}, u32[]{:S(2)}) %collective-permute-start.7) | collective-permute-done | bytes 16416 | tf_op jit(solution)/shard_map/ppermute | solution.py:200
  79.6 0.6 add_add_fusion
  (57 shorter events, 2.6 us)
Async XLA Ops:
  0.6 6.0 %copy-start = (bf16[320,1280]{1,0:T(8,128)(2,1)S(1)}, bf16[320,1280]{1,0:T(8,128)(2,1)}, u32[]{:S(2)}) copy-start(bf16[320,1280]{1,0:T(8,128)(2,1)} %param.21) | copy-start | bytes 2457604
  1.6 5.3 %copy-start.4 = (f32[1024]{0:T(1024)S(1)}, f32[1024]{0:T(1024)}, u32[]{:S(2)}) copy-start(f32[1024]{0:T(1024)} %param.20) | copy-start | bytes 12292
  1.6 7.8 %copy-start.3 = (f32[1,4,4,2,128]{4,3,2,1,0:T(2,128)S(1)}, f32[1,4,4,2,128]{4,3,2,1,0:T(2,128)}, u32[]{:S(2)}) copy-start(f32[1,4,4,2,128]{4,3,2,1,0:T(2,128)} %param.17) | copy-start | bytes 49156
  1.6 8.0 %copy-start.6 = (bf16[9,320,4]{1,2,0:T(4,128)(2,1)S(1)}, bf16[9,320,4]{1,2,0:T(4,128)(2,1)}, u32[]{:S(2)}) copy-start(bf16[9,320,4]{1,2,0:T(4,128)(2,1)} %param.24) | copy-start | bytes 69124
  5.4 8.7 %collective-permute-start = (f32[1024]{0:T(1024)S(1)}, f32[1024]{0:T(1024)S(1)}, u32[]{:S(2)}, u32[]{:S(2)}) collective-permute-start(f32[1024]{0:T(1024)S(1)} %bitcast.137), channel_id=1, source_target_pairs={{0,1},{1,0},{2,3},{3,2},{4,5},{5,4},{6,7},{7,6},{8,9},{9,8},{10,11... | collective-permute-start | bytes 12296 | tf_op jit(solution)/shard_map/ppermute | solution.py:186
  12.6 12.4 %copy-start.2 = (bf16[1280,320]{0,1:T(8,128)(2,1)S(1)}, bf16[1280,320]{0,1:T(8,128)(2,1)}, u32[]{:S(2)}) copy-start(bf16[1280,320]{0,1:T(8,128)(2,1)} %param.22) | copy-start | bytes 2457604
  14.1 4.2 %collective-permute-start.1 = (f32[1024]{0:T(1024)S(1)}, f32[1024]{0:T(1024)S(1)}, u32[]{:S(2)}, u32[]{:S(2)}) collective-permute-start(f32[1024]{0:T(1024)S(1)} %add.192), channel_id=1, source_target_pairs={{0,2},{1,3},{2,0},{3,1},{4,6},{5,7},{6,4},{7,5},{8,10},{9,11},{10,... | collective-permute-start | bytes 12296 | tf_op jit(solution)/shard_map/ppermute | solution.py:186
  18.3 3.6 %collective-permute-start.2 = (f32[1024]{0:T(1024)S(1)}, f32[1024]{0:T(1024)S(1)}, u32[]{:S(2)}, u32[]{:S(2)}) collective-permute-start(f32[1024]{0:T(1024)S(1)} %add.193), channel_id=1, source_target_pairs={{0,4},{1,5},{2,6},{3,7},{4,0},{5,1},{6,2},{7,3},{8,12},{9,13},{10,... | collective-permute-start | bytes 12296 | tf_op jit(solution)/shard_map/ppermute | solution.py:186
  22.0 5.8 %collective-permute-start.3 = (f32[1024]{0:T(1024)S(1)}, f32[1024]{0:T(1024)S(1)}, u32[]{:S(2)}, u32[]{:S(2)}) collective-permute-start(f32[1024]{0:T(1024)S(1)} %add.194), channel_id=1, source_target_pairs={{0,8},{1,9},{2,10},{3,11},{4,12},{5,13},{6,14},{7,15},{8,0},{9,1},... | collective-permute-start | bytes 12296 | tf_op jit(solution)/shard_map/ppermute | solution.py:186
  25.6 1.8 %copy-start.5 = (bf16[9,4,320]{2,1,0:T(4,128)(2,1)S(1)}, bf16[9,4,320]{2,1,0:T(4,128)(2,1)}, u32[]{:S(2)}) copy-start(bf16[9,4,320]{2,1,0:T(4,128)(2,1)} %param.27) | copy-start | bytes 69124
  32.0 1.4 %copy-start.1 = (bf16[2,3,320,320]{3,2,1,0:T(8,128)(2,1)S(1)}, bf16[2,3,320,320]{3,2,1,0:T(8,128)(2,1)}, u32[]{:S(2)}) copy-start(bf16[2,3,320,320]{3,2,1,0:T(8,128)(2,1)} %wt_ref.1) | copy-start | bytes 3686404
  33.4 32.6 %copy-start.7 = (f32[1,4,4,2,128]{4,3,2,1,0:T(2,128)S(1)}, f32[1,4,4,2,128]{4,3,2,1,0:T(2,128)}, u32[]{:S(2)}) copy-start(f32[1,4,4,2,128]{4,3,2,1,0:T(2,128)} %param.18) | copy-start | bytes 49156
  33.4 46.2 %copy-start.8 = (f32[4,4,2,128]{3,2,1,0:T(2,128)S(1)}, f32[4,4,2,128]{3,2,1,0:T(2,128)}, u32[]{:S(2)}) copy-start(f32[4,4,2,128]{3,2,1,0:T(2,128)} %param.16) | copy-start | bytes 49156
  66.0 1.2 %collective-permute-start.4 = (f32[4,4,2,128]{3,2,1,0:T(2,128)S(1)}, f32[4,4,2,128]{3,2,1,0:T(2,128)S(1)}, u32[]{:S(2)}, u32[]{:S(2)}) collective-permute-start(f32[4,4,2,128]{3,2,1,0:T(2,128)S(1)} %fusion.7), channel_id=1, source_target_pairs={{0,1},{1,0},{2,3},{3,2},{4,5},{5,4},{6,7},{7,6},{8,9},{9,8},{10,11... | collective-permute-start | bytes 49160 | tf_op jit(solution)/shard_map/ppermute | solution.py:200
  67.3 3.8 %collective-permute-start.5 = (f32[4,4,2,128]{3,2,1,0:T(2,128)S(1)}, f32[4,4,2,128]{3,2,1,0:T(2,128)S(1)}, u32[]{:S(2)}, u32[]{:S(2)}) collective-permute-start(f32[4,4,2,128]{3,2,1,0:T(2,128)S(1)} %add.208), channel_id=1, source_target_pairs={{0,2},{1,3},{2,0},{3,1},{4,6},{5,7},{6,4},{7,5},{8,10},{9,11},{10,... | collective-permute-start | bytes 49160 | tf_op jit(solution)/shard_map/ppermute | solution.py:200
  71.1 3.8 %collective-permute-start.6 = (f32[4,4,2,128]{3,2,1,0:T(2,128)S(1)}, f32[4,4,2,128]{3,2,1,0:T(2,128)S(1)}, u32[]{:S(2)}, u32[]{:S(2)}) collective-permute-start(f32[4,4,2,128]{3,2,1,0:T(2,128)S(1)} %add.210), channel_id=1, source_target_pairs={{0,4},{1,5},{2,6},{3,7},{4,0},{5,1},{6,2},{7,3},{8,12},{9,13},{10,... | collective-permute-start | bytes 49160 | tf_op jit(solution)/shard_map/ppermute | solution.py:200
  74.9 4.7 %collective-permute-start.7 = (f32[4,4,2,128]{3,2,1,0:T(2,128)S(1)}, f32[4,4,2,128]{3,2,1,0:T(2,128)S(1)}, u32[]{:S(2)}, u32[]{:S(2)}) collective-permute-start(f32[4,4,2,128]{3,2,1,0:T(2,128)S(1)} %add.212), channel_id=1, source_target_pairs={{0,8},{1,9},{2,10},{3,11},{4,12},{5,13},{6,14},{7,15},{8,0},{9,1},... | collective-permute-start | bytes 49160 | tf_op jit(solution)/shard_map/ppermute | solution.py:200

commit v3 on v2

--- a/solution.py
+++ b/solution.py
@@ -1,3 +1,5 @@
+import functools
+
 import jax
 import jax.numpy as jnp
 from jax import lax
@@ -73,12 +75,32 @@
     return result
 
 
-def unet_body(state_ref, wsp_ref, wt_ref, wl_ref, same_ref, batch_ref, out_ref):
-    rows, blocks, cols, chans = state_ref.shape
-    frames = blocks // 2
+def unet_body(
+    first_ref, emb_u_ref, time_ref, pooled_ref, tproj_ref, wl_ref, same_ref, batch_ref,
+    wsp_hbm, wt_hbm, out_ref, wsp_ref, wt_ref, sems, *, count
+):
+    rows, frames, cols, chans = first_ref.shape
+    blocks = 2 * frames
+    copy_sp = pltpu.make_async_copy(wsp_hbm, wsp_ref, sems.at[0])
+    copy_sp.start()
+    copy_tm = pltpu.make_async_copy(wt_hbm, wt_ref, sems.at[1])
+    copy_tm.start()
     same = same_ref[...]
     batch_mix = batch_ref[...]
     hi = lax.Precision.HIGHEST
+
+    pooled = pooled_ref[...] / count
+    average = jnp.mean(pooled, axis=1, keepdims=True)
+    spread = jnp.mean((pooled - average) ** 2, axis=1, keepdims=True)
+    text = ((pooled - average) * lax.rsqrt(spread + NORM_EPS)).astype(jnp.bfloat16)
+    text = jnp.broadcast_to(text, (8, text.shape[1]))
+    vector = jnp.dot(text, tproj_ref[...], preferred_element_type=jnp.float32)[0:1]
+    emb_c = (vector + time_ref[...]).reshape(1, 1, 1, chans)
+    emb_u = emb_u_ref[...].reshape(1, 1, 1, chans)
+    first = first_ref[...]
+    state = jnp.concatenate(
+        [(first + emb_c).astype(jnp.bfloat16), (first + emb_u).astype(jnp.bfloat16)], axis=1
+    )
 
     def group_stats(sums, count, mix):
         if mix is not None:
@@ -131,18 +153,22 @@
 
     per_frame = float(chans // GROUPS * rows * cols)
     per_sample = per_frame * frames
-    state = state_ref[...]
     for section in range(wsp_ref.shape[0]):
         x = state.astype(jnp.float32)
         normed = norm_silu(x, None, per_frame)
+        if section == 0:
+            copy_sp.wait()
         state = (x + conv_sp(normed, section)).astype(jnp.bfloat16)
         x = state.astype(jnp.float32)
         normed = norm_silu(x, batch_mix, per_sample)
+        if section == 0:
+            copy_tm.wait()
         state = (x + conv_tm(normed, section)).astype(jnp.bfloat16)
     last = norm_silu(state.astype(jnp.float32), None, per_frame)
     x0 = last[0].reshape(blocks * cols, chans)
     x1 = last[1].reshape(blocks * cols, chans)
-    lane = lax.broadcasted_iota(jnp.int32, (wl_ref.shape[1], blocks * cols), 1) % cols
+    stride = out_ref.shape[1]
+    lane = lax.broadcasted_iota(jnp.int32, (stride, blocks * cols), 1) % cols
 
     def mm_t(w, a):
         return lax.dot_general(w, a, (((1,), (1,)), ((), ())), preferred_element_type=jnp.float32)
@@ -150,31 +176,49 @@
     for row in range(rows):
         own, other = (x0, x1) if row == 0 else (x1, x0)
         other_dr = 1 if row == 0 else -1
+        y = mm_t(wl_ref[3 * stride : 6 * stride], own)
+        y = y + mm_t(wl_ref[(other_dr + 1) * 3 * stride : (other_dr + 2) * 3 * stride], other)
         acc = None
         for dc in (-1, 0, 1):
-            y = mm_t(wl_ref[3 + dc + 1], own) + mm_t(wl_ref[(other_dr + 1) * 3 + dc + 1], other)
+            part = y[(dc + 1) * stride : (dc + 2) * stride]
             if dc == -1:
-                y = jnp.where(lane == 0, 0.0, pltpu.roll(y, 1, 1))
+                part = jnp.where(lane == 0, 0.0, pltpu.roll(part, 1, 1))
             elif dc == 1:
-                y = jnp.where(lane == cols - 1, 0.0, pltpu.roll(y, blocks * cols - 1, 1))
-            acc = y if acc is None else acc + y
+                part = jnp.where(lane == cols - 1, 0.0, pltpu.roll(part, blocks * cols - 1, 1))
+            acc = part if acc is None else acc + part
         out_ref[row] = acc
 
 
-def unet_sections(state, spatial_weights, temporal_weights, conv_last):
-    rows, blocks, cols, chans = state.shape
+def unet(first, emb_u, time_vector, pooled, text_proj, spatial_weights, temporal_weights, conv_last, count):
+    rows, frames, cols, chans = first.shape
+    blocks = 2 * frames
     taps, outs, _ = conv_last.shape
     padded = -(-outs // 16) * 16
     last = jnp.concatenate([conv_last, jnp.zeros((taps, padded - outs, chans), conv_last.dtype)], axis=1)
+    last = last.reshape(taps * padded, chans)
     group = jnp.arange(chans) // (chans // GROUPS)
     same = (group[:, None] == group[None, :]).astype(jnp.float32)
-    block_of = jnp.arange(blocks) // (blocks // 2)
+    block_of = jnp.arange(blocks) // frames
     batch_mix = (block_of[:, None] == block_of[None, :]).astype(jnp.float32)
+    vmem = pl.BlockSpec(memory_space=pltpu.MemorySpace.VMEM)
+    anywhere = pl.BlockSpec(memory_space=pl.ANY)
     return pl.pallas_call(
-        unet_body,
+        functools.partial(unet_body, count=float(count)),
         out_shape=jax.ShapeDtypeStruct((rows, padded, blocks * cols), jnp.float32),
+        in_specs=[vmem] * 8 + [anywhere, anywhere],
+        out_specs=vmem,
+        scratch_shapes=[
+            pltpu.VMEM(spatial_weights.shape, spatial_weights.dtype),
+            pltpu.VMEM(temporal_weights.shape, temporal_weights.dtype),
+            pltpu.SemaphoreType.DMA((2,)),
+        ],
         compiler_params=pltpu.CompilerParams(vmem_limit_bytes=100 * 1024 * 1024 // 2),
-    )(state, spatial_weights, temporal_weights, last, same, batch_mix)[:, :outs]
+        cost_estimate=pl.CostEstimate(
+            flops=2 * rows * blocks * cols * chans * chans * 9 * spatial_weights.shape[0],
+            transcendentals=rows * blocks * cols * chans * 5,
+            bytes_accessed=spatial_weights.size * 2 + temporal_weights.size * 2 + first.size * 4,
+        ),
+    )(first, emb_u, time_vector, pooled, text_proj, last, same, batch_mix, spatial_weights, temporal_weights)[:, :outs]
 
 
 def butterfly_sum(x, axis):
@@ -226,9 +270,9 @@
     hits = local_ids[:, None] == jnp.arange(shard_rows, dtype=jnp.int32)[None, :]
     counts = jnp.sum(hits.astype(jnp.float32), axis=0).astype(jnp.bfloat16)[None]
     partial = jnp.dot(counts, token_table, preferred_element_type=jnp.float32)[0]
-    pooled = butterfly_sum(partial, "slot") / prompt_ids.shape[0]
-    text_pair = jnp.stack([layer_norm(pooled), layer_norm(empty_text)]).astype(jnp.bfloat16)
-    text_vector = jnp.dot(text_pair, text_proj, preferred_element_type=jnp.float32)
+    pooled = butterfly_sum(partial, "slot")[None]
+    text_uncond = layer_norm(empty_text).astype(jnp.bfloat16)[None]
+    vector_uncond = jnp.dot(text_uncond, text_proj, preferred_element_type=jnp.float32)
     half_width = time_in.shape[0] // 2
     frequency = jnp.exp(-jnp.log(10000.0) * jnp.arange(half_width, dtype=jnp.float32) / half_width)
     step_value = timesteps[0].astype(jnp.float32)
@@ -238,16 +282,14 @@
         jnp.bfloat16
     )
     time_vector = jnp.dot(hidden, time_out, preferred_element_type=jnp.float32)
-    embedding = text_vector + time_vector
     latent = iterate[0]
-    state = (
-        conv_space(latent.astype(jnp.bfloat16)[None], conv_first)
-        + embedding[:, :, None, None, None]
-    ).astype(jnp.bfloat16)
-    batch, chans, frames, rows, cols = state.shape
-    laid = state.transpose(3, 0, 2, 4, 1).reshape(rows, batch * frames, cols, chans)
-    predicted = unet_sections(laid, spatial_weights, temporal_weights, conv_last)
-    predicted = predicted.reshape(rows, -1, batch, frames, cols).transpose(2, 1, 3, 0, 4)
+    first = conv_space(latent.astype(jnp.bfloat16)[None], conv_first)[0].transpose(2, 1, 3, 0)
+    rows, frames, cols, chans = first.shape
+    predicted = unet(
+        first, vector_uncond + time_vector, time_vector, pooled, text_proj,
+        spatial_weights, temporal_weights, conv_last, prompt_ids.shape[0],
+    )
+    predicted = predicted.reshape(rows, -1, 2, frames, cols).transpose(2, 1, 3, 0, 4)
     guided = predicted[1] + GUIDANCE_SCALE * (predicted[0] - predicted[1])
     alpha_now = alpha_bar(step_value)
     alpha_prev = alpha_bar(step_value - DT)

time: 80.6 us -> 94.5 us (1.17)
  matrix products: 9.92 us -> 23 us
  starting transfers between devices: 13.3 us -> 15 us
  local copies, waits for them, and re-layouts: 3.48 us -> 5.01 us
  waiting for transfers between devices: 11.5 us -> 10 us
  between operations: 4.85 us -> 3.4 us
  Pallas kernels: 32.5 us -> 33.9 us
    dot_general x9, matrix products: 4.23 us -> 16 us  [conv_space(): jnp.einsum('oc,bcfrw->bofrw', weight[row_step * 3 + col_step], window, pr...]
    ppermute x4, waiting for transfers between devices: 8.39 us -> 6.6 us  [butterfly_scan(): got = lax.ppermute(total, axis, [(i, i ^ k) for i in range(peers)])]
    ppermute x4, starting transfers between devices: 5.16 us -> 6.95 us  [butterfly_scan(): got = lax.ppermute(total, axis, [(i, i ^ k) for i in range(peers)])]
    dot_general x1, matrix products: 0.34 us -> 2.07 us  [local(): time_vector = jnp.dot(hidden, time_out, preferred_element_type=jnp.float32)]
    pallas_call x1, Pallas kernels: 32.5 us -> 33.9 us  [unet(): pl.pallas_call(functools.partial(unet_body, count=float(count)), out_shap...]
    dot_general x1, matrix products: 1.38 us -> 0.33 us  [local(): jnp.dot(text_uncond, text_proj, preferred_element_type=jnp.float32)]
    add x4 -> x2, local copies, waits for them, and re-layouts: 2.13 us -> 2.94 us  [the longest x1 2.94 us: conv_space(): result = term if result is None else result + term]
  transfers between devices with their start and end apart: 8 -> 8, of which waited for: 6 -> 7; matrix products, arithmetic and copies ran while one was open for 10% -> 25% of each run, Pallas kernels for 0% -> 0%
where the time goes in v3:
time: 94.5 us; the launch traced here: 94.2 us
  Pallas kernels  33.9 us (36%)
  matrix products  23 us (24%)
  starting transfers between devices  15 us (16%)
  waiting for transfers between devices  10 us (11%)
  local copies, waits for them, and re-layouts  5.01 us (5%)
  other arithmetic  3.9 us (4%)
  between operations  3.4 us (4%)
    pallas_call x1, Pallas kernels, unet(): pl.pallas_call(functools.partial(unet_body, count=float(count)), out_shap...  33.9 us
    dot_general x9, matrix products, conv_space(): jnp.einsum('oc,bcfrw->bofrw', weight[row_step * 3 + col_step], window, pr...  16 us
    ppermute x4, starting transfers between devices, butterfly_sum(): x = x + lax.ppermute(x, axis, [(i, i ^ k) for i in range(peers)])  8.07 us
    ppermute x4, starting transfers between devices, butterfly_scan(): got = lax.ppermute(total, axis, [(i, i ^ k) for i in range(peers)])  6.95 us
    ppermute x4, waiting for transfers between devices, butterfly_scan(): got = lax.ppermute(total, axis, [(i, i ^ k) for i in range(peers)])  6.6 us
    dot_general x1, matrix products, local(): jnp.dot(counts, token_table, preferred_element_type=jnp.float32)[0]  4.33 us
    ppermute x4, waiting for transfers between devices, butterfly_sum(): x = x + lax.ppermute(x, axis, [(i, i ^ k) for i in range(peers)])  3.4 us
    add x1, local copies, waits for them, and re-layouts, conv_space(): result = term if result is None else result + term  2.94 us
  transfers between devices with their start and end apart: 8, of which 7 were waited for; matrix products, arithmetic and copies ran while one was open for 25% of the time, Pallas kernels for 0%

profile of v3, /device:TPU:0, one launch (start us, length us, event | category | flops | bytes accessed | tf_op | source)
XLA Modules:
  0.0 94.2 jit_solution(12515462562084579952)
XLA Ops:
  0.6 0.7 broadcast_subtract_fusion
  1.6 4.3 %fusion.57 = f32[1,1024]{1,0:T(1,128)} fusion(bf16[3088,1]{0,1:T(2,128)(2,1)S(1)} %reshape.162, bf16[3088,1024]{1,0:T(8,128)(2,1)} %param.19), kind=kOutput, calls=%fused_computation.95 | convolution fusion | flops 6324224 | bytes 6334496 | tf_op jit(solution)/shard_map/dot_general | solution.py:272
  6.0 0.5 collective-permute-start
  6.6 0.4 fusion.9
  7.0 0.4 fusion.28
  7.4 1.6 %fusion.24 = f32[4,2,128,320]{3,2,0,1:T(8,128)} fusion(bf16[9,320,4]{1,2,0:T(4,128)(2,1)S(1)} %copy-done.7, f32[1,4,4,2,128]{4,3,2,1,0:T(2,128)S(1)} %copy-done.3), kind=kOutput, calls=%fused_computation.44 | convolution fusion | flops 2621440 | bytes 1330176 | tf_op jit(solution)/shard_map/oc,bcfrw->bofrw/dot_general | solution.py:55
  9.0 1.4 %convolution_add_fusion = f32[4,2,128,320]{2,3,1,0:T(8,128)} fusion(f32[4,2,128,320]{2,3,1,0:T(8,128)S(1)} %fusion.9, bf16[9,320,4]{1,2,0:T(4,128)(2,1)S(1)} %copy-done.7, bf16[1,4,4,2,127]{4,1,3,2,0:T(4,128)(2,1)S(1)} %get-tuple-element.6), kind=kOutput, calls=%fused_computation.1 | convolution fusion | flops 2949120 | bytes 2632704 | tf_op jit(solution)/shard_map/oc,bcfrw->bofrw/dot_general | solution.py:55
  10.4 2.9 %copy.41 = f32[4,2,128,320]{3,2,0,1:T(8,128)} copy(f32[4,2,128,320]{2,3,1,0:T(8,128)} %convolution_add_fusion) | data formatting | bytes 2621440 | tf_op jit(solution)/shard_map/add | solution.py:61
  13.4 1.6 %fusion.20 = f32[4,2,128,320]{3,2,0,1:T(8,128)} fusion(bf16[4,4,2,128]{3,0,2,1:T(4,128)(2,1)S(1)} %get-tuple-element.5, bf16[9,320,4]{1,2,0:T(4,128)(2,1)S(1)} %copy-done.7), kind=kOutput, calls=%fused_computation.40 | convolution fusion | flops 2621440 | bytes 1321984 | tf_op jit(solution)/shard_map/oc,bcfrw->bofrw/dot_general | solution.py:55
  15.0 1.7 %fusion.18 = f32[4,2,128,320]{3,2,0,1:T(8,128)} fusion(bf16[4,4,2,128]{3,0,2,1:T(4,128)(2,1)S(1)} %get-tuple-element.11, bf16[9,320,4]{1,2,0:T(4,128)(2,1)S(1)} %copy-done.7), kind=kOutput, calls=%fused_computation.38 | convolution fusion | flops 2621440 | bytes 1321984 | tf_op jit(solution)/shard_map/oc,bcfrw->bofrw/dot_general | solution.py:55
  16.6 1.6 %fusion.22 = f32[4,2,128,320]{3,2,0,1:T(8,128)} fusion(bf16[4,4,2,128]{3,0,2,1:T(4,128)(2,1)S(1)} %get-tuple-element.9, bf16[9,320,4]{1,2,0:T(4,128)(2,1)S(1)} %copy-done.7), kind=kOutput, calls=%fused_computation.42 | convolution fusion | flops 2621440 | bytes 1321984 | tf_op jit(solution)/shard_map/oc,bcfrw->bofrw/dot_general | solution.py:55
  18.2 1.6 %fusion.26 = f32[4,2,128,320]{3,2,0,1:T(8,128)} fusion(bf16[4,4,2,128]{3,0,2,1:T(4,128)(2,1)S(1)} %get-tuple-element.8, bf16[9,320,4]{1,2,0:T(4,128)(2,1)S(1)} %copy-done.7), kind=kOutput, calls=%fused_computation.46 | convolution fusion | flops 2621440 | bytes 1321984 | tf_op jit(solution)/shard_map/oc,bcfrw->bofrw/dot_general | solution.py:55
  20.8 0.6 reduce_sum.27
  22.1 0.6 multiply_reduce_fusion
  23.5 2.1 %fusion.55 = (f32[320]{0:T(512)}, f32[1,320]{1,0:T(1,128)S(1)}) fusion(bf16[1280,1]{0,1:T(2,128)(2,1)S(1)} %reshape.160, bf16[1280,320]{0,1:T(8,128)(2,1)} %param.22), kind=kOutput, calls=%fused_computation.93 | convolution fusion | flops 819200 | bytes 824320 | tf_op jit(solution)/shard_map/dot_general | solution.py:284
  25.6 5.9 %add_bitcast_fusion.first_ref = f32[2,4,128,320]{3,2,1,0:T(8,128)} fusion(f32[4,2,128,320]{3,2,0,1:T(8,128)} %fusion.18, f32[4,2,128,320]{3,2,0,1:T(8,128)} %fusion.20, f32[4,2,128,320]{3,2,0,1:T(8,128)} %fusion.22, f32[4,2,128,320]{3,2,0,1:T(8,128)} %fusion.24, f32[4,2,128,320]{3,2,0,1:T(8,128)} %fusion.26, f32[4,2,128,320]{3,2,0,1:T(8,128)} %copy.41, ...), kind=kOutput, calls=%fused_computation | convolution fusion | flops 4915200 | bytes 12069888 | tf_op jit(solution)/shard_map/oc,bcfrw->bofrw/dot_general | solution.py:55
  31.4 0.7 add.153
  32.2 2.5 %collective-permute-start.1 = (f32[1024]{0:T(1024)S(1)}, f32[1024]{0:T(1024)S(1)}, u32[]{:S(2)}, u32[]{:S(2)}) collective-permute-start(f32[1024]{0:T(1024)S(1)} %add.153), channel_id=1, source_target_pairs={{0,2},{1,3},{2,0},{3,1},{4,6},{5,7},{6,4},{7,5},{8,10},{9,11},{10,... | collective-permute-start | bytes 12296 | tf_op jit(solution)/shard_map/ppermute | solution.py:230
  34.7 1.6 %collective-permute-done.1 = f32[1024]{0:T(1024)S(1)} collective-permute-done((f32[1024]{0:T(1024)S(1)}, f32[1024]{0:T(1024)S(1)}, u32[]{:S(2)}, u32[]{:S(2)}) %collective-permute-start.1) | collective-permute-done | bytes 4128 | tf_op jit(solution)/shard_map/ppermute | solution.py:230
  36.3 2.1 %collective-permute-start.2 = (f32[1024]{0:T(1024)S(1)}, f32[1024]{0:T(1024)S(1)}, u32[]{:S(2)}, u32[]{:S(2)}) collective-permute-start(f32[1024]{0:T(1024)S(1)} %add.154), channel_id=1, source_target_pairs={{0,4},{1,5},{2,6},{3,7},{4,0},{5,1},{6,2},{7,3},{8,12},{9,13},{10,... | collective-permute-start | bytes 12296 | tf_op jit(solution)/shard_map/ppermute | solution.py:230
  38.4 1.5 %collective-permute-done.2 = f32[1024]{0:T(1024)S(1)} collective-permute-done((f32[1024]{0:T(1024)S(1)}, f32[1024]{0:T(1024)S(1)}, u32[]{:S(2)}, u32[]{:S(2)}) %collective-permute-start.2) | collective-permute-done | bytes 4128 | tf_op jit(solution)/shard_map/ppermute | solution.py:230
  39.9 3.0 %collective-permute-start.3 = (f32[1024]{0:T(1024)S(1)}, f32[1024]{0:T(1024)S(1)}, u32[]{:S(2)}, u32[]{:S(2)}) collective-permute-start(f32[1024]{0:T(1024)S(1)} %add.155), channel_id=1, source_target_pairs={{0,8},{1,9},{2,10},{3,11},{4,12},{5,13},{6,14},{7,15},{8,0},{9,1},... | collective-permute-start | bytes 12296 | tf_op jit(solution)/shard_map/ppermute | solution.py:230
  44.5 1.4 %copy-done.1 = bf16[2,3,320,320]{3,2,1,0:T(8,128)(2,1)S(1)} copy-done((bf16[2,3,320,320]{3,2,1,0:T(8,128)(2,1)S(1)}, bf16[2,3,320,320]{3,2,1,0:T(8,128)(2,1)}, u32[]{:S(2)}) %copy-start.1) | copy-done | bytes 1228824
  45.9 33.9 %shard_map.149 = f32[2,16,1024]{2,1,0:T(8,128)S(1)} custom-call(f32[2,4,128,320]{3,2,1,0:T(8,128)} %add_bitcast_fusion.first_ref, f32[1,320]{1,0:T(1,128)S(1)} %add.152.emb_u_ref, f32[1,320]{1,0:T(1,128)S(1)} %get-tuple-element.13.time_ref, f32[1,1024]{1,0:T(1,128)S(1)} %bitcast.121, bf16[1024,320]{1,0:T(8,128)(2,1)S(1)} %copy.49.tproj_ref, ...), custom_call_target="tpu_custom_call" | custom-call | flops 7549747200 | bytes 6225920 | tf_op jit(solution)/shard_map/pallas_call | solution.py:205
  80.0 1.2 %collective-permute-done.4 = f32[4,4,2,128]{3,2,1,0:T(2,128)S(1)} collective-permute-done((f32[4,4,2,128]{3,2,1,0:T(2,128)S(1)}, f32[4,4,2,128]{3,2,1,0:T(2,128)S(1)}, u32[]{:S(2)}, u32[]{:S(2)}) %collective-permute-start.4) | collective-permute-done | bytes 16416 | tf_op jit(solution)/shard_map/ppermute | solution.py:244
  81.2 1.9 %collective-permute-start.5 = (f32[4,4,2,128]{3,2,1,0:T(2,128)S(1)}, f32[4,4,2,128]{3,2,1,0:T(2,128)S(1)}, u32[]{:S(2)}, u32[]{:S(2)}) collective-permute-start(f32[4,4,2,128]{3,2,1,0:T(2,128)S(1)} %add.160), channel_id=1, source_target_pairs={{0,2},{1,3},{2,0},{3,1},{4,6},{5,7},{6,4},{7,5},{8,10},{9,11},{10,... | collective-permute-start | bytes 49160 | tf_op jit(solution)/shard_map/ppermute | solution.py:244
  83.1 1.9 %collective-permute-done.5 = f32[4,4,2,128]{3,2,1,0:T(2,128)S(1)} collective-permute-done((f32[4,4,2,128]{3,2,1,0:T(2,128)S(1)}, f32[4,4,2,128]{3,2,1,0:T(2,128)S(1)}, u32[]{:S(2)}, u32[]{:S(2)}) %collective-permute-start.5) | collective-permute-done | bytes 16416 | tf_op jit(solution)/shard_map/ppermute | solution.py:244
  85.0 2.0 %collective-permute-start.6 = (f32[4,4,2,128]{3,2,1,0:T(2,128)S(1)}, f32[4,4,2,128]{3,2,1,0:T(2,128)S(1)}, u32[]{:S(2)}, u32[]{:S(2)}) collective-permute-start(f32[4,4,2,128]{3,2,1,0:T(2,128)S(1)} %add.162), channel_id=1, source_target_pairs={{0,4},{1,5},{2,6},{3,7},{4,0},{5,1},{6,2},{7,3},{8,12},{9,13},{10,... | collective-permute-start | bytes 49160 | tf_op jit(solution)/shard_map/ppermute | solution.py:244
  87.0 1.8 %collective-permute-done.6 = f32[4,4,2,128]{3,2,1,0:T(2,128)S(1)} collective-permute-done((f32[4,4,2,128]{3,2,1,0:T(2,128)S(1)}, f32[4,4,2,128]{3,2,1,0:T(2,128)S(1)}, u32[]{:S(2)}, u32[]{:S(2)}) %collective-permute-start.6) | collective-permute-done | bytes 16416 | tf_op jit(solution)/shard_map/ppermute | solution.py:244
  88.8 3.0 %collective-permute-start.7 = (f32[4,4,2,128]{3,2,1,0:T(2,128)S(1)}, f32[4,4,2,128]{3,2,1,0:T(2,128)S(1)}, u32[]{:S(2)}, u32[]{:S(2)}) collective-permute-start(f32[4,4,2,128]{3,2,1,0:T(2,128)S(1)} %add.164), channel_id=1, source_target_pairs={{0,8},{1,9},{2,10},{3,11},{4,12},{5,13},{6,14},{7,15},{8,0},{9,1},... | collective-permute-start | bytes 49160 | tf_op jit(solution)/shard_map/ppermute | solution.py:244
  91.8 1.7 %collective-permute-done.7 = f32[4,4,2,128]{3,2,1,0:T(2,128)S(1)} collective-permute-done((f32[4,4,2,128]{3,2,1,0:T(2,128)S(1)}, f32[4,4,2,128]{3,2,1,0:T(2,128)S(1)}, u32[]{:S(2)}, u32[]{:S(2)}) %collective-permute-start.7) | collective-permute-done | bytes 16416 | tf_op jit(solution)/shard_map/ppermute | solution.py:244
  93.5 0.6 add_add_fusion
  (59 shorter events, 2.3 us)
Async XLA Ops:
  0.6 19.9 %copy-start = (bf16[320,1280]{1,0:T(8,128)(2,1)S(1)}, bf16[320,1280]{1,0:T(8,128)(2,1)}, u32[]{:S(2)}) copy-start(bf16[320,1280]{1,0:T(8,128)(2,1)} %param.21) | copy-start | bytes 2457604
  1.6 4.8 %copy-start.3 = (f32[1,4,4,2,128]{4,3,2,1,0:T(2,128)S(1)}, f32[1,4,4,2,128]{4,3,2,1,0:T(2,128)}, u32[]{:S(2)}) copy-start(f32[1,4,4,2,128]{4,3,2,1,0:T(2,128)} %param.17) | copy-start | bytes 49156
  1.6 5.0 %copy-start.7 = (bf16[9,320,4]{1,2,0:T(4,128)(2,1)S(1)}, bf16[9,320,4]{1,2,0:T(4,128)(2,1)}, u32[]{:S(2)}) copy-start(bf16[9,320,4]{1,2,0:T(4,128)(2,1)} %param.24) | copy-start | bytes 69124
  6.0 25.5 %collective-permute-start = (f32[1024]{0:T(1024)}, f32[1024]{0:T(1024)}, u32[]{:S(2)}, u32[]{:S(2)}) collective-permute-start(f32[1024]{0:T(1024)} %bitcast.35), channel_id=1, source_target_pairs={{0,1},{1,0},{2,3},{3,2},{4,5},{5,4},{6,7},{7,6},{8,9},{9,8},{10,11... | collective-permute-start | bytes 12296 | tf_op jit(solution)/shard_map/ppermute | solution.py:230
  18.2 2.6 %copy-start.5 = (f32[1024]{0:T(1024)S(1)}, f32[1024]{0:T(1024)}, u32[]{:S(2)}) copy-start(f32[1024]{0:T(1024)} %param.20) | copy-start | bytes 12292
  25.6 17.4 %copy-start.2 = (bf16[1024,320]{0,1:T(8,128)(2,1)S(1)}, bf16[1024,320]{0,1:T(8,128)(2,1)}, u32[]{:S(2)}) copy-start(bf16[1024,320]{0,1:T(8,128)(2,1)} %param.23) | copy-start | bytes 1966084
  31.4 12.5 %copy-start.10 = (f32[320]{0:T(512)S(1)}, f32[320]{0:T(512)}, u32[]{:S(2)}) copy-start(f32[320]{0:T(512)} %get-tuple-element.12) | copy-start | bytes 3844
  31.4 12.5 %copy-start.6 = (bf16[9,4,320]{2,1,0:T(4,128)(2,1)S(1)}, bf16[9,4,320]{2,1,0:T(4,128)(2,1)}, u32[]{:S(2)}) copy-start(bf16[9,4,320]{2,1,0:T(4,128)(2,1)} %param.27) | copy-start | bytes 69124
  32.2 4.1 %collective-permute-start.1 = (f32[1024]{0:T(1024)S(1)}, f32[1024]{0:T(1024)S(1)}, u32[]{:S(2)}, u32[]{:S(2)}) collective-permute-start(f32[1024]{0:T(1024)S(1)} %add.153), channel_id=1, source_target_pairs={{0,2},{1,3},{2,0},{3,1},{4,6},{5,7},{6,4},{7,5},{8,10},{9,11},{10,... | collective-permute-start | bytes 12296 | tf_op jit(solution)/shard_map/ppermute | solution.py:230
  36.3 3.7 %collective-permute-start.2 = (f32[1024]{0:T(1024)S(1)}, f32[1024]{0:T(1024)S(1)}, u32[]{:S(2)}, u32[]{:S(2)}) collective-permute-start(f32[1024]{0:T(1024)S(1)} %add.154), channel_id=1, source_target_pairs={{0,4},{1,5},{2,6},{3,7},{4,0},{5,1},{6,2},{7,3},{8,12},{9,13},{10,... | collective-permute-start | bytes 12296 | tf_op jit(solution)/shard_map/ppermute | solution.py:230
  39.9 4.6 %collective-permute-start.3 = (f32[1024]{0:T(1024)S(1)}, f32[1024]{0:T(1024)S(1)}, u32[]{:S(2)}, u32[]{:S(2)}) collective-permute-start(f32[1024]{0:T(1024)S(1)} %add.155), channel_id=1, source_target_pairs={{0,8},{1,9},{2,10},{3,11},{4,12},{5,13},{6,14},{7,15},{8,0},{9,1},... | collective-permute-start | bytes 12296 | tf_op jit(solution)/shard_map/ppermute | solution.py:230
  44.5 1.4 %copy-start.1 = (bf16[2,3,320,320]{3,2,1,0:T(8,128)(2,1)S(1)}, bf16[2,3,320,320]{3,2,1,0:T(8,128)(2,1)}, u32[]{:S(2)}) copy-start(bf16[2,3,320,320]{3,2,1,0:T(8,128)(2,1)} %wt_hbm.1) | copy-start | bytes 3686404
  45.9 34.0 %copy-start.4 = (f32[1,4,4,2,128]{4,3,2,1,0:T(2,128)S(1)}, f32[1,4,4,2,128]{4,3,2,1,0:T(2,128)}, u32[]{:S(2)}) copy-start(f32[1,4,4,2,128]{4,3,2,1,0:T(2,128)} %param.17) | copy-start | bytes 49156
  45.9 34.0 %copy-start.8 = (f32[1,4,4,2,128]{4,3,2,1,0:T(2,128)S(1)}, f32[1,4,4,2,128]{4,3,2,1,0:T(2,128)}, u32[]{:S(2)}) copy-start(f32[1,4,4,2,128]{4,3,2,1,0:T(2,128)} %param.18) | copy-start | bytes 49156
  45.9 47.6 %copy-start.9 = (f32[4,4,2,128]{3,2,1,0:T(2,128)S(1)}, f32[4,4,2,128]{3,2,1,0:T(2,128)}, u32[]{:S(2)}) copy-start(f32[4,4,2,128]{3,2,1,0:T(2,128)} %param.16) | copy-start | bytes 49156
  79.9 1.2 %collective-permute-start.4 = (f32[4,4,2,128]{3,2,1,0:T(2,128)S(1)}, f32[4,4,2,128]{3,2,1,0:T(2,128)S(1)}, u32[]{:S(2)}, u32[]{:S(2)}) collective-permute-start(f32[4,4,2,128]{3,2,1,0:T(2,128)S(1)} %fusion.6), channel_id=1, source_target_pairs={{0,1},{1,0},{2,3},{3,2},{4,5},{5,4},{6,7},{7,6},{8,9},{9,8},{10,11... | collective-permute-start | bytes 49160 | tf_op jit(solution)/shard_map/ppermute | solution.py:244
  81.2 3.8 %collective-permute-start.5 = (f32[4,4,2,128]{3,2,1,0:T(2,128)S(1)}, f32[4,4,2,128]{3,2,1,0:T(2,128)S(1)}, u32[]{:S(2)}, u32[]{:S(2)}) collective-permute-start(f32[4,4,2,128]{3,2,1,0:T(2,128)S(1)} %add.160), channel_id=1, source_target_pairs={{0,2},{1,3},{2,0},{3,1},{4,6},{5,7},{6,4},{7,5},{8,10},{9,11},{10,... | collective-permute-start | bytes 49160 | tf_op jit(solution)/shard_map/ppermute | solution.py:244
  85.0 3.8 %collective-permute-start.6 = (f32[4,4,2,128]{3,2,1,0:T(2,128)S(1)}, f32[4,4,2,128]{3,2,1,0:T(2,128)S(1)}, u32[]{:S(2)}, u32[]{:S(2)}) collective-permute-start(f32[4,4,2,128]{3,2,1,0:T(2,128)S(1)} %add.162), channel_id=1, source_target_pairs={{0,4},{1,5},{2,6},{3,7},{4,0},{5,1},{6,2},{7,3},{8,12},{9,13},{10,... | collective-permute-start | bytes 49160 | tf_op jit(solution)/shard_map/ppermute | solution.py:244
  88.8 4.7 %collective-permute-start.7 = (f32[4,4,2,128]{3,2,1,0:T(2,128)S(1)}, f32[4,4,2,128]{3,2,1,0:T(2,128)S(1)}, u32[]{:S(2)}, u32[]{:S(2)}) collective-permute-start(f32[4,4,2,128]{3,2,1,0:T(2,128)S(1)} %add.164), channel_id=1, source_target_pairs={{0,8},{1,9},{2,10},{3,11},{4,12},{5,13},{6,14},{7,15},{8,0},{9,1},... | collective-permute-start | bytes 49160 | tf_op jit(solution)/shard_map/ppermute | solution.py:244

commit v4 on v3

--- a/solution.py
+++ b/solution.py
@@ -60,6 +60,18 @@
             )
             result = term if result is None else result + term
     return result
+
+
+def conv_lifted(inputs, weight):
+    row_count, col_count = inputs.shape[2], inputs.shape[3]
+    padded = jnp.pad(inputs, ((0, 0), (0, 0), (1, 1), (1, 1)))
+    windows = jnp.concatenate(
+        [padded[:, :, tap // 3 : tap // 3 + row_count, tap % 3 : tap % 3 + col_count] for tap in range(9)],
+        axis=0,
+    )
+    stacked = weight.transpose(1, 0, 2).reshape(weight.shape[1], -1)
+    result = lax.dot_general(windows, stacked, (((0,), (1,)), ((), ())), preferred_element_type=jnp.float32)
+    return result.transpose(1, 0, 2, 3)
 
 
 def conv_time(inputs, weight):
@@ -283,7 +295,7 @@
     )
     time_vector = jnp.dot(hidden, time_out, preferred_element_type=jnp.float32)
     latent = iterate[0]
-    first = conv_space(latent.astype(jnp.bfloat16)[None], conv_first)[0].transpose(2, 1, 3, 0)
+    first = conv_lifted(latent.astype(jnp.bfloat16), conv_first)
     rows, frames, cols, chans = first.shape
     predicted = unet(
         first, vector_uncond + time_vector, time_vector, pooled, text_proj,

time: 94.5 us -> 74.3 us (0.79)
  matrix products: 23 us -> 6.2 us
  local copies, waits for them, and re-layouts: 5.01 us -> 2.15 us
    dot_general x9 -> x1, matrix products: 16 us -> 1.56 us  [conv_lifted(): lax.dot_general(windows, stacked, (((0,), (1,)), ((), ())), preferred_ele...]
    add x1 -> x0, local copies, waits for them, and re-layouts: 2.94 us -> none  [conv_space(): result = term if result is None else result + term]
    dot_general x1, matrix products: 2.07 us -> 0.34 us  [local(): time_vector = jnp.dot(hidden, time_out, preferred_element_type=jnp.float32)]
  transfers between devices with their start and end apart: 8 -> 8, of which waited for: 7 -> 7; matrix products, arithmetic and copies ran while one was open for 25% -> 6% of each run, Pallas kernels for 0% -> 0%
where the time goes in v4:
time: 74.3 us; the launch traced here: 74 us
  Pallas kernels  33.8 us (45%)
  starting transfers between devices  15.1 us (20%)
  waiting for transfers between devices  10 us (13%)
  matrix products  6.2 us (8%)
  between operations  3.42 us (5%)
  other arithmetic  3.28 us (4%)
  local copies, waits for them, and re-layouts  2.15 us (3%)
    pallas_call x1, Pallas kernels, unet(): pl.pallas_call(functools.partial(unet_body, count=float(count)), out_shap...  33.8 us
    ppermute x4, starting transfers between devices, butterfly_sum(): x = x + lax.ppermute(x, axis, [(i, i ^ k) for i in range(peers)])  8.16 us
    ppermute x4, starting transfers between devices, butterfly_scan(): got = lax.ppermute(total, axis, [(i, i ^ k) for i in range(peers)])  6.96 us
    ppermute x4, waiting for transfers between devices, butterfly_scan(): got = lax.ppermute(total, axis, [(i, i ^ k) for i in range(peers)])  6.6 us
    dot_general x1, matrix products, local(): jnp.dot(counts, token_table, preferred_element_type=jnp.float32)[0]  3.73 us
    ppermute x4, waiting for transfers between devices, butterfly_sum(): x = x + lax.ppermute(x, axis, [(i, i ^ k) for i in range(peers)])  3.41 us
    unnamed x22, local copies, waits for them, and re-layouts  1.78 us
    dot_general x1, matrix products, conv_lifted(): lax.dot_general(windows, stacked, (((0,), (1,)), ((), ())), preferred_ele...  1.56 us
  transfers between devices with their start and end apart: 8, of which 7 were waited for; matrix products, arithmetic and copies ran while one was open for 6% of the time, Pallas kernels for 0%

profile of v4, /device:TPU:0, one launch (start us, length us, event | category | flops | bytes accessed | tf_op | source)
XLA Modules:
  0.0 74.0 jit_solution(2824410981013497801)
XLA Ops:
  0.7 0.8 %broadcast_subtract_fusion = s32[77]{0:T(128)S(1)} fusion(s32[77]{0:T(128)} %param.15, s32[]{:T(128)S(6)} %mul.88), kind=kLoop, calls=%fused_computation.51 | loop fusion | flops 77 | bytes 620 | tf_op jit(solution)/shard_map/sub | solution.py:281
  1.5 0.2 convert_reduce_fusion
  1.7 3.7 %fusion.14 = f32[1,1024]{1,0:T(1,128)S(1)} fusion(bf16[3088,1]{0,1:T(2,128)(2,1)S(1)} %reshape.106, bf16[3088,1024]{1,0:T(8,128)(2,1)} %param.19), kind=kOutput, calls=%fused_computation.53 | convolution fusion | flops 6324224 | bytes 6334496 | tf_op jit(solution)/shard_map/dot_general | solution.py:284
  5.5 0.5 collective-permute-start
  6.0 0.1 pad_slice_fusion
  6.8 0.1 pad_maximum_fusion
  6.9 0.2 convolution_reduce_fusion
  7.2 0.6 reduce_sum.27
  8.4 0.6 multiply_reduce_fusion
  9.7 0.1 compare_convert_fusion.same_ref
  9.8 0.2 concatenate.11
  10.0 1.6 %convolution_bitcast_fusion.first_ref = f32[2,4,128,320]{3,2,1,0:T(8,128)} fusion(bf16[320,36,1,1]{0,1,2,3:T(8,128)(2,1)S(1)} %reshape.99, bf16[36,4,2,128]{3,0,2,1:T(8,128)(2,1)S(1)} %concatenate.11), kind=kOutput, calls=%fused_computation | convolution fusion | flops 23592960 | bytes 1407488 | tf_op jit(solution)/shard_map/dot_general | solution.py:73
  11.6 0.3 fusion.13
  11.9 2.6 %collective-permute-start.1 = (f32[1024]{0:T(1024)S(1)}, f32[1024]{0:T(1024)S(1)}, u32[]{:S(2)}, u32[]{:S(2)}) collective-permute-start(f32[1024]{0:T(1024)S(1)} %add.100), channel_id=1, source_target_pairs={{0,2},{1,3},{2,0},{3,1},{4,6},{5,7},{6,4},{7,5},{8,10},{9,11},{10,... | collective-permute-start | bytes 12296 | tf_op jit(solution)/shard_map/ppermute | solution.py:242
  14.5 1.6 %collective-permute-done.1 = f32[1024]{0:T(1024)S(1)} collective-permute-done((f32[1024]{0:T(1024)S(1)}, f32[1024]{0:T(1024)S(1)}, u32[]{:S(2)}, u32[]{:S(2)}) %collective-permute-start.1) | collective-permute-done | bytes 4128 | tf_op jit(solution)/shard_map/ppermute | solution.py:242
  16.1 2.1 %collective-permute-start.2 = (f32[1024]{0:T(1024)S(1)}, f32[1024]{0:T(1024)S(1)}, u32[]{:S(2)}, u32[]{:S(2)}) collective-permute-start(f32[1024]{0:T(1024)S(1)} %add.101), channel_id=1, source_target_pairs={{0,4},{1,5},{2,6},{3,7},{4,0},{5,1},{6,2},{7,3},{8,12},{9,13},{10,... | collective-permute-start | bytes 12296 | tf_op jit(solution)/shard_map/ppermute | solution.py:242
  18.3 1.5 %collective-permute-done.2 = f32[1024]{0:T(1024)S(1)} collective-permute-done((f32[1024]{0:T(1024)S(1)}, f32[1024]{0:T(1024)S(1)}, u32[]{:S(2)}, u32[]{:S(2)}) %collective-permute-start.2) | collective-permute-done | bytes 4128 | tf_op jit(solution)/shard_map/ppermute | solution.py:242
  19.8 3.0 %collective-permute-start.3 = (f32[1024]{0:T(1024)S(1)}, f32[1024]{0:T(1024)S(1)}, u32[]{:S(2)}, u32[]{:S(2)}) collective-permute-start(f32[1024]{0:T(1024)S(1)} %add.102), channel_id=1, source_target_pairs={{0,8},{1,9},{2,10},{3,11},{4,12},{5,13},{6,14},{7,15},{8,0},{9,1},... | collective-permute-start | bytes 12296 | tf_op jit(solution)/shard_map/ppermute | solution.py:242
  22.8 0.3 convolution_reduce_fusion.1
  23.1 0.4 copy.22.tproj_ref
  24.1 0.3 collective-permute-done.3
  24.4 1.4 %copy-done.1 = bf16[2,3,320,320]{3,2,1,0:T(8,128)(2,1)S(1)} copy-done((bf16[2,3,320,320]{3,2,1,0:T(8,128)(2,1)S(1)}, bf16[2,3,320,320]{3,2,1,0:T(8,128)(2,1)}, u32[]{:S(2)}) %copy-start.1) | copy-done | bytes 1228824
  25.8 33.8 %shard_map.149 = f32[2,16,1024]{2,1,0:T(8,128)S(1)} custom-call(f32[2,4,128,320]{3,2,1,0:T(8,128)} %convolution_bitcast_fusion.first_ref, f32[1,320]{1,0:T(1,128)S(1)} %add.99.emb_u_ref, f32[1,320]{1,0:T(1,128)S(1)} %get-tuple-element.13.time_ref, f32[1,1024]{1,0:T(1,128)S(1)} %bitcast.49, bf16[1024,320]{1,0:T(8,128)(2,1)S(1)} %copy.22.tproj_ref, ...), custom_call_target="tpu_custom_call" | custom-call | flops 7549747200 | bytes 6225920 | tf_op jit(solution)/shard_map/pallas_call | solution.py:217
  59.8 0.1 collective-permute-start.4
  59.8 1.2 %collective-permute-done.4 = f32[4,4,2,128]{3,2,1,0:T(2,128)S(1)} collective-permute-done((f32[4,4,2,128]{3,2,1,0:T(2,128)S(1)}, f32[4,4,2,128]{3,2,1,0:T(2,128)S(1)}, u32[]{:S(2)}, u32[]{:S(2)}) %collective-permute-start.4) | collective-permute-done | bytes 16416 | tf_op jit(solution)/shard_map/ppermute | solution.py:256
  61.0 1.9 %collective-permute-start.5 = (f32[4,4,2,128]{3,2,1,0:T(2,128)S(1)}, f32[4,4,2,128]{3,2,1,0:T(2,128)S(1)}, u32[]{:S(2)}, u32[]{:S(2)}) collective-permute-start(f32[4,4,2,128]{3,2,1,0:T(2,128)S(1)} %add.107), channel_id=1, source_target_pairs={{0,2},{1,3},{2,0},{3,1},{4,6},{5,7},{6,4},{7,5},{8,10},{9,11},{10,... | collective-permute-start | bytes 49160 | tf_op jit(solution)/shard_map/ppermute | solution.py:256
  62.9 1.9 %collective-permute-done.5 = f32[4,4,2,128]{3,2,1,0:T(2,128)S(1)} collective-permute-done((f32[4,4,2,128]{3,2,1,0:T(2,128)S(1)}, f32[4,4,2,128]{3,2,1,0:T(2,128)S(1)}, u32[]{:S(2)}, u32[]{:S(2)}) %collective-permute-start.5) | collective-permute-done | bytes 16416 | tf_op jit(solution)/shard_map/ppermute | solution.py:256
  64.8 2.0 %collective-permute-start.6 = (f32[4,4,2,128]{3,2,1,0:T(2,128)S(1)}, f32[4,4,2,128]{3,2,1,0:T(2,128)S(1)}, u32[]{:S(2)}, u32[]{:S(2)}) collective-permute-start(f32[4,4,2,128]{3,2,1,0:T(2,128)S(1)} %add.109), channel_id=1, source_target_pairs={{0,4},{1,5},{2,6},{3,7},{4,0},{5,1},{6,2},{7,3},{8,12},{9,13},{10,... | collective-permute-start | bytes 49160 | tf_op jit(solution)/shard_map/ppermute | solution.py:256
  66.8 1.8 %collective-permute-done.6 = f32[4,4,2,128]{3,2,1,0:T(2,128)S(1)} collective-permute-done((f32[4,4,2,128]{3,2,1,0:T(2,128)S(1)}, f32[4,4,2,128]{3,2,1,0:T(2,128)S(1)}, u32[]{:S(2)}, u32[]{:S(2)}) %collective-permute-start.6) | collective-permute-done | bytes 16416 | tf_op jit(solution)/shard_map/ppermute | solution.py:256
  68.7 3.0 %collective-permute-start.7 = (f32[4,4,2,128]{3,2,1,0:T(2,128)S(1)}, f32[4,4,2,128]{3,2,1,0:T(2,128)S(1)}, u32[]{:S(2)}, u32[]{:S(2)}) collective-permute-start(f32[4,4,2,128]{3,2,1,0:T(2,128)S(1)} %add.111), channel_id=1, source_target_pairs={{0,8},{1,9},{2,10},{3,11},{4,12},{5,13},{6,14},{7,15},{8,0},{9,1},... | collective-permute-start | bytes 49160 | tf_op jit(solution)/shard_map/ppermute | solution.py:256
  71.7 1.7 %collective-permute-done.7 = f32[4,4,2,128]{3,2,1,0:T(2,128)S(1)} collective-permute-done((f32[4,4,2,128]{3,2,1,0:T(2,128)S(1)}, f32[4,4,2,128]{3,2,1,0:T(2,128)S(1)}, u32[]{:S(2)}, u32[]{:S(2)}) %collective-permute-start.7) | collective-permute-done | bytes 16416 | tf_op jit(solution)/shard_map/ppermute | solution.py:256
  73.4 0.6 add_add_fusion
  (46 shorter events, 0.4 us)
Async XLA Ops:
  0.6 6.3 %copy-start = (bf16[320,1280]{1,0:T(8,128)(2,1)S(1)}, bf16[320,1280]{1,0:T(8,128)(2,1)}, u32[]{:S(2)}) copy-start(bf16[320,1280]{1,0:T(8,128)(2,1)} %param.21) | copy-start | bytes 2457604
  0.6 5.3 %copy-start.4 = (f32[1,4,4,2,128]{4,3,2,1,0:T(2,128)S(1)}, f32[1,4,4,2,128]{4,3,2,1,0:T(2,128)}, u32[]{:S(2)}) copy-start(f32[1,4,4,2,128]{4,3,2,1,0:T(2,128)} %param.17) | copy-start | bytes 49156
  0.7 5.4 %copy-start.6 = (bf16[9,320,4]{1,2,0:T(4,128)(2,1)S(1)}, bf16[9,320,4]{1,2,0:T(4,128)(2,1)}, u32[]{:S(2)}) copy-start(bf16[9,320,4]{1,2,0:T(4,128)(2,1)} %param.24) | copy-start | bytes 69124
  0.7 6.5 %copy-start.5 = (f32[1024]{0:T(1024)S(1)}, f32[1024]{0:T(1024)}, u32[]{:S(2)}) copy-start(f32[1024]{0:T(1024)} %param.20) | copy-start | bytes 12292
  0.7 10.9 %copy-start.3 = (bf16[1280,320]{0,1:T(8,128)(2,1)S(1)}, bf16[1280,320]{0,1:T(8,128)(2,1)}, u32[]{:S(2)}) copy-start(bf16[1280,320]{0,1:T(8,128)(2,1)} %param.22) | copy-start | bytes 2457604
  0.7 22.1 %copy-start.2 = (bf16[1024,320]{0,1:T(8,128)(2,1)S(1)}, bf16[1024,320]{0,1:T(8,128)(2,1)}, u32[]{:S(2)}) copy-start(bf16[1024,320]{0,1:T(8,128)(2,1)} %param.23) | copy-start | bytes 1966084
  1.7 22.3 %copy-start.7 = (bf16[9,4,320]{2,1,0:T(4,128)(2,1)S(1)}, bf16[9,4,320]{2,1,0:T(4,128)(2,1)}, u32[]{:S(2)}) copy-start(bf16[9,4,320]{2,1,0:T(4,128)(2,1)} %param.27) | copy-start | bytes 69124
  5.5 6.4 %collective-permute-start = (f32[1024]{0:T(1024)S(1)}, f32[1024]{0:T(1024)S(1)}, u32[]{:S(2)}, u32[]{:S(2)}) collective-permute-start(f32[1024]{0:T(1024)S(1)} %bitcast.54), channel_id=1, source_target_pairs={{0,1},{1,0},{2,3},{3,2},{4,5},{5,4},{6,7},{7,6},{8,9},{9,8},{10,11... | collective-permute-start | bytes 12296 | tf_op jit(solution)/shard_map/ppermute | solution.py:242
  11.9 4.2 %collective-permute-start.1 = (f32[1024]{0:T(1024)S(1)}, f32[1024]{0:T(1024)S(1)}, u32[]{:S(2)}, u32[]{:S(2)}) collective-permute-start(f32[1024]{0:T(1024)S(1)} %add.100), channel_id=1, source_target_pairs={{0,2},{1,3},{2,0},{3,1},{4,6},{5,7},{6,4},{7,5},{8,10},{9,11},{10,... | collective-permute-start | bytes 12296 | tf_op jit(solution)/shard_map/ppermute | solution.py:242
  16.1 3.7 %collective-permute-start.2 = (f32[1024]{0:T(1024)S(1)}, f32[1024]{0:T(1024)S(1)}, u32[]{:S(2)}, u32[]{:S(2)}) collective-permute-start(f32[1024]{0:T(1024)S(1)} %add.101), channel_id=1, source_target_pairs={{0,4},{1,5},{2,6},{3,7},{4,0},{5,1},{6,2},{7,3},{8,12},{9,13},{10,... | collective-permute-start | bytes 12296 | tf_op jit(solution)/shard_map/ppermute | solution.py:242
  19.8 4.6 %collective-permute-start.3 = (f32[1024]{0:T(1024)S(1)}, f32[1024]{0:T(1024)S(1)}, u32[]{:S(2)}, u32[]{:S(2)}) collective-permute-start(f32[1024]{0:T(1024)S(1)} %add.102), channel_id=1, source_target_pairs={{0,8},{1,9},{2,10},{3,11},{4,12},{5,13},{6,14},{7,15},{8,0},{9,1},... | collective-permute-start | bytes 12296 | tf_op jit(solution)/shard_map/ppermute | solution.py:242
  24.4 1.4 %copy-start.1 = (bf16[2,3,320,320]{3,2,1,0:T(8,128)(2,1)S(1)}, bf16[2,3,320,320]{3,2,1,0:T(8,128)(2,1)}, u32[]{:S(2)}) copy-start(bf16[2,3,320,320]{3,2,1,0:T(8,128)(2,1)} %wt_hbm.1) | copy-start | bytes 3686404
  25.8 33.9 %copy-start.8 = (f32[1,4,4,2,128]{4,3,2,1,0:T(2,128)S(1)}, f32[1,4,4,2,128]{4,3,2,1,0:T(2,128)}, u32[]{:S(2)}) copy-start(f32[1,4,4,2,128]{4,3,2,1,0:T(2,128)} %param.18) | copy-start | bytes 49156
  25.8 47.6 %copy-start.9 = (f32[4,4,2,128]{3,2,1,0:T(2,128)S(1)}, f32[4,4,2,128]{3,2,1,0:T(2,128)}, u32[]{:S(2)}) copy-start(f32[4,4,2,128]{3,2,1,0:T(2,128)} %param.16) | copy-start | bytes 49156
  59.8 1.2 %collective-permute-start.4 = (f32[4,4,2,128]{3,2,1,0:T(2,128)S(1)}, f32[4,4,2,128]{3,2,1,0:T(2,128)S(1)}, u32[]{:S(2)}, u32[]{:S(2)}) collective-permute-start(f32[4,4,2,128]{3,2,1,0:T(2,128)S(1)} %fusion.7), channel_id=1, source_target_pairs={{0,1},{1,0},{2,3},{3,2},{4,5},{5,4},{6,7},{7,6},{8,9},{9,8},{10,11... | collective-permute-start | bytes 49160 | tf_op jit(solution)/shard_map/ppermute | solution.py:256
  61.0 3.8 %collective-permute-start.5 = (f32[4,4,2,128]{3,2,1,0:T(2,128)S(1)}, f32[4,4,2,128]{3,2,1,0:T(2,128)S(1)}, u32[]{:S(2)}, u32[]{:S(2)}) collective-permute-start(f32[4,4,2,128]{3,2,1,0:T(2,128)S(1)} %add.107), channel_id=1, source_target_pairs={{0,2},{1,3},{2,0},{3,1},{4,6},{5,7},{6,4},{7,5},{8,10},{9,11},{10,... | collective-permute-start | bytes 49160 | tf_op jit(solution)/shard_map/ppermute | solution.py:256
  64.8 3.8 %collective-permute-start.6 = (f32[4,4,2,128]{3,2,1,0:T(2,128)S(1)}, f32[4,4,2,128]{3,2,1,0:T(2,128)S(1)}, u32[]{:S(2)}, u32[]{:S(2)}) collective-permute-start(f32[4,4,2,128]{3,2,1,0:T(2,128)S(1)} %add.109), channel_id=1, source_target_pairs={{0,4},{1,5},{2,6},{3,7},{4,0},{5,1},{6,2},{7,3},{8,12},{9,13},{10,... | collective-permute-start | bytes 49160 | tf_op jit(solution)/shard_map/ppermute | solution.py:256
  68.7 4.7 %collective-permute-start.7 = (f32[4,4,2,128]{3,2,1,0:T(2,128)S(1)}, f32[4,4,2,128]{3,2,1,0:T(2,128)S(1)}, u32[]{:S(2)}, u32[]{:S(2)}) collective-permute-start(f32[4,4,2,128]{3,2,1,0:T(2,128)S(1)} %add.111), channel_id=1, source_target_pairs={{0,8},{1,9},{2,10},{3,11},{4,12},{5,13},{6,14},{7,15},{8,0},{9,1},... | collective-permute-start | bytes 49160 | tf_op jit(solution)/shard_map/ppermute | solution.py:256

commit v5 on v4

--- a/solution.py
+++ b/solution.py
@@ -88,11 +88,11 @@
 
 
 def unet_body(
-    first_ref, emb_u_ref, time_ref, pooled_ref, tproj_ref, wl_ref, same_ref, batch_ref,
-    wsp_hbm, wt_hbm, out_ref, wsp_ref, wt_ref, sems, *, count
+    first_ref, emb_ref, time_ref, pooled_ref, tproj_ref, wl_ref, same_ref, batch_ref,
+    wsp_hbm, wt_hbm, out_ref, wsp_ref, wt_ref, sems, *, count, conditional
 ):
     rows, frames, cols, chans = first_ref.shape
-    blocks = 2 * frames
+    blocks = frames
     copy_sp = pltpu.make_async_copy(wsp_hbm, wsp_ref, sems.at[0])
     copy_sp.start()
     copy_tm = pltpu.make_async_copy(wt_hbm, wt_ref, sems.at[1])
@@ -101,18 +101,17 @@
     batch_mix = batch_ref[...]
     hi = lax.Precision.HIGHEST
 
-    pooled = pooled_ref[...] / count
-    average = jnp.mean(pooled, axis=1, keepdims=True)
-    spread = jnp.mean((pooled - average) ** 2, axis=1, keepdims=True)
-    text = ((pooled - average) * lax.rsqrt(spread + NORM_EPS)).astype(jnp.bfloat16)
-    text = jnp.broadcast_to(text, (8, text.shape[1]))
-    vector = jnp.dot(text, tproj_ref[...], preferred_element_type=jnp.float32)[0:1]
-    emb_c = (vector + time_ref[...]).reshape(1, 1, 1, chans)
-    emb_u = emb_u_ref[...].reshape(1, 1, 1, chans)
-    first = first_ref[...]
-    state = jnp.concatenate(
-        [(first + emb_c).astype(jnp.bfloat16), (first + emb_u).astype(jnp.bfloat16)], axis=1
-    )
+    if conditional:
+        pooled = pooled_ref[...] / count
+        average = jnp.mean(pooled, axis=1, keepdims=True)
+        spread = jnp.mean((pooled - average) ** 2, axis=1, keepdims=True)
+        text = ((pooled - average) * lax.rsqrt(spread + NORM_EPS)).astype(jnp.bfloat16)
+        text = jnp.broadcast_to(text, (8, text.shape[1]))
+        vector = jnp.dot(text, tproj_ref[...], preferred_element_type=jnp.float32)[0:1]
+        embedding = vector + time_ref[...]
+    else:
+        embedding = emb_ref[...]
+    state = (first_ref[...] + embedding.reshape(1, 1, 1, chans)).astype(jnp.bfloat16)
 
     def group_stats(sums, count, mix):
         if mix is not None:
@@ -153,10 +152,9 @@
         return jnp.stack(outs)
 
     def conv_tm(n, section):
-        n5 = n.reshape(rows, 2, frames, cols, chans)
-        blank = jnp.zeros((rows, 2, 1, cols, chans), n.dtype)
-        before = jnp.concatenate([blank, n5[:, :, :-1]], axis=2)
-        after = jnp.concatenate([n5[:, :, 1:], blank], axis=2)
+        blank = jnp.zeros((rows, 1, cols, chans), n.dtype)
+        before = jnp.concatenate([blank, n[:, :-1]], axis=1)
+        after = jnp.concatenate([n[:, 1:], blank], axis=1)
         flat = rows * blocks * cols
         acc = mm(before.reshape(flat, chans), wt_ref[section, 0])
         acc = acc + mm(n.reshape(flat, chans), wt_ref[section, 1])
@@ -201,9 +199,9 @@
         out_ref[row] = acc
 
 
-def unet(first, emb_u, time_vector, pooled, text_proj, spatial_weights, temporal_weights, conv_last, count):
+def unet(first, emb, time_vector, pooled, text_proj, spatial_weights, temporal_weights, conv_last, count, conditional):
     rows, frames, cols, chans = first.shape
-    blocks = 2 * frames
+    blocks = frames
     taps, outs, _ = conv_last.shape
     padded = -(-outs // 16) * 16
     last = jnp.concatenate([conv_last, jnp.zeros((taps, padded - outs, chans), conv_last.dtype)], axis=1)
@@ -215,7 +213,7 @@
     vmem = pl.BlockSpec(memory_space=pltpu.MemorySpace.VMEM)
     anywhere = pl.BlockSpec(memory_space=pl.ANY)
     return pl.pallas_call(
-        functools.partial(unet_body, count=float(count)),
+        functools.partial(unet_body, count=float(count), conditional=conditional),
         out_shape=jax.ShapeDtypeStruct((rows, padded, blocks * cols), jnp.float32),
         in_specs=[vmem] * 8 + [anywhere, anywhere],
         out_specs=vmem,
@@ -230,18 +228,21 @@
             transcendentals=rows * blocks * cols * chans * 5,
             bytes_accessed=spatial_weights.size * 2 + temporal_weights.size * 2 + first.size * 4,
         ),
-    )(first, emb_u, time_vector, pooled, text_proj, last, same, batch_mix, spatial_weights, temporal_weights)[:, :outs]
-
-
-def butterfly_sum(x, axis):
+    )(first, emb, time_vector, pooled, text_proj, last, same, batch_mix, spatial_weights, temporal_weights)[:, :outs]
+
+
+def butterfly_sum(x, axis, cover):
     peers = lax.axis_size(axis)
     if peers & (peers - 1):
-        return jnp.sum(lax.all_gather(x, axis), axis=0)
+        return jnp.sum(lax.all_gather(x, axis), axis=0), cover
     k = 1
     while k < peers:
-        x = x + lax.ppermute(x, axis, [(i, i ^ k) for i in range(peers)])
+        got = lax.ppermute(x, axis, [(i, i ^ k) for i in range(peers)])
+        if k == 1:
+            got, cover = lax.optimization_barrier((got, cover))
+        x = x + got
         k *= 2
-    return x
+    return x, cover
 
 
 def butterfly_scan(x, axis):
@@ -282,7 +283,6 @@
     hits = local_ids[:, None] == jnp.arange(shard_rows, dtype=jnp.int32)[None, :]
     counts = jnp.sum(hits.astype(jnp.float32), axis=0).astype(jnp.bfloat16)[None]
     partial = jnp.dot(counts, token_table, preferred_element_type=jnp.float32)[0]
-    pooled = butterfly_sum(partial, "slot")[None]
     text_uncond = layer_norm(empty_text).astype(jnp.bfloat16)[None]
     vector_uncond = jnp.dot(text_uncond, text_proj, preferred_element_type=jnp.float32)
     half_width = time_in.shape[0] // 2
@@ -297,11 +297,13 @@
     latent = iterate[0]
     first = conv_lifted(latent.astype(jnp.bfloat16), conv_first)
     rows, frames, cols, chans = first.shape
-    predicted = unet(
-        first, vector_uncond + time_vector, time_vector, pooled, text_proj,
-        spatial_weights, temporal_weights, conv_last, prompt_ids.shape[0],
-    )
-    predicted = predicted.reshape(rows, -1, 2, frames, cols).transpose(2, 1, 3, 0, 4)
+    weights = (spatial_weights, temporal_weights, conv_last, prompt_ids.shape[0])
+    emb_uncond = vector_uncond + time_vector
+    predicted_uncond = unet(first, emb_uncond, time_vector, emb_uncond, emb_uncond, *weights, False)
+    pooled, predicted_uncond = butterfly_sum(partial, "slot", predicted_uncond)
+    predicted_cond = unet(first, time_vector, time_vector, pooled[None], text_proj, *weights, True)
+    predicted = jnp.stack([predicted_cond, predicted_uncond])
+    predicted = predicted.reshape(2, rows, -1, frames, cols).transpose(0, 2, 3, 1, 4)
     guided = predicted[1] + GUIDANCE_SCALE * (predicted[0] - predicted[1])
     alpha_now = alpha_bar(step_value)
     alpha_prev = alpha_bar(step_value - DT)

time: 74.3 us -> 80.8 us (1.087)
  Pallas kernels: 33.8 us -> 39 us
  local copies, waits for them, and re-layouts: 2.15 us -> 4.08 us
  matrix products: 6.2 us -> 5.03 us
    pallas_call x1 -> x2, Pallas kernels: 33.8 us -> 39 us  [unet(): pl.pallas_call(functools.partial(unet_body, count=float(count), condition...]
    unnamed x22 -> x26, local copies, waits for them, and re-layouts: 1.78 us -> 3.7 us
    dot_general x1, matrix products: 1.56 us -> 0.4 us  [conv_lifted(): lax.dot_general(windows, stacked, (((0,), (1,)), ((), ())), preferred_ele...]
  transfers between devices with their start and end apart: 8 -> 8, of which waited for: 7 -> 7; matrix products, arithmetic and copies ran while one was open for 6% -> 4% of each run, Pallas kernels for 0% -> 23%
where the time goes in v5:
time: 80.8 us; the launch traced here: 80.5 us
  Pallas kernels  39 us (48%)
  starting transfers between devices  15.1 us (19%)
  waiting for transfers between devices  10.5 us (13%)
  matrix products  5.03 us (6%)
  local copies, waits for them, and re-layouts  4.08 us (5%)
  between operations  3.47 us (4%)
  other arithmetic  3.29 us (4%)
    pallas_call x2, Pallas kernels, unet(): pl.pallas_call(functools.partial(unet_body, count=float(count), condition...  39 us
    ppermute x4, starting transfers between devices, butterfly_sum(): got = lax.ppermute(x, axis, [(i, i ^ k) for i in range(peers)])  8.15 us
    ppermute x4, starting transfers between devices, butterfly_scan(): got = lax.ppermute(total, axis, [(i, i ^ k) for i in range(peers)])  6.96 us
    ppermute x4, waiting for transfers between devices, butterfly_scan(): got = lax.ppermute(total, axis, [(i, i ^ k) for i in range(peers)])  6.6 us
    ppermute x4, waiting for transfers between devices, butterfly_sum(): got = lax.ppermute(x, axis, [(i, i ^ k) for i in range(peers)])  3.86 us
    dot_general x1, matrix products, local(): jnp.dot(counts, token_table, preferred_element_type=jnp.float32)[0]  3.73 us
    unnamed x26, local copies, waits for them, and re-layouts  3.7 us
  transfers between devices with their start and end apart: 8, of which 7 were waited for; matrix products, arithmetic and copies ran while one was open for 4% of the time, Pallas kernels for 23%

profile of v5, /device:TPU:0, one launch (start us, length us, event | category | flops | bytes accessed | tf_op | source)
XLA Modules:
  0.0 80.5 jit_solution(3581288288770895197)
XLA Ops:
  0.7 0.8 %broadcast_subtract_fusion = s32[77]{0:T(128)S(1)} fusion(s32[77]{0:T(128)} %param.15, s32[]{:T(128)S(6)} %mul.86), kind=kLoop, calls=%fused_computation.51 | loop fusion | flops 77 | bytes 620 | tf_op jit(solution)/shard_map/sub | solution.py:282
  1.5 0.2 convert_reduce_fusion
  1.7 3.7 %fusion.14 = f32[1,1024]{1,0:T(1,128)S(1)} fusion(bf16[3088,1]{0,1:T(2,128)(2,1)S(1)} %reshape.106, bf16[3088,1024]{1,0:T(8,128)(2,1)} %param.19), kind=kOutput, calls=%fused_computation.53 | convolution fusion | flops 6324224 | bytes 6334496 | tf_op jit(solution)/shard_map/dot_general | solution.py:285
  5.5 0.5 collective-permute-start
  6.0 0.1 pad_slice_fusion
  6.1 0.6 reduce_sum.28
  7.4 0.6 multiply_reduce_fusion
  9.5 0.2 convolution_reduce_fusion
  9.8 0.3 convolution_reduce_fusion.1
  10.1 0.3 fusion.13
  10.5 0.1 compare_convert_fusion.same_ref
  10.7 0.1 concatenate.13
  10.8 0.4 convolution_bitcast_fusion.first_ref
  11.3 1.9 %copy-done.2 = bf16[2,3,320,320]{3,2,1,0:T(8,128)(2,1)S(1)} copy-done((bf16[2,3,320,320]{3,2,1,0:T(8,128)(2,1)S(1)}, bf16[2,3,320,320]{3,2,1,0:T(8,128)(2,1)}, u32[]{:S(2)}) %copy-start.2) | copy-done | bytes 1228824
  13.2 18.7 %shard_map.149 = f32[2,16,512]{2,1,0:T(8,128)S(1)} custom-call(f32[2,4,128,320]{3,2,1,0:T(8,128)S(1)} %convolution_bitcast_fusion.first_ref, f32[1,320]{1,0:T(1,128)S(1)} %add.99.emb_ref.pooled_ref.tproj_ref, f32[1,320]{1,0:T(1,128)S(1)} %get-tuple-element.17.time_ref.emb_ref, f32[1,320]{1,0:T(1,128)S(1)} %add.99.emb_ref.pooled_ref.tproj_ref, ...), custom_call_target="tpu_custom_call" | custom-call | flops 3774873600 | bytes 6225920 | tf_op jit(solution)/shard_map/pallas_call | solution.py:215
  32.0 2.6 %collective-permute-start.1 = (f32[1024]{0:T(1024)S(1)}, f32[1024]{0:T(1024)S(1)}, u32[]{:S(2)}, u32[]{:S(2)}) collective-permute-start(f32[1024]{0:T(1024)S(1)} %add.100), channel_id=1, source_target_pairs={{0,2},{1,3},{2,0},{3,1},{4,6},{5,7},{6,4},{7,5},{8,10},{9,11},{10,... | collective-permute-start | bytes 12296 | tf_op jit(solution)/shard_map/ppermute | solution.py:240
  34.6 1.6 %collective-permute-done.1 = f32[1024]{0:T(1024)S(1)} collective-permute-done((f32[1024]{0:T(1024)S(1)}, f32[1024]{0:T(1024)S(1)}, u32[]{:S(2)}, u32[]{:S(2)}) %collective-permute-start.1) | collective-permute-done | bytes 4128 | tf_op jit(solution)/shard_map/ppermute | solution.py:240
  36.1 2.1 %collective-permute-start.2 = (f32[1024]{0:T(1024)S(1)}, f32[1024]{0:T(1024)S(1)}, u32[]{:S(2)}, u32[]{:S(2)}) collective-permute-start(f32[1024]{0:T(1024)S(1)} %add.101), channel_id=1, source_target_pairs={{0,4},{1,5},{2,6},{3,7},{4,0},{5,1},{6,2},{7,3},{8,12},{9,13},{10,... | collective-permute-start | bytes 12296 | tf_op jit(solution)/shard_map/ppermute | solution.py:240
  38.2 1.6 %collective-permute-done.2 = f32[1024]{0:T(1024)S(1)} collective-permute-done((f32[1024]{0:T(1024)S(1)}, f32[1024]{0:T(1024)S(1)}, u32[]{:S(2)}, u32[]{:S(2)}) %collective-permute-start.2) | collective-permute-done | bytes 4128 | tf_op jit(solution)/shard_map/ppermute | solution.py:240
  39.8 3.0 %collective-permute-start.3 = (f32[1024]{0:T(1024)S(1)}, f32[1024]{0:T(1024)S(1)}, u32[]{:S(2)}, u32[]{:S(2)}) collective-permute-start(f32[1024]{0:T(1024)S(1)} %add.102), channel_id=1, source_target_pairs={{0,8},{1,9},{2,10},{3,11},{4,12},{5,13},{6,14},{7,15},{8,0},{9,1},... | collective-permute-start | bytes 12296 | tf_op jit(solution)/shard_map/ppermute | solution.py:240
  42.8 0.4 copy.23.tproj_ref
  43.7 0.7 collective-permute-done.3
  44.4 1.4 %copy-done.3 = bf16[2,3,320,320]{3,2,1,0:T(8,128)(2,1)S(1)} copy-done((bf16[2,3,320,320]{3,2,1,0:T(8,128)(2,1)S(1)}, bf16[2,3,320,320]{3,2,1,0:T(8,128)(2,1)}, u32[]{:S(2)}) %copy-start.3) | copy-done | bytes 1228824
  45.8 20.3 %shard_map.150 = f32[2,16,512]{2,1,0:T(8,128)S(1)} custom-call(f32[2,4,128,320]{3,2,1,0:T(8,128)} %copy-done.1, f32[1,320]{1,0:T(1,128)S(1)} %get-tuple-element.17.time_ref.emb_ref, f32[1,320]{1,0:T(1,128)S(1)} %get-tuple-element.17.time_ref.emb_ref, f32[1,1024]{1,0:T(1,128)S(1)} %bitcast.49, bf16[1024,320]{1,0:T(8,128)(2,1)S(1)} %copy.23.tproj_ref, ...), custom_call_target="tpu_custom_call" | custom-call | flops 3774873600 | bytes 6225920 | tf_op jit(solution)/shard_map/pallas_call | solution.py:215
  66.3 1.2 %collective-permute-done.4 = f32[4,4,2,128]{3,2,1,0:T(2,128)S(1)} collective-permute-done((f32[4,4,2,128]{3,2,1,0:T(2,128)S(1)}, f32[4,4,2,128]{3,2,1,0:T(2,128)S(1)}, u32[]{:S(2)}, u32[]{:S(2)}) %collective-permute-start.4) | collective-permute-done | bytes 16416 | tf_op jit(solution)/shard_map/ppermute | solution.py:257
  67.5 1.9 %collective-permute-start.5 = (f32[4,4,2,128]{3,2,1,0:T(2,128)S(1)}, f32[4,4,2,128]{3,2,1,0:T(2,128)S(1)}, u32[]{:S(2)}, u32[]{:S(2)}) collective-permute-start(f32[4,4,2,128]{3,2,1,0:T(2,128)S(1)} %add.107), channel_id=1, source_target_pairs={{0,2},{1,3},{2,0},{3,1},{4,6},{5,7},{6,4},{7,5},{8,10},{9,11},{10,... | collective-permute-start | bytes 49160 | tf_op jit(solution)/shard_map/ppermute | solution.py:257
  69.4 1.9 %collective-permute-done.5 = f32[4,4,2,128]{3,2,1,0:T(2,128)S(1)} collective-permute-done((f32[4,4,2,128]{3,2,1,0:T(2,128)S(1)}, f32[4,4,2,128]{3,2,1,0:T(2,128)S(1)}, u32[]{:S(2)}, u32[]{:S(2)}) %collective-permute-start.5) | collective-permute-done | bytes 16416 | tf_op jit(solution)/shard_map/ppermute | solution.py:257
  71.3 2.0 %collective-permute-start.6 = (f32[4,4,2,128]{3,2,1,0:T(2,128)S(1)}, f32[4,4,2,128]{3,2,1,0:T(2,128)S(1)}, u32[]{:S(2)}, u32[]{:S(2)}) collective-permute-start(f32[4,4,2,128]{3,2,1,0:T(2,128)S(1)} %add.109), channel_id=1, source_target_pairs={{0,4},{1,5},{2,6},{3,7},{4,0},{5,1},{6,2},{7,3},{8,12},{9,13},{10,... | collective-permute-start | bytes 49160 | tf_op jit(solution)/shard_map/ppermute | solution.py:257
  73.3 1.8 %collective-permute-done.6 = f32[4,4,2,128]{3,2,1,0:T(2,128)S(1)} collective-permute-done((f32[4,4,2,128]{3,2,1,0:T(2,128)S(1)}, f32[4,4,2,128]{3,2,1,0:T(2,128)S(1)}, u32[]{:S(2)}, u32[]{:S(2)}) %collective-permute-start.6) | collective-permute-done | bytes 16416 | tf_op jit(solution)/shard_map/ppermute | solution.py:257
  75.1 3.0 %collective-permute-start.7 = (f32[4,4,2,128]{3,2,1,0:T(2,128)S(1)}, f32[4,4,2,128]{3,2,1,0:T(2,128)S(1)}, u32[]{:S(2)}, u32[]{:S(2)}) collective-permute-start(f32[4,4,2,128]{3,2,1,0:T(2,128)S(1)} %add.111), channel_id=1, source_target_pairs={{0,8},{1,9},{2,10},{3,11},{4,12},{5,13},{6,14},{7,15},{8,0},{9,1},... | collective-permute-start | bytes 49160 | tf_op jit(solution)/shard_map/ppermute | solution.py:257
  78.1 1.7 %collective-permute-done.7 = f32[4,4,2,128]{3,2,1,0:T(2,128)S(1)} collective-permute-done((f32[4,4,2,128]{3,2,1,0:T(2,128)S(1)}, f32[4,4,2,128]{3,2,1,0:T(2,128)S(1)}, u32[]{:S(2)}, u32[]{:S(2)}) %collective-permute-start.7) | collective-permute-done | bytes 16416 | tf_op jit(solution)/shard_map/ppermute | solution.py:257
  79.8 0.6 add_add_fusion
  (55 shorter events, 0.6 us)
Async XLA Ops:
  0.6 8.8 %copy-start = (bf16[320,1280]{1,0:T(8,128)(2,1)S(1)}, bf16[320,1280]{1,0:T(8,128)(2,1)}, u32[]{:S(2)}) copy-start(bf16[320,1280]{1,0:T(8,128)(2,1)} %param.21) | copy-start | bytes 2457604
  0.6 5.3 %copy-start.8 = (bf16[9,320,4]{1,2,0:T(4,128)(2,1)S(1)}, bf16[9,320,4]{1,2,0:T(4,128)(2,1)}, u32[]{:S(2)}) copy-start(bf16[9,320,4]{1,2,0:T(4,128)(2,1)} %param.24) | copy-start | bytes 69124
  0.7 5.3 %copy-start.6 = (f32[1,4,4,2,128]{4,3,2,1,0:T(2,128)S(1)}, f32[1,4,4,2,128]{4,3,2,1,0:T(2,128)}, u32[]{:S(2)}) copy-start(f32[1,4,4,2,128]{4,3,2,1,0:T(2,128)} %param.17) | copy-start | bytes 49156
  0.7 5.4 %copy-start.7 = (f32[1024]{0:T(1024)S(1)}, f32[1024]{0:T(1024)}, u32[]{:S(2)}) copy-start(f32[1024]{0:T(1024)} %param.20) | copy-start | bytes 12292
  0.7 9.1 %copy-start.4 = (bf16[1024,320]{0,1:T(8,128)(2,1)S(1)}, bf16[1024,320]{0,1:T(8,128)(2,1)}, u32[]{:S(2)}) copy-start(bf16[1024,320]{0,1:T(8,128)(2,1)} %param.23) | copy-start | bytes 1966084
  0.7 9.4 %copy-start.5 = (bf16[1280,320]{0,1:T(8,128)(2,1)S(1)}, bf16[1280,320]{0,1:T(8,128)(2,1)}, u32[]{:S(2)}) copy-start(bf16[1280,320]{0,1:T(8,128)(2,1)} %param.22) | copy-start | bytes 2457604
  0.7 10.5 %copy-start.9 = (bf16[9,4,320]{2,1,0:T(4,128)(2,1)S(1)}, bf16[9,4,320]{2,1,0:T(4,128)(2,1)}, u32[]{:S(2)}) copy-start(bf16[9,4,320]{2,1,0:T(4,128)(2,1)} %param.27) | copy-start | bytes 69124
  5.5 26.5 %collective-permute-start = (f32[1024]{0:T(1024)S(1)}, f32[1024]{0:T(1024)S(1)}, u32[]{:S(2)}, u32[]{:S(2)}) collective-permute-start(f32[1024]{0:T(1024)S(1)} %bitcast.53), channel_id=1, source_target_pairs={{0,1},{1,0},{2,3},{3,2},{4,5},{5,4},{6,7},{7,6},{8,9},{9,8},{10,11... | collective-permute-start | bytes 12296 | tf_op jit(solution)/shard_map/ppermute | solution.py:240
  11.2 20.7 %copy-start.1 = (f32[2,4,128,320]{3,2,1,0:T(8,128)}, f32[2,4,128,320]{3,2,1,0:T(8,128)S(1)}, u32[]{:S(2)}) copy-start(f32[2,4,128,320]{3,2,1,0:T(8,128)S(1)} %convolution_bitcast_fusion.first_ref) | copy-start | bytes 3932164
  11.2 1.9 %copy-start.2 = (bf16[2,3,320,320]{3,2,1,0:T(8,128)(2,1)S(1)}, bf16[2,3,320,320]{3,2,1,0:T(8,128)(2,1)}, u32[]{:S(2)}) copy-start(bf16[2,3,320,320]{3,2,1,0:T(8,128)(2,1)} %wt_hbm.3) | copy-start | bytes 3686404
  32.0 4.2 %collective-permute-start.1 = (f32[1024]{0:T(1024)S(1)}, f32[1024]{0:T(1024)S(1)}, u32[]{:S(2)}, u32[]{:S(2)}) collective-permute-start(f32[1024]{0:T(1024)S(1)} %add.100), channel_id=1, source_target_pairs={{0,2},{1,3},{2,0},{3,1},{4,6},{5,7},{6,4},{7,5},{8,10},{9,11},{10,... | collective-permute-start | bytes 12296 | tf_op jit(solution)/shard_map/ppermute | solution.py:240
  36.1 3.7 %collective-permute-start.2 = (f32[1024]{0:T(1024)S(1)}, f32[1024]{0:T(1024)S(1)}, u32[]{:S(2)}, u32[]{:S(2)}) collective-permute-start(f32[1024]{0:T(1024)S(1)} %add.101), channel_id=1, source_target_pairs={{0,4},{1,5},{2,6},{3,7},{4,0},{5,1},{6,2},{7,3},{8,12},{9,13},{10,... | collective-permute-start | bytes 12296 | tf_op jit(solution)/shard_map/ppermute | solution.py:240
  39.8 4.6 %collective-permute-start.3 = (f32[1024]{0:T(1024)S(1)}, f32[1024]{0:T(1024)S(1)}, u32[]{:S(2)}, u32[]{:S(2)}) collective-permute-start(f32[1024]{0:T(1024)S(1)} %add.102), channel_id=1, source_target_pairs={{0,8},{1,9},{2,10},{3,11},{4,12},{5,13},{6,14},{7,15},{8,0},{9,1},... | collective-permute-start | bytes 12296 | tf_op jit(solution)/shard_map/ppermute | solution.py:240
  44.4 1.4 %copy-start.3 = (bf16[2,3,320,320]{3,2,1,0:T(8,128)(2,1)S(1)}, bf16[2,3,320,320]{3,2,1,0:T(8,128)(2,1)}, u32[]{:S(2)}) copy-start(bf16[2,3,320,320]{3,2,1,0:T(8,128)(2,1)} %wt_hbm.3) | copy-start | bytes 3686404
  45.8 20.4 %copy-start.10 = (f32[1,4,4,2,128]{4,3,2,1,0:T(2,128)S(1)}, f32[1,4,4,2,128]{4,3,2,1,0:T(2,128)}, u32[]{:S(2)}) copy-start(f32[1,4,4,2,128]{4,3,2,1,0:T(2,128)} %param.18) | copy-start | bytes 49156
  45.8 34.0 %copy-start.11 = (f32[4,4,2,128]{3,2,1,0:T(2,128)S(1)}, f32[4,4,2,128]{3,2,1,0:T(2,128)}, u32[]{:S(2)}) copy-start(f32[4,4,2,128]{3,2,1,0:T(2,128)} %param.16) | copy-start | bytes 49156
  66.2 1.2 %collective-permute-start.4 = (f32[4,4,2,128]{3,2,1,0:T(2,128)S(1)}, f32[4,4,2,128]{3,2,1,0:T(2,128)S(1)}, u32[]{:S(2)}, u32[]{:S(2)}) collective-permute-start(f32[4,4,2,128]{3,2,1,0:T(2,128)S(1)} %fusion.7), channel_id=1, source_target_pairs={{0,1},{1,0},{2,3},{3,2},{4,5},{5,4},{6,7},{7,6},{8,9},{9,8},{10,11... | collective-permute-start | bytes 49160 | tf_op jit(solution)/shard_map/ppermute | solution.py:257
  67.5 3.8 %collective-permute-start.5 = (f32[4,4,2,128]{3,2,1,0:T(2,128)S(1)}, f32[4,4,2,128]{3,2,1,0:T(2,128)S(1)}, u32[]{:S(2)}, u32[]{:S(2)}) collective-permute-start(f32[4,4,2,128]{3,2,1,0:T(2,128)S(1)} %add.107), channel_id=1, source_target_pairs={{0,2},{1,3},{2,0},{3,1},{4,6},{5,7},{6,4},{7,5},{8,10},{9,11},{10,... | collective-permute-start | bytes 49160 | tf_op jit(solution)/shard_map/ppermute | solution.py:257
  71.3 3.8 %collective-permute-start.6 = (f32[4,4,2,128]{3,2,1,0:T(2,128)S(1)}, f32[4,4,2,128]{3,2,1,0:T(2,128)S(1)}, u32[]{:S(2)}, u32[]{:S(2)}) collective-permute-start(f32[4,4,2,128]{3,2,1,0:T(2,128)S(1)} %add.109), channel_id=1, source_target_pairs={{0,4},{1,5},{2,6},{3,7},{4,0},{5,1},{6,2},{7,3},{8,12},{9,13},{10,... | collective-permute-start | bytes 49160 | tf_op jit(solution)/shard_map/ppermute | solution.py:257
  75.1 4.7 %collective-permute-start.7 = (f32[4,4,2,128]{3,2,1,0:T(2,128)S(1)}, f32[4,4,2,128]{3,2,1,0:T(2,128)S(1)}, u32[]{:S(2)}, u32[]{:S(2)}) collective-permute-start(f32[4,4,2,128]{3,2,1,0:T(2,128)S(1)} %add.111), channel_id=1, source_target_pairs={{0,8},{1,9},{2,10},{3,11},{4,12},{5,13},{6,14},{7,15},{8,0},{9,1},... | collective-permute-start | bytes 49160 | tf_op jit(solution)/shard_map/ppermute | solution.py:257

commit v6 on v4

--- a/solution.py
+++ b/solution.py
@@ -233,6 +233,52 @@
     )(first, emb_u, time_vector, pooled, text_proj, last, same, batch_mix, spatial_weights, temporal_weights)[:, :outs]
 
 
+def gather_body(starts_ref, pick_ref, table_hbm, out_ref, buf, sems):
+    count = starts_ref.shape[0]
+    span = buf.shape[1]
+
+    def start(t, carry):
+        first = pl.multiple_of(starts_ref[t], span)
+        pltpu.make_async_copy(table_hbm.at[pl.ds(first, span)], buf.at[t], sems.at[t]).start()
+        return carry
+
+    def finish(t, carry):
+        pltpu.make_async_copy(table_hbm.at[pl.ds(0, span)], buf.at[t], sems.at[t]).wait()
+        return carry
+
+    lax.fori_loop(0, count, start, 0)
+    lax.fori_loop(0, count, finish, 0)
+    rows = jnp.where(pick_ref[...] > 0.0, buf[...].astype(jnp.float32), 0.0)
+    out_ref[...] = jnp.sum(jnp.sum(rows, axis=0), axis=0, keepdims=True)
+
+
+def pool_rows(local_ids, table):
+    span = 16
+    count = local_ids.shape[0]
+    shard_rows = table.shape[0]
+    if shard_rows % span:
+        hits = local_ids[:, None] == jnp.arange(shard_rows, dtype=jnp.int32)[None, :]
+        counts = jnp.sum(hits.astype(jnp.float32), axis=0).astype(jnp.bfloat16)[None]
+        return jnp.dot(counts, table, preferred_element_type=jnp.float32)[0]
+    held = (local_ids >= 0) & (local_ids < shard_rows)
+    row = jnp.clip(local_ids, 0, shard_rows - 1)
+    starts = (row // span) * span
+    pick = (jnp.arange(span)[None, :] == (row - starts)[:, None]) & held[:, None]
+    padded = -(-count // 8) * 8
+    pick = jnp.zeros((padded, span, 1), jnp.float32).at[:count, :, 0].set(pick.astype(jnp.float32))
+    return pl.pallas_call(
+        gather_body,
+        out_shape=jax.ShapeDtypeStruct((1, table.shape[1]), jnp.float32),
+        in_specs=[
+            pl.BlockSpec(memory_space=pltpu.MemorySpace.SMEM),
+            pl.BlockSpec(memory_space=pltpu.MemorySpace.VMEM),
+            pl.BlockSpec(memory_space=pl.ANY),
+        ],
+        out_specs=pl.BlockSpec(memory_space=pltpu.MemorySpace.VMEM),
+        scratch_shapes=[pltpu.VMEM((padded, span, table.shape[1]), table.dtype), pltpu.SemaphoreType.DMA((count,))],
+    )(starts, pick, table)[0]
+
+
 def butterfly_sum(x, axis):
     peers = lax.axis_size(axis)
     if peers & (peers - 1):
@@ -279,9 +325,7 @@
     shard_rows = token_table.shape[0]
     first_row = lax.axis_index("slot") * shard_rows
     local_ids = prompt_ids - first_row
-    hits = local_ids[:, None] == jnp.arange(shard_rows, dtype=jnp.int32)[None, :]
-    counts = jnp.sum(hits.astype(jnp.float32), axis=0).astype(jnp.bfloat16)[None]
-    partial = jnp.dot(counts, token_table, preferred_element_type=jnp.float32)[0]
+    partial = pool_rows(local_ids, token_table)
     pooled = butterfly_sum(partial, "slot")[None]
     text_uncond = layer_norm(empty_text).astype(jnp.bfloat16)[None]
     vector_uncond = jnp.dot(text_uncond, text_proj, preferred_element_type=jnp.float32)

time: 74.3 us -> 80.4 us (1.082)
  Pallas kernels: 33.8 us -> 40.2 us
  matrix products: 6.2 us -> 3.6 us
  other arithmetic: 3.28 us -> 5.31 us
    pallas_call x0 -> x1, Pallas kernels: none -> 6.32 us  [pool_rows(): pl.pallas_call(gather_body, out_shape=jax.ShapeDtypeStruct((1, table.shap...]
    dot_general x1 -> x0, matrix products: 3.73 us -> none  [local(): jnp.dot(counts, token_table, preferred_element_type=jnp.float32)[0]]
    dot_general x1, matrix products: 0.34 us -> 1.49 us  [local(): time_vector = jnp.dot(hidden, time_out, preferred_element_type=jnp.float32)]
    scatter x0 -> x1, other arithmetic: none -> 0.9 us  [pool_rows(): jnp.zeros((padded, span, 1), jnp.float32).at[:count, :, 0]]
    and x0 -> x2, other arithmetic: none -> 0.89 us  [the longest x1 0.66 us: pool_rows(): held = (local_ids >= 0) & (local_ids < shard_rows)]
  transfers between devices with their start and end apart: 8 -> 8, of which waited for: 7 -> 7; matrix products, arithmetic and copies ran while one was open for 6% -> 7% of each run, Pallas kernels for 0% -> 0%
where the time goes in v6:
time: 80.4 us; the launch traced here: 80 us
  Pallas kernels  40.2 us (50%)
  starting transfers between devices  15.3 us (19%)
  waiting for transfers between devices  10.1 us (13%)
  other arithmetic  5.31 us (7%)
  matrix products  3.6 us (4%)
  between operations  3.4 us (4%)
  local copies, waits for them, and re-layouts  2.14 us (3%)
    pallas_call x1, Pallas kernels, unet(): pl.pallas_call(functools.partial(unet_body, count=float(count)), out_shap...  33.8 us
    ppermute x4, starting transfers between devices, butterfly_sum(): x = x + lax.ppermute(x, axis, [(i, i ^ k) for i in range(peers)])  8.37 us
    ppermute x4, starting transfers between devices, butterfly_scan(): got = lax.ppermute(total, axis, [(i, i ^ k) for i in range(peers)])  6.91 us
    ppermute x4, waiting for transfers between devices, butterfly_scan(): got = lax.ppermute(total, axis, [(i, i ^ k) for i in range(peers)])  6.65 us
    pallas_call x1, Pallas kernels, pool_rows(): pl.pallas_call(gather_body, out_shape=jax.ShapeDtypeStruct((1, table.shap...  6.32 us
    ppermute x4, waiting for transfers between devices, butterfly_sum(): x = x + lax.ppermute(x, axis, [(i, i ^ k) for i in range(peers)])  3.41 us
    unnamed x22, local copies, waits for them, and re-layouts  1.78 us
  transfers between devices with their start and end apart: 8, of which 7 were waited for; matrix products, arithmetic and copies ran while one was open for 7% of the time, Pallas kernels for 0%

profile of v6, /device:TPU:0, one launch (start us, length us, event | category | flops | bytes accessed | tf_op | source)
XLA Modules:
  0.0 80.0 jit_solution(14085564469839578945)
XLA Ops:
  0.6 1.3 %clamp_subtract_fusion = (s32[77]{0:T(128)S(1)}, s32[77]{0:T(128)}) fusion(s32[77]{0:T(128)} %param.17, s32[]{:T(128)S(6)} %mul.92), kind=kLoop, calls=%fused_computation.58 | loop fusion | flops 1463 | bytes 928 | tf_op jit(solution)/shard_map/sub | solution.py:266
  1.9 0.7 compare_and_fusion
  2.6 0.2 fusion
  2.8 0.9 %pad_convert_fusion.pick_ref = f32[80,16,1]{2,1,0:T(8,128)} fusion(pred[77,16,1]{2,1,0:T(8,128)(4,1)S(1)} %fusion), kind=kLoop, calls=%fused_computation.3 | loop fusion | flops 1280 | bytes 6352 | tf_op jit(solution)/shard_map/scatter | solution.py:268
  3.7 6.3 %shard_map.149 = f32[1,1024]{1,0:T(1,128)} custom-call(s32[77]{0:T(128)} %get-tuple-element.15.starts_ref, f32[80,16,1]{2,1,0:T(8,128)} %pad_convert_fusion.pick_ref, bf16[3088,1024]{1,0:T(8,128)(2,1)} %table_hbm.1), custom_call_target="tpu_custom_call" | custom-call | tf_op jit(solution)/shard_map/pallas_call | solution.py:269
  10.0 0.6 collective-permute-start
  10.7 0.1 pad_slice_fusion
  11.6 0.2 convolution_reduce_fusion
  11.9 0.6 reduce_sum.18
  13.2 0.6 multiply_reduce_fusion
  14.5 0.1 compare_convert_fusion.same_ref
  14.6 0.2 concatenate.13
  14.7 1.5 %convolution_bitcast_fusion.first_ref = f32[2,4,128,320]{3,2,1,0:T(8,128)} fusion(bf16[320,36,1,1]{0,1,2,3:T(8,128)(2,1)S(1)} %reshape.170, bf16[36,4,2,128]{3,0,2,1:T(8,128)(2,1)S(1)} %concatenate.13), kind=kOutput, calls=%fused_computation | convolution fusion | flops 23592960 | bytes 1407488 | tf_op jit(solution)/shard_map/dot_general | solution.py:73
  16.3 1.5 %fusion.16 = (f32[320]{0:T(512)S(1)}, f32[1,320]{1,0:T(1,128)S(1)}) fusion(bf16[1280,1]{0,1:T(2,128)(2,1)S(1)} %reshape.175, bf16[1280,320]{0,1:T(8,128)(2,1)} %param.24), kind=kOutput, calls=%fused_computation.60 | convolution fusion | flops 819200 | bytes 824320 | tf_op jit(solution)/shard_map/dot_general | solution.py:340
  17.8 2.6 %collective-permute-start.1 = (f32[1024]{0:T(1024)S(1)}, f32[1024]{0:T(1024)S(1)}, u32[]{:S(2)}, u32[]{:S(2)}) collective-permute-start(f32[1024]{0:T(1024)S(1)} %add.103), channel_id=1, source_target_pairs={{0,2},{1,3},{2,0},{3,1},{4,6},{5,7},{6,4},{7,5},{8,10},{9,11},{10,... | collective-permute-start | bytes 12296 | tf_op jit(solution)/shard_map/ppermute | solution.py:288
  20.4 1.6 %collective-permute-done.1 = f32[1024]{0:T(1024)S(1)} collective-permute-done((f32[1024]{0:T(1024)S(1)}, f32[1024]{0:T(1024)S(1)}, u32[]{:S(2)}, u32[]{:S(2)}) %collective-permute-start.1) | collective-permute-done | bytes 4128 | tf_op jit(solution)/shard_map/ppermute | solution.py:288
  22.0 2.1 %collective-permute-start.2 = (f32[1024]{0:T(1024)S(1)}, f32[1024]{0:T(1024)S(1)}, u32[]{:S(2)}, u32[]{:S(2)}) collective-permute-start(f32[1024]{0:T(1024)S(1)} %add.104), channel_id=1, source_target_pairs={{0,4},{1,5},{2,6},{3,7},{4,0},{5,1},{6,2},{7,3},{8,12},{9,13},{10,... | collective-permute-start | bytes 12296 | tf_op jit(solution)/shard_map/ppermute | solution.py:288
  24.2 1.5 %collective-permute-done.2 = f32[1024]{0:T(1024)S(1)} collective-permute-done((f32[1024]{0:T(1024)S(1)}, f32[1024]{0:T(1024)S(1)}, u32[]{:S(2)}, u32[]{:S(2)}) %collective-permute-start.2) | collective-permute-done | bytes 4128 | tf_op jit(solution)/shard_map/ppermute | solution.py:288
  25.7 3.0 %collective-permute-start.3 = (f32[1024]{0:T(1024)S(1)}, f32[1024]{0:T(1024)S(1)}, u32[]{:S(2)}, u32[]{:S(2)}) collective-permute-start(f32[1024]{0:T(1024)S(1)} %add.105), channel_id=1, source_target_pairs={{0,8},{1,9},{2,10},{3,11},{4,12},{5,13},{6,14},{7,15},{8,0},{9,1},... | collective-permute-start | bytes 12296 | tf_op jit(solution)/shard_map/ppermute | solution.py:288
  28.8 0.3 convolution_reduce_fusion.1
  29.1 0.4 copy.18.tproj_ref
  30.0 0.3 collective-permute-done.3
  30.3 1.4 %copy-done.1 = bf16[2,3,320,320]{3,2,1,0:T(8,128)(2,1)S(1)} copy-done((bf16[2,3,320,320]{3,2,1,0:T(8,128)(2,1)S(1)}, bf16[2,3,320,320]{3,2,1,0:T(8,128)(2,1)}, u32[]{:S(2)}) %copy-start.1) | copy-done | bytes 1228824
  31.7 33.8 %shard_map.150 = f32[2,16,1024]{2,1,0:T(8,128)S(1)} custom-call(f32[2,4,128,320]{3,2,1,0:T(8,128)} %convolution_bitcast_fusion.first_ref, f32[1,320]{1,0:T(1,128)S(1)} %add.102.emb_u_ref, f32[1,320]{1,0:T(1,128)S(1)} %get-tuple-element.27.time_ref, f32[1,1024]{1,0:T(1,128)S(1)} %bitcast.47, bf16[1024,320]{1,0:T(8,128)(2,1)S(1)} %copy.18.tproj_ref, ...), custom_call_target="tpu_custom_call" | custom-call | flops 7549747200 | bytes 6225920 | tf_op jit(solution)/shard_map/pallas_call | solution.py:217
  65.8 1.2 %collective-permute-done.4 = f32[4,4,2,128]{3,2,1,0:T(2,128)S(1)} collective-permute-done((f32[4,4,2,128]{3,2,1,0:T(2,128)S(1)}, f32[4,4,2,128]{3,2,1,0:T(2,128)S(1)}, u32[]{:S(2)}, u32[]{:S(2)}) %collective-permute-start.4) | collective-permute-done | bytes 16416 | tf_op jit(solution)/shard_map/ppermute | solution.py:302
  67.0 1.9 %collective-permute-start.5 = (f32[4,4,2,128]{3,2,1,0:T(2,128)S(1)}, f32[4,4,2,128]{3,2,1,0:T(2,128)S(1)}, u32[]{:S(2)}, u32[]{:S(2)}) collective-permute-start(f32[4,4,2,128]{3,2,1,0:T(2,128)S(1)} %add.110), channel_id=1, source_target_pairs={{0,2},{1,3},{2,0},{3,1},{4,6},{5,7},{6,4},{7,5},{8,10},{9,11},{10,... | collective-permute-start | bytes 49160 | tf_op jit(solution)/shard_map/ppermute | solution.py:302
  68.8 1.9 %collective-permute-done.5 = f32[4,4,2,128]{3,2,1,0:T(2,128)S(1)} collective-permute-done((f32[4,4,2,128]{3,2,1,0:T(2,128)S(1)}, f32[4,4,2,128]{3,2,1,0:T(2,128)S(1)}, u32[]{:S(2)}, u32[]{:S(2)}) %collective-permute-start.5) | collective-permute-done | bytes 16416 | tf_op jit(solution)/shard_map/ppermute | solution.py:302
  70.8 2.0 %collective-permute-start.6 = (f32[4,4,2,128]{3,2,1,0:T(2,128)S(1)}, f32[4,4,2,128]{3,2,1,0:T(2,128)S(1)}, u32[]{:S(2)}, u32[]{:S(2)}) collective-permute-start(f32[4,4,2,128]{3,2,1,0:T(2,128)S(1)} %add.112), channel_id=1, source_target_pairs={{0,4},{1,5},{2,6},{3,7},{4,0},{5,1},{6,2},{7,3},{8,12},{9,13},{10,... | collective-permute-start | bytes 49160 | tf_op jit(solution)/shard_map/ppermute | solution.py:302
  72.8 1.8 %collective-permute-done.6 = f32[4,4,2,128]{3,2,1,0:T(2,128)S(1)} collective-permute-done((f32[4,4,2,128]{3,2,1,0:T(2,128)S(1)}, f32[4,4,2,128]{3,2,1,0:T(2,128)S(1)}, u32[]{:S(2)}, u32[]{:S(2)}) %collective-permute-start.6) | collective-permute-done | bytes 16416 | tf_op jit(solution)/shard_map/ppermute | solution.py:302
  74.6 3.0 %collective-permute-start.7 = (f32[4,4,2,128]{3,2,1,0:T(2,128)S(1)}, f32[4,4,2,128]{3,2,1,0:T(2,128)S(1)}, u32[]{:S(2)}, u32[]{:S(2)}) collective-permute-start(f32[4,4,2,128]{3,2,1,0:T(2,128)S(1)} %add.114), channel_id=1, source_target_pairs={{0,8},{1,9},{2,10},{3,11},{4,12},{5,13},{6,14},{7,15},{8,0},{9,1},... | collective-permute-start | bytes 49160 | tf_op jit(solution)/shard_map/ppermute | solution.py:302
  77.6 1.7 %collective-permute-done.7 = f32[4,4,2,128]{3,2,1,0:T(2,128)S(1)} collective-permute-done((f32[4,4,2,128]{3,2,1,0:T(2,128)S(1)}, f32[4,4,2,128]{3,2,1,0:T(2,128)S(1)}, u32[]{:S(2)}, u32[]{:S(2)}) %collective-permute-start.7) | collective-permute-done | bytes 16416 | tf_op jit(solution)/shard_map/ppermute | solution.py:302
  79.3 0.6 add_add_fusion
  (47 shorter events, 0.6 us)
Async XLA Ops:
  0.6 11.0 %copy-start = (bf16[320,1280]{1,0:T(8,128)(2,1)S(1)}, bf16[320,1280]{1,0:T(8,128)(2,1)}, u32[]{:S(2)}) copy-start(bf16[320,1280]{1,0:T(8,128)(2,1)} %param.23) | copy-start | bytes 2457604
  3.7 7.0 %copy-start.3 = (f32[1,4,4,2,128]{4,3,2,1,0:T(2,128)S(1)}, f32[1,4,4,2,128]{4,3,2,1,0:T(2,128)}, u32[]{:S(2)}) copy-start(f32[1,4,4,2,128]{4,3,2,1,0:T(2,128)} %param.19) | copy-start | bytes 49156
  3.7 7.1 %copy-start.5 = (bf16[9,320,4]{1,2,0:T(4,128)(2,1)S(1)}, bf16[9,320,4]{1,2,0:T(4,128)(2,1)}, u32[]{:S(2)}) copy-start(bf16[9,320,4]{1,2,0:T(4,128)(2,1)} %param.26) | copy-start | bytes 69124
  3.7 8.2 %copy-start.4 = (f32[1024]{0:T(1024)S(1)}, f32[1024]{0:T(1024)}, u32[]{:S(2)}) copy-start(f32[1024]{0:T(1024)} %param.22) | copy-start | bytes 12292
  10.0 7.8 %collective-permute-start = (f32[1024]{0:T(1024)}, f32[1024]{0:T(1024)S(1)}, u32[]{:S(2)}, u32[]{:S(2)}) collective-permute-start(f32[1024]{0:T(1024)} %bitcast.52), channel_id=1, source_target_pairs={{0,1},{1,0},{2,3},{3,2},{4,5},{5,4},{6,7},{7,6},{8,9},{9,8},{10,11... | collective-permute-start | bytes 12296 | tf_op jit(solution)/shard_map/ppermute | solution.py:288
  14.4 3.4 %copy-start.7 = (f32[1,1024]{1,0:T(1,128)S(1)}, f32[1,1024]{1,0:T(1,128)}, u32[]{:S(2)}) copy-start(f32[1,1024]{1,0:T(1,128)} %shard_map.149) | copy-start | bytes 12292
  14.5 14.3 %copy-start.2 = (bf16[1024,320]{0,1:T(8,128)(2,1)S(1)}, bf16[1024,320]{0,1:T(8,128)(2,1)}, u32[]{:S(2)}) copy-start(bf16[1024,320]{0,1:T(8,128)(2,1)} %param.25) | copy-start | bytes 1966084
  16.3 13.7 %copy-start.6 = (bf16[9,4,320]{2,1,0:T(4,128)(2,1)S(1)}, bf16[9,4,320]{2,1,0:T(4,128)(2,1)}, u32[]{:S(2)}) copy-start(bf16[9,4,320]{2,1,0:T(4,128)(2,1)} %param.29) | copy-start | bytes 69124
  17.8 4.2 %collective-permute-start.1 = (f32[1024]{0:T(1024)S(1)}, f32[1024]{0:T(1024)S(1)}, u32[]{:S(2)}, u32[]{:S(2)}) collective-permute-start(f32[1024]{0:T(1024)S(1)} %add.103), channel_id=1, source_target_pairs={{0,2},{1,3},{2,0},{3,1},{4,6},{5,7},{6,4},{7,5},{8,10},{9,11},{10,... | collective-permute-start | bytes 12296 | tf_op jit(solution)/shard_map/ppermute | solution.py:288
  22.0 3.7 %collective-permute-start.2 = (f32[1024]{0:T(1024)S(1)}, f32[1024]{0:T(1024)S(1)}, u32[]{:S(2)}, u32[]{:S(2)}) collective-permute-start(f32[1024]{0:T(1024)S(1)} %add.104), channel_id=1, source_target_pairs={{0,4},{1,5},{2,6},{3,7},{4,0},{5,1},{6,2},{7,3},{8,12},{9,13},{10,... | collective-permute-start | bytes 12296 | tf_op jit(solution)/shard_map/ppermute | solution.py:288
  25.7 4.6 %collective-permute-start.3 = (f32[1024]{0:T(1024)S(1)}, f32[1024]{0:T(1024)S(1)}, u32[]{:S(2)}, u32[]{:S(2)}) collective-permute-start(f32[1024]{0:T(1024)S(1)} %add.105), channel_id=1, source_target_pairs={{0,8},{1,9},{2,10},{3,11},{4,12},{5,13},{6,14},{7,15},{8,0},{9,1},... | collective-permute-start | bytes 12296 | tf_op jit(solution)/shard_map/ppermute | solution.py:288
  30.3 1.4 %copy-start.1 = (bf16[2,3,320,320]{3,2,1,0:T(8,128)(2,1)S(1)}, bf16[2,3,320,320]{3,2,1,0:T(8,128)(2,1)}, u32[]{:S(2)}) copy-start(bf16[2,3,320,320]{3,2,1,0:T(8,128)(2,1)} %wt_hbm.1) | copy-start | bytes 3686404
  31.7 33.9 %copy-start.8 = (f32[1,4,4,2,128]{4,3,2,1,0:T(2,128)S(1)}, f32[1,4,4,2,128]{4,3,2,1,0:T(2,128)}, u32[]{:S(2)}) copy-start(f32[1,4,4,2,128]{4,3,2,1,0:T(2,128)} %param.20) | copy-start | bytes 49156
  31.7 47.6 %copy-start.9 = (f32[4,4,2,128]{3,2,1,0:T(2,128)S(1)}, f32[4,4,2,128]{3,2,1,0:T(2,128)}, u32[]{:S(2)}) copy-start(f32[4,4,2,128]{3,2,1,0:T(2,128)} %param.18) | copy-start | bytes 49156
  65.7 1.2 %collective-permute-start.4 = (f32[4,4,2,128]{3,2,1,0:T(2,128)S(1)}, f32[4,4,2,128]{3,2,1,0:T(2,128)S(1)}, u32[]{:S(2)}, u32[]{:S(2)}) collective-permute-start(f32[4,4,2,128]{3,2,1,0:T(2,128)S(1)} %fusion.8), channel_id=1, source_target_pairs={{0,1},{1,0},{2,3},{3,2},{4,5},{5,4},{6,7},{7,6},{8,9},{9,8},{10,11... | collective-permute-start | bytes 49160 | tf_op jit(solution)/shard_map/ppermute | solution.py:302
  67.0 3.8 %collective-permute-start.5 = (f32[4,4,2,128]{3,2,1,0:T(2,128)S(1)}, f32[4,4,2,128]{3,2,1,0:T(2,128)S(1)}, u32[]{:S(2)}, u32[]{:S(2)}) collective-permute-start(f32[4,4,2,128]{3,2,1,0:T(2,128)S(1)} %add.110), channel_id=1, source_target_pairs={{0,2},{1,3},{2,0},{3,1},{4,6},{5,7},{6,4},{7,5},{8,10},{9,11},{10,... | collective-permute-start | bytes 49160 | tf_op jit(solution)/shard_map/ppermute | solution.py:302
  70.8 3.8 %collective-permute-start.6 = (f32[4,4,2,128]{3,2,1,0:T(2,128)S(1)}, f32[4,4,2,128]{3,2,1,0:T(2,128)S(1)}, u32[]{:S(2)}, u32[]{:S(2)}) collective-permute-start(f32[4,4,2,128]{3,2,1,0:T(2,128)S(1)} %add.112), channel_id=1, source_target_pairs={{0,4},{1,5},{2,6},{3,7},{4,0},{5,1},{6,2},{7,3},{8,12},{9,13},{10,... | collective-permute-start | bytes 49160 | tf_op jit(solution)/shard_map/ppermute | solution.py:302
  74.6 4.7 %collective-permute-start.7 = (f32[4,4,2,128]{3,2,1,0:T(2,128)S(1)}, f32[4,4,2,128]{3,2,1,0:T(2,128)S(1)}, u32[]{:S(2)}, u32[]{:S(2)}) collective-permute-start(f32[4,4,2,128]{3,2,1,0:T(2,128)S(1)} %add.114), channel_id=1, source_target_pairs={{0,8},{1,9},{2,10},{3,11},{4,12},{5,13},{6,14},{7,15},{8,0},{9,1},... | collective-permute-start | bytes 49160 | tf_op jit(solution)/shard_map/ppermute | solution.py:302

commit v7 on v4

--- a/solution.py
+++ b/solution.py
@@ -129,7 +129,7 @@
         return (v * (0.5 + 0.5 * jnp.tanh(0.5 * v))).astype(jnp.bfloat16)
 
     def mm(a, w):
-        return lax.dot_general(a, w, (((1,), (1,)), ((), ())), preferred_element_type=jnp.float32)
+        return jnp.dot(a, w, preferred_element_type=jnp.float32)
 
     col = lax.broadcasted_iota(jnp.int32, (blocks, cols, chans), 1)
 
@@ -230,7 +230,7 @@
             transcendentals=rows * blocks * cols * chans * 5,
             bytes_accessed=spatial_weights.size * 2 + temporal_weights.size * 2 + first.size * 4,
         ),
-    )(first, emb_u, time_vector, pooled, text_proj, last, same, batch_mix, spatial_weights, temporal_weights)[:, :outs]
+    )(first, emb_u, time_vector, pooled, text_proj, last, same, batch_mix, spatial_weights.swapaxes(2, 3), temporal_weights.swapaxes(2, 3))[:, :outs]
 
 
 def butterfly_sum(x, axis):

time: 74.3 us -> 83 us (1.12)
  local copies, waits for them, and re-layouts: 2.15 us -> 10.2 us
  starting transfers between devices: 15.1 us -> 11.5 us
  waiting for transfers between devices: 10 us -> 13.3 us
    unnamed x22 -> x24, local copies, waits for them, and re-layouts: 1.78 us -> 9.86 us
    ppermute x4, starting transfers between devices: 6.96 us -> 3.36 us  [butterfly_scan(): got = lax.ppermute(total, axis, [(i, i ^ k) for i in range(peers)])]
    ppermute x4, waiting for transfers between devices: 6.6 us -> 10.2 us  [butterfly_scan(): got = lax.ppermute(total, axis, [(i, i ^ k) for i in range(peers)])]
  transfers between devices with their start and end apart: 8 -> 8, of which waited for: 7 -> 6; matrix products, arithmetic and copies ran while one was open for 6% -> 17% of each run, Pallas kernels for 0% -> 0%
where the time goes in v7:
time: 83 us; the launch traced here: 82.6 us
  Pallas kernels  33.8 us (41%)
  waiting for transfers between devices  13.3 us (16%)
  starting transfers between devices  11.5 us (14%)
  local copies, waits for them, and re-layouts  10.2 us (12%)
  matrix products  6.33 us (8%)
  other arithmetic  4.01 us (5%)
  between operations  3.44 us (4%)
    pallas_call x1, Pallas kernels, unet(): pl.pallas_call(functools.partial(unet_body, count=float(count)), out_shap...  33.8 us
    ppermute x4, waiting for transfers between devices, butterfly_scan(): got = lax.ppermute(total, axis, [(i, i ^ k) for i in range(peers)])  10.2 us
    unnamed x24, local copies, waits for them, and re-layouts  9.86 us
    ppermute x4, starting transfers between devices, butterfly_sum(): x = x + lax.ppermute(x, axis, [(i, i ^ k) for i in range(peers)])  8.17 us
    dot_general x1, matrix products, local(): jnp.dot(counts, token_table, preferred_element_type=jnp.float32)[0]  3.83 us
    ppermute x4, starting transfers between devices, butterfly_scan(): got = lax.ppermute(total, axis, [(i, i ^ k) for i in range(peers)])  3.36 us
    ppermute x4, waiting for transfers between devices, butterfly_sum(): x = x + lax.ppermute(x, axis, [(i, i ^ k) for i in range(peers)])  3.1 us
  transfers between devices with their start and end apart: 8, of which 6 were waited for; matrix products, arithmetic and copies ran while one was open for 17% of the time, Pallas kernels for 0%

profile of v7, /device:TPU:0, one launch (start us, length us, event | category | flops | bytes accessed | tf_op | source)
XLA Modules:
  0.0 82.6 jit_solution(7759217310463861396)
XLA Ops:
  0.7 0.7 broadcast_subtract_fusion
  1.4 0.2 convert_reduce_fusion
  1.7 3.8 %fusion.14 = f32[1,1024]{1,0:T(1,128)S(1)} fusion(bf16[3088,1]{0,1:T(2,128)(2,1)S(1)} %reshape.106, bf16[3088,1024]{1,0:T(8,128)(2,1)} %param.19), kind=kOutput, calls=%fused_computation.53 | convolution fusion | flops 6324224 | bytes 6334496 | tf_op jit(solution)/shard_map/dot_general | solution.py:284
  5.5 0.5 collective-permute-start
  6.0 0.1 pad_slice_fusion
  6.8 0.1 pad_maximum_fusion
  6.9 0.2 convolution_reduce_fusion
  7.2 0.6 reduce_sum.27
  8.4 0.6 multiply_reduce_fusion
  9.7 0.9 %compare_convert_fusion.same_ref = f32[320,320]{1,0:T(8,128)} fusion(s32[320]{0:T(512)S(1)} %add_select_fusion.3), kind=kLoop, calls=%fused_computation.5 | loop fusion | flops 204800 | bytes 410880 | tf_op jit(solution)/shard_map/convert_element_type | solution.py:212
  10.7 0.1 concatenate.11
  10.8 1.6 %convolution_bitcast_fusion.first_ref = f32[2,4,128,320]{3,2,1,0:T(8,128)} fusion(bf16[320,36,1,1]{0,1,2,3:T(8,128)(2,1)S(1)} %reshape.99, bf16[36,4,2,128]{3,0,2,1:T(8,128)(2,1)S(1)} %concatenate.11), kind=kOutput, calls=%fused_computation | convolution fusion | flops 23592960 | bytes 1407488 | tf_op jit(solution)/shard_map/dot_general | solution.py:73
  12.4 0.3 fusion.13
  12.8 2.6 %collective-permute-start.1 = (f32[1024]{0:T(1024)S(1)}, f32[1024]{0:T(1024)S(1)}, u32[]{:S(2)}, u32[]{:S(2)}) collective-permute-start(f32[1024]{0:T(1024)S(1)} %add.100), channel_id=1, source_target_pairs={{0,2},{1,3},{2,0},{3,1},{4,6},{5,7},{6,4},{7,5},{8,10},{9,11},{10,... | collective-permute-start | bytes 12296 | tf_op jit(solution)/shard_map/ppermute | solution.py:242
  15.4 1.6 %collective-permute-done.1 = f32[1024]{0:T(1024)S(1)} collective-permute-done((f32[1024]{0:T(1024)S(1)}, f32[1024]{0:T(1024)S(1)}, u32[]{:S(2)}, u32[]{:S(2)}) %collective-permute-start.1) | collective-permute-done | bytes 4128 | tf_op jit(solution)/shard_map/ppermute | solution.py:242
  17.0 2.1 %collective-permute-start.2 = (f32[1024]{0:T(1024)S(1)}, f32[1024]{0:T(1024)S(1)}, u32[]{:S(2)}, u32[]{:S(2)}) collective-permute-start(f32[1024]{0:T(1024)S(1)} %add.101), channel_id=1, source_target_pairs={{0,4},{1,5},{2,6},{3,7},{4,0},{5,1},{6,2},{7,3},{8,12},{9,13},{10,... | collective-permute-start | bytes 12296 | tf_op jit(solution)/shard_map/ppermute | solution.py:242
  19.1 1.5 %collective-permute-done.2 = f32[1024]{0:T(1024)S(1)} collective-permute-done((f32[1024]{0:T(1024)S(1)}, f32[1024]{0:T(1024)S(1)}, u32[]{:S(2)}, u32[]{:S(2)}) %collective-permute-start.2) | collective-permute-done | bytes 4128 | tf_op jit(solution)/shard_map/ppermute | solution.py:242
  20.6 3.0 %collective-permute-start.3 = (f32[1024]{0:T(1024)S(1)}, f32[1024]{0:T(1024)S(1)}, u32[]{:S(2)}, u32[]{:S(2)}) collective-permute-start(f32[1024]{0:T(1024)S(1)} %add.102), channel_id=1, source_target_pairs={{0,8},{1,9},{2,10},{3,11},{4,12},{5,13},{6,14},{7,15},{8,0},{9,1},... | collective-permute-start | bytes 12296 | tf_op jit(solution)/shard_map/ppermute | solution.py:242
  23.7 0.3 convolution_reduce_fusion.1
  24.0 0.4 copy.26.tproj_ref
  24.6 6.5 %copy.24 = bf16[2,9,320,320]{2,3,1,0:T(8,128)(2,1)} copy(bf16[2,9,320,320]{3,2,1,0:T(8,128)(2,1)} %param.25) | data formatting | bytes 7372800 | tf_op args[11]
  31.2 1.9 %copy.25 = bf16[2,3,320,320]{2,3,1,0:T(8,128)(2,1)S(1)} copy(bf16[2,3,320,320]{3,2,1,0:T(8,128)(2,1)} %param.26) | data formatting | bytes 2457600 | tf_op args[12]
  33.4 1.0 %copy-done.1 = f32[320,320]{1,0:T(8,128)S(1)} copy-done((f32[320,320]{1,0:T(8,128)S(1)}, f32[320,320]{1,0:T(8,128)}, u32[]{:S(2)}) %copy-start.1) | copy-done | bytes 409624
  34.4 33.8 %shard_map.149 = f32[2,16,1024]{2,1,0:T(8,128)S(1)} custom-call(f32[2,4,128,320]{3,2,1,0:T(8,128)} %convolution_bitcast_fusion.first_ref, f32[1,320]{1,0:T(1,128)S(1)} %add.99.emb_u_ref, f32[1,320]{1,0:T(1,128)S(1)} %get-tuple-element.13.time_ref, f32[1,1024]{1,0:T(1,128)S(1)} %bitcast.52, bf16[1024,320]{1,0:T(8,128)(2,1)S(1)} %copy.26.tproj_ref, ...), custom_call_target="tpu_custom_call" | custom-call | flops 7549747200 | bytes 6225920 | tf_op jit(solution)/shard_map/pallas_call | solution.py:217
  68.5 1.2 %collective-permute-done.4 = f32[4,4,2,128]{3,2,1,0:T(2,128)S(1)} collective-permute-done((f32[4,4,2,128]{3,2,1,0:T(2,128)S(1)}, f32[4,4,2,128]{3,2,1,0:T(2,128)S(1)}, u32[]{:S(2)}, u32[]{:S(2)}) %collective-permute-start.4) | collective-permute-done | bytes 16416 | tf_op jit(solution)/shard_map/ppermute | solution.py:256
  69.7 1.6 %collective-permute-start.5 = (f32[4,4,2,128]{3,2,1,0:T(2,128)S(1)}, f32[4,4,2,128]{3,2,1,0:T(2,128)S(1)}, u32[]{:S(2)}, u32[]{:S(2)}) collective-permute-start(f32[4,4,2,128]{3,2,1,0:T(2,128)S(1)} %add.107), channel_id=1, source_target_pairs={{0,2},{1,3},{2,0},{3,1},{4,6},{5,7},{6,4},{7,5},{8,10},{9,11},{10,... | collective-permute-start | bytes 49160 | tf_op jit(solution)/shard_map/ppermute | solution.py:256
  71.2 2.2 %collective-permute-done.5 = f32[4,4,2,128]{3,2,1,0:T(2,128)S(1)} collective-permute-done((f32[4,4,2,128]{3,2,1,0:T(2,128)S(1)}, f32[4,4,2,128]{3,2,1,0:T(2,128)S(1)}, u32[]{:S(2)}, u32[]{:S(2)}) %collective-permute-start.5) | collective-permute-done | bytes 16416 | tf_op jit(solution)/shard_map/ppermute | solution.py:256
  73.5 1.6 %collective-permute-start.6 = (f32[4,4,2,128]{3,2,1,0:T(2,128)S(1)}, f32[4,4,2,128]{3,2,1,0:T(2,128)S(1)}, u32[]{:S(2)}, u32[]{:S(2)}) collective-permute-start(f32[4,4,2,128]{3,2,1,0:T(2,128)S(1)} %add.109), channel_id=1, source_target_pairs={{0,4},{1,5},{2,6},{3,7},{4,0},{5,1},{6,2},{7,3},{8,12},{9,13},{10,... | collective-permute-start | bytes 49160 | tf_op jit(solution)/shard_map/ppermute | solution.py:256
  75.1 2.2 %collective-permute-done.6 = f32[4,4,2,128]{3,2,1,0:T(2,128)S(1)} collective-permute-done((f32[4,4,2,128]{3,2,1,0:T(2,128)S(1)}, f32[4,4,2,128]{3,2,1,0:T(2,128)S(1)}, u32[]{:S(2)}, u32[]{:S(2)}) %collective-permute-start.6) | collective-permute-done | bytes 16416 | tf_op jit(solution)/shard_map/ppermute | solution.py:256
  77.3 0.1 collective-permute-start.7
  77.4 4.6 %collective-permute-done.7 = f32[4,4,2,128]{3,2,1,0:T(2,128)S(1)} collective-permute-done((f32[4,4,2,128]{3,2,1,0:T(2,128)S(1)}, f32[4,4,2,128]{3,2,1,0:T(2,128)S(1)}, u32[]{:S(2)}, u32[]{:S(2)}) %collective-permute-start.7) | collective-permute-done | bytes 16416 | tf_op jit(solution)/shard_map/ppermute | solution.py:256
  82.0 0.6 add_add_fusion
  (48 shorter events, 0.5 us)
Async XLA Ops:
  0.6 6.3 %copy-start = (bf16[320,1280]{1,0:T(8,128)(2,1)S(1)}, bf16[320,1280]{1,0:T(8,128)(2,1)}, u32[]{:S(2)}) copy-start(bf16[320,1280]{1,0:T(8,128)(2,1)} %param.21) | copy-start | bytes 2457604
  0.6 5.3 %copy-start.4 = (f32[1,4,4,2,128]{4,3,2,1,0:T(2,128)S(1)}, f32[1,4,4,2,128]{4,3,2,1,0:T(2,128)}, u32[]{:S(2)}) copy-start(f32[1,4,4,2,128]{4,3,2,1,0:T(2,128)} %param.17) | copy-start | bytes 49156
  0.7 5.4 %copy-start.6 = (bf16[9,320,4]{1,2,0:T(4,128)(2,1)S(1)}, bf16[9,320,4]{1,2,0:T(4,128)(2,1)}, u32[]{:S(2)}) copy-start(bf16[9,320,4]{1,2,0:T(4,128)(2,1)} %param.24) | copy-start | bytes 69124
  0.7 6.5 %copy-start.5 = (f32[1024]{0:T(1024)S(1)}, f32[1024]{0:T(1024)}, u32[]{:S(2)}) copy-start(f32[1024]{0:T(1024)} %param.20) | copy-start | bytes 12292
  1.6 10.8 %copy-start.3 = (bf16[1280,320]{0,1:T(8,128)(2,1)S(1)}, bf16[1280,320]{0,1:T(8,128)(2,1)}, u32[]{:S(2)}) copy-start(bf16[1280,320]{0,1:T(8,128)(2,1)} %param.22) | copy-start | bytes 2457604
  1.6 22.0 %copy-start.2 = (bf16[1024,320]{0,1:T(8,128)(2,1)S(1)}, bf16[1024,320]{0,1:T(8,128)(2,1)}, u32[]{:S(2)}) copy-start(bf16[1024,320]{0,1:T(8,128)(2,1)} %param.23) | copy-start | bytes 1966084
  5.5 7.3 %collective-permute-start = (f32[1024]{0:T(1024)S(1)}, f32[1024]{0:T(1024)S(1)}, u32[]{:S(2)}, u32[]{:S(2)}) collective-permute-start(f32[1024]{0:T(1024)S(1)} %bitcast.58), channel_id=1, source_target_pairs={{0,1},{1,0},{2,3},{3,2},{4,5},{5,4},{6,7},{7,6},{8,9},{9,8},{10,11... | collective-permute-start | bytes 12296 | tf_op jit(solution)/shard_map/ppermute | solution.py:242
  12.8 4.2 %collective-permute-start.1 = (f32[1024]{0:T(1024)S(1)}, f32[1024]{0:T(1024)S(1)}, u32[]{:S(2)}, u32[]{:S(2)}) collective-permute-start(f32[1024]{0:T(1024)S(1)} %add.100), channel_id=1, source_target_pairs={{0,2},{1,3},{2,0},{3,1},{4,6},{5,7},{6,4},{7,5},{8,10},{9,11},{10,... | collective-permute-start | bytes 12296 | tf_op jit(solution)/shard_map/ppermute | solution.py:242
  17.0 3.7 %collective-permute-start.2 = (f32[1024]{0:T(1024)S(1)}, f32[1024]{0:T(1024)S(1)}, u32[]{:S(2)}, u32[]{:S(2)}) collective-permute-start(f32[1024]{0:T(1024)S(1)} %add.101), channel_id=1, source_target_pairs={{0,4},{1,5},{2,6},{3,7},{4,0},{5,1},{6,2},{7,3},{8,12},{9,13},{10,... | collective-permute-start | bytes 12296 | tf_op jit(solution)/shard_map/ppermute | solution.py:242
  20.6 12.8 %collective-permute-start.3 = (f32[1024]{0:T(1024)S(1)}, f32[1024]{0:T(1024)S(1)}, u32[]{:S(2)}, u32[]{:S(2)}) collective-permute-start(f32[1024]{0:T(1024)S(1)} %add.102), channel_id=1, source_target_pairs={{0,8},{1,9},{2,10},{3,11},{4,12},{5,13},{6,14},{7,15},{8,0},{9,1},... | collective-permute-start | bytes 12296 | tf_op jit(solution)/shard_map/ppermute | solution.py:242
  24.6 8.7 %copy-start.7 = (bf16[9,4,320]{2,1,0:T(4,128)(2,1)S(1)}, bf16[9,4,320]{2,1,0:T(4,128)(2,1)}, u32[]{:S(2)}) copy-start(bf16[9,4,320]{2,1,0:T(4,128)(2,1)} %param.27) | copy-start | bytes 69124
  33.4 1.0 %copy-start.1 = (f32[320,320]{1,0:T(8,128)S(1)}, f32[320,320]{1,0:T(8,128)}, u32[]{:S(2)}) copy-start(f32[320,320]{1,0:T(8,128)} %compare_convert_fusion.same_ref) | copy-start | bytes 1228804
  34.4 33.9 %copy-start.8 = (f32[1,4,4,2,128]{4,3,2,1,0:T(2,128)S(1)}, f32[1,4,4,2,128]{4,3,2,1,0:T(2,128)}, u32[]{:S(2)}) copy-start(f32[1,4,4,2,128]{4,3,2,1,0:T(2,128)} %param.18) | copy-start | bytes 49156
  34.4 47.6 %copy-start.9 = (f32[4,4,2,128]{3,2,1,0:T(2,128)S(1)}, f32[4,4,2,128]{3,2,1,0:T(2,128)}, u32[]{:S(2)}) copy-start(f32[4,4,2,128]{3,2,1,0:T(2,128)} %param.16) | copy-start | bytes 49156
  68.4 1.2 %collective-permute-start.4 = (f32[4,4,2,128]{3,2,1,0:T(2,128)S(1)}, f32[4,4,2,128]{3,2,1,0:T(2,128)S(1)}, u32[]{:S(2)}, u32[]{:S(2)}) collective-permute-start(f32[4,4,2,128]{3,2,1,0:T(2,128)S(1)} %fusion.7), channel_id=1, source_target_pairs={{0,1},{1,0},{2,3},{3,2},{4,5},{5,4},{6,7},{7,6},{8,9},{9,8},{10,11... | collective-permute-start | bytes 49160 | tf_op jit(solution)/shard_map/ppermute | solution.py:256
  69.7 3.8 %collective-permute-start.5 = (f32[4,4,2,128]{3,2,1,0:T(2,128)S(1)}, f32[4,4,2,128]{3,2,1,0:T(2,128)S(1)}, u32[]{:S(2)}, u32[]{:S(2)}) collective-permute-start(f32[4,4,2,128]{3,2,1,0:T(2,128)S(1)} %add.107), channel_id=1, source_target_pairs={{0,2},{1,3},{2,0},{3,1},{4,6},{5,7},{6,4},{7,5},{8,10},{9,11},{10,... | collective-permute-start | bytes 49160 | tf_op jit(solution)/shard_map/ppermute | solution.py:256
  73.5 3.8 %collective-permute-start.6 = (f32[4,4,2,128]{3,2,1,0:T(2,128)S(1)}, f32[4,4,2,128]{3,2,1,0:T(2,128)S(1)}, u32[]{:S(2)}, u32[]{:S(2)}) collective-permute-start(f32[4,4,2,128]{3,2,1,0:T(2,128)S(1)} %add.109), channel_id=1, source_target_pairs={{0,4},{1,5},{2,6},{3,7},{4,0},{5,1},{6,2},{7,3},{8,12},{9,13},{10,... | collective-permute-start | bytes 49160 | tf_op jit(solution)/shard_map/ppermute | solution.py:256
  77.3 4.7 %collective-permute-start.7 = (f32[4,4,2,128]{3,2,1,0:T(2,128)S(1)}, f32[4,4,2,128]{3,2,1,0:T(2,128)S(1)}, u32[]{:S(2)}, u32[]{:S(2)}) collective-permute-start(f32[4,4,2,128]{3,2,1,0:T(2,128)S(1)} %add.111), channel_id=1, source_target_pairs={{0,8},{1,9},{2,10},{3,11},{4,12},{5,13},{6,14},{7,15},{8,0},{9,1},... | collective-permute-start | bytes 49160 | tf_op jit(solution)/shard_map/ppermute | solution.py:256

commit v8 on v4

--- a/solution.py
+++ b/solution.py
@@ -280,8 +280,8 @@
     first_row = lax.axis_index("slot") * shard_rows
     local_ids = prompt_ids - first_row
     hits = local_ids[:, None] == jnp.arange(shard_rows, dtype=jnp.int32)[None, :]
-    counts = jnp.sum(hits.astype(jnp.float32), axis=0).astype(jnp.bfloat16)[None]
-    partial = jnp.dot(counts, token_table, preferred_element_type=jnp.float32)[0]
+    counts = jnp.sum(hits.astype(jnp.float32), axis=0)
+    partial = jnp.sum(token_table.astype(jnp.float32) * counts[:, None], axis=0)
     pooled = butterfly_sum(partial, "slot")[None]
     text_uncond = layer_norm(empty_text).astype(jnp.bfloat16)[None]
     vector_uncond = jnp.dot(text_uncond, text_proj, preferred_element_type=jnp.float32)

time: 74.3 us -> 74.7 us (level)
  other arithmetic: 3.28 us -> 7.36 us
  matrix products: 6.2 us -> 2.46 us
    reduce_sum x1 -> x2, other arithmetic: 0.21 us -> 4.29 us  [the longest x1 4.1 us: local(): partial = jnp.sum(token_table.astype(jnp.float32) * counts[:, None], axis=0)]
    dot_general x1 -> x0, matrix products: 3.73 us -> none  [local(): jnp.dot(counts, token_table, preferred_element_type=jnp.float32)[0]]
where the time goes in v8:
time: 74.7 us; the launch traced here: 74.4 us
  Pallas kernels  33.8 us (45%)
  starting transfers between devices  15.2 us (20%)
  waiting for transfers between devices  10 us (13%)
  other arithmetic  7.36 us (10%)
  between operations  3.42 us (5%)
  matrix products  2.46 us (3%)
  local copies, waits for them, and re-layouts  2.14 us (3%)
    pallas_call x1, Pallas kernels, unet(): pl.pallas_call(functools.partial(unet_body, count=float(count)), out_shap...  33.8 us
    ppermute x4, starting transfers between devices, butterfly_sum(): x = x + lax.ppermute(x, axis, [(i, i ^ k) for i in range(peers)])  8.24 us
    ppermute x4, starting transfers between devices, butterfly_scan(): got = lax.ppermute(total, axis, [(i, i ^ k) for i in range(peers)])  6.95 us
    ppermute x4, waiting for transfers between devices, butterfly_scan(): got = lax.ppermute(total, axis, [(i, i ^ k) for i in range(peers)])  6.61 us
    reduce_sum x1, other arithmetic, local(): partial = jnp.sum(token_table.astype(jnp.float32) * counts[:, None], axis=0)  4.1 us
    ppermute x4, waiting for transfers between devices, butterfly_sum(): x = x + lax.ppermute(x, axis, [(i, i ^ k) for i in range(peers)])  3.41 us
    unnamed x22, local copies, waits for them, and re-layouts  1.78 us
    dot_general x1, matrix products, conv_lifted(): lax.dot_general(windows, stacked, (((0,), (1,)), ((), ())), preferred_ele...  1.56 us
  transfers between devices with their start and end apart: 8, of which 7 were waited for; matrix products, arithmetic and copies ran while one was open for 6% of the time, Pallas kernels for 0%

profile of v8, /device:TPU:0, one launch (start us, length us, event | category | flops | bytes accessed | tf_op | source)
XLA Modules:
  0.0 74.4 jit_solution(16027735265396281579)
XLA Ops:
  0.7 0.8 %broadcast_subtract_fusion = s32[77]{0:T(128)S(1)} fusion(s32[77]{0:T(128)} %param.15, s32[]{:T(128)S(6)} %mul.96), kind=kLoop, calls=%fused_computation.52 | loop fusion | flops 77 | bytes 620 | tf_op jit(solution)/shard_map/sub | solution.py:281
  1.5 0.2 convert_reduce_fusion
  1.7 4.1 %multiply_reduce_fusion = f32[1024]{0:T(1024)S(1)} fusion(bf16[3088,1024]{1,0:T(8,128)(2,1)} %param.19, f32[3088]{0:T(1024)S(1)} %convert_reduce_fusion), kind=kLoop, calls=%fused_computation | loop fusion | flops 9485312 | bytes 6340672 | tf_op jit(solution)/shard_map/reduce_sum | solution.py:284
  5.8 0.5 collective-permute-start
  6.4 0.1 pad_slice_fusion
  7.2 0.1 pad_maximum_fusion
  7.3 0.2 convolution_reduce_fusion
  7.6 0.6 reduce_sum.36
  8.8 0.6 multiply_reduce_fusion.1
  10.1 0.1 compare_convert_fusion.same_ref
  10.2 0.2 concatenate.11
  10.4 1.6 %convolution_bitcast_fusion.first_ref = f32[2,4,128,320]{3,2,1,0:T(8,128)} fusion(bf16[320,36,1,1]{0,1,2,3:T(8,128)(2,1)S(1)} %reshape.95, bf16[36,4,2,128]{3,0,2,1:T(8,128)(2,1)S(1)} %concatenate.11), kind=kOutput, calls=%fused_computation.1 | convolution fusion | flops 23592960 | bytes 1407488 | tf_op jit(solution)/shard_map/dot_general | solution.py:73
  12.0 0.3 fusion.13
  12.3 2.6 %collective-permute-start.1 = (f32[1024]{0:T(1024)S(1)}, f32[1024]{0:T(1024)S(1)}, u32[]{:S(2)}, u32[]{:S(2)}) collective-permute-start(f32[1024]{0:T(1024)S(1)} %add.100), channel_id=1, source_target_pairs={{0,2},{1,3},{2,0},{3,1},{4,6},{5,7},{6,4},{7,5},{8,10},{9,11},{10,... | collective-permute-start | bytes 12296 | tf_op jit(solution)/shard_map/ppermute | solution.py:242
  14.9 1.6 %collective-permute-done.1 = f32[1024]{0:T(1024)S(1)} collective-permute-done((f32[1024]{0:T(1024)S(1)}, f32[1024]{0:T(1024)S(1)}, u32[]{:S(2)}, u32[]{:S(2)}) %collective-permute-start.1) | collective-permute-done | bytes 4128 | tf_op jit(solution)/shard_map/ppermute | solution.py:242
  16.5 2.1 %collective-permute-start.2 = (f32[1024]{0:T(1024)S(1)}, f32[1024]{0:T(1024)S(1)}, u32[]{:S(2)}, u32[]{:S(2)}) collective-permute-start(f32[1024]{0:T(1024)S(1)} %add.101), channel_id=1, source_target_pairs={{0,4},{1,5},{2,6},{3,7},{4,0},{5,1},{6,2},{7,3},{8,12},{9,13},{10,... | collective-permute-start | bytes 12296 | tf_op jit(solution)/shard_map/ppermute | solution.py:242
  18.7 1.5 %collective-permute-done.2 = f32[1024]{0:T(1024)S(1)} collective-permute-done((f32[1024]{0:T(1024)S(1)}, f32[1024]{0:T(1024)S(1)}, u32[]{:S(2)}, u32[]{:S(2)}) %collective-permute-start.2) | collective-permute-done | bytes 4128 | tf_op jit(solution)/shard_map/ppermute | solution.py:242
  20.2 3.0 %collective-permute-start.3 = (f32[1024]{0:T(1024)S(1)}, f32[1024]{0:T(1024)S(1)}, u32[]{:S(2)}, u32[]{:S(2)}) collective-permute-start(f32[1024]{0:T(1024)S(1)} %add.102), channel_id=1, source_target_pairs={{0,8},{1,9},{2,10},{3,11},{4,12},{5,13},{6,14},{7,15},{8,0},{9,1},... | collective-permute-start | bytes 12296 | tf_op jit(solution)/shard_map/ppermute | solution.py:242
  23.2 0.3 convolution_reduce_fusion.1
  23.6 0.4 copy.22.tproj_ref
  24.5 0.3 collective-permute-done.3
  24.8 1.4 %copy-done.1 = bf16[2,3,320,320]{3,2,1,0:T(8,128)(2,1)S(1)} copy-done((bf16[2,3,320,320]{3,2,1,0:T(8,128)(2,1)S(1)}, bf16[2,3,320,320]{3,2,1,0:T(8,128)(2,1)}, u32[]{:S(2)}) %copy-start.1) | copy-done | bytes 1228824
  26.2 33.8 %shard_map.149 = f32[2,16,1024]{2,1,0:T(8,128)S(1)} custom-call(f32[2,4,128,320]{3,2,1,0:T(8,128)} %convolution_bitcast_fusion.first_ref, f32[1,320]{1,0:T(1,128)S(1)} %add.99.emb_u_ref, f32[1,320]{1,0:T(1,128)S(1)} %get-tuple-element.13.time_ref, f32[1,1024]{1,0:T(1,128)S(1)} %bitcast.46, bf16[1024,320]{1,0:T(8,128)(2,1)S(1)} %copy.22.tproj_ref, ...), custom_call_target="tpu_custom_call" | custom-call | flops 7549747200 | bytes 6225920 | tf_op jit(solution)/shard_map/pallas_call | solution.py:217
  60.2 0.1 collective-permute-start.4
  60.3 1.2 %collective-permute-done.4 = f32[4,4,2,128]{3,2,1,0:T(2,128)S(1)} collective-permute-done((f32[4,4,2,128]{3,2,1,0:T(2,128)S(1)}, f32[4,4,2,128]{3,2,1,0:T(2,128)S(1)}, u32[]{:S(2)}, u32[]{:S(2)}) %collective-permute-start.4) | collective-permute-done | bytes 16416 | tf_op jit(solution)/shard_map/ppermute | solution.py:256
  61.4 1.9 %collective-permute-start.5 = (f32[4,4,2,128]{3,2,1,0:T(2,128)S(1)}, f32[4,4,2,128]{3,2,1,0:T(2,128)S(1)}, u32[]{:S(2)}, u32[]{:S(2)}) collective-permute-start(f32[4,4,2,128]{3,2,1,0:T(2,128)S(1)} %add.107), channel_id=1, source_target_pairs={{0,2},{1,3},{2,0},{3,1},{4,6},{5,7},{6,4},{7,5},{8,10},{9,11},{10,... | collective-permute-start | bytes 49160 | tf_op jit(solution)/shard_map/ppermute | solution.py:256
  63.4 1.9 %collective-permute-done.5 = f32[4,4,2,128]{3,2,1,0:T(2,128)S(1)} collective-permute-done((f32[4,4,2,128]{3,2,1,0:T(2,128)S(1)}, f32[4,4,2,128]{3,2,1,0:T(2,128)S(1)}, u32[]{:S(2)}, u32[]{:S(2)}) %collective-permute-start.5) | collective-permute-done | bytes 16416 | tf_op jit(solution)/shard_map/ppermute | solution.py:256
  65.3 2.0 %collective-permute-start.6 = (f32[4,4,2,128]{3,2,1,0:T(2,128)S(1)}, f32[4,4,2,128]{3,2,1,0:T(2,128)S(1)}, u32[]{:S(2)}, u32[]{:S(2)}) collective-permute-start(f32[4,4,2,128]{3,2,1,0:T(2,128)S(1)} %add.109), channel_id=1, source_target_pairs={{0,4},{1,5},{2,6},{3,7},{4,0},{5,1},{6,2},{7,3},{8,12},{9,13},{10,... | collective-permute-start | bytes 49160 | tf_op jit(solution)/shard_map/ppermute | solution.py:256
  67.2 1.8 %collective-permute-done.6 = f32[4,4,2,128]{3,2,1,0:T(2,128)S(1)} collective-permute-done((f32[4,4,2,128]{3,2,1,0:T(2,128)S(1)}, f32[4,4,2,128]{3,2,1,0:T(2,128)S(1)}, u32[]{:S(2)}, u32[]{:S(2)}) %collective-permute-start.6) | collective-permute-done | bytes 16416 | tf_op jit(solution)/shard_map/ppermute | solution.py:256
  69.1 3.0 %collective-permute-start.7 = (f32[4,4,2,128]{3,2,1,0:T(2,128)S(1)}, f32[4,4,2,128]{3,2,1,0:T(2,128)S(1)}, u32[]{:S(2)}, u32[]{:S(2)}) collective-permute-start(f32[4,4,2,128]{3,2,1,0:T(2,128)S(1)} %add.111), channel_id=1, source_target_pairs={{0,8},{1,9},{2,10},{3,11},{4,12},{5,13},{6,14},{7,15},{8,0},{9,1},... | collective-permute-start | bytes 49160 | tf_op jit(solution)/shard_map/ppermute | solution.py:256
  72.1 1.7 %collective-permute-done.7 = f32[4,4,2,128]{3,2,1,0:T(2,128)S(1)} collective-permute-done((f32[4,4,2,128]{3,2,1,0:T(2,128)S(1)}, f32[4,4,2,128]{3,2,1,0:T(2,128)S(1)}, u32[]{:S(2)}, u32[]{:S(2)}) %collective-permute-start.7) | collective-permute-done | bytes 16416 | tf_op jit(solution)/shard_map/ppermute | solution.py:256
  73.8 0.6 add_add_fusion
  (45 shorter events, 0.4 us)
Async XLA Ops:
  0.6 6.7 %copy-start = (bf16[320,1280]{1,0:T(8,128)(2,1)S(1)}, bf16[320,1280]{1,0:T(8,128)(2,1)}, u32[]{:S(2)}) copy-start(bf16[320,1280]{1,0:T(8,128)(2,1)} %param.21) | copy-start | bytes 2457604
  0.6 5.7 %copy-start.4 = (f32[1,4,4,2,128]{4,3,2,1,0:T(2,128)S(1)}, f32[1,4,4,2,128]{4,3,2,1,0:T(2,128)}, u32[]{:S(2)}) copy-start(f32[1,4,4,2,128]{4,3,2,1,0:T(2,128)} %param.17) | copy-start | bytes 49156
  0.7 5.8 %copy-start.6 = (bf16[9,320,4]{1,2,0:T(4,128)(2,1)S(1)}, bf16[9,320,4]{1,2,0:T(4,128)(2,1)}, u32[]{:S(2)}) copy-start(bf16[9,320,4]{1,2,0:T(4,128)(2,1)} %param.24) | copy-start | bytes 69124
  0.7 6.9 %copy-start.5 = (f32[1024]{0:T(1024)S(1)}, f32[1024]{0:T(1024)}, u32[]{:S(2)}) copy-start(f32[1024]{0:T(1024)} %param.20) | copy-start | bytes 12292
  0.7 11.3 %copy-start.3 = (bf16[1280,320]{0,1:T(8,128)(2,1)S(1)}, bf16[1280,320]{0,1:T(8,128)(2,1)}, u32[]{:S(2)}) copy-start(bf16[1280,320]{0,1:T(8,128)(2,1)} %param.22) | copy-start | bytes 2457604
  0.7 22.5 %copy-start.2 = (bf16[1024,320]{0,1:T(8,128)(2,1)S(1)}, bf16[1024,320]{0,1:T(8,128)(2,1)}, u32[]{:S(2)}) copy-start(bf16[1024,320]{0,1:T(8,128)(2,1)} %param.23) | copy-start | bytes 1966084
  1.7 22.8 %copy-start.7 = (bf16[9,4,320]{2,1,0:T(4,128)(2,1)S(1)}, bf16[9,4,320]{2,1,0:T(4,128)(2,1)}, u32[]{:S(2)}) copy-start(bf16[9,4,320]{2,1,0:T(4,128)(2,1)} %param.27) | copy-start | bytes 69124
  5.8 6.5 %collective-permute-start = (f32[1024]{0:T(1024)S(1)}, f32[1024]{0:T(1024)S(1)}, u32[]{:S(2)}, u32[]{:S(2)}) collective-permute-start(f32[1024]{0:T(1024)S(1)} %multiply_reduce_fusion), channel_id=1, source_target_pairs={{0,1},{1,0},{2,3},{3,2},{4,5},{5,4},{6,7},{7,6},{8,9},{9,8},{10,11... | collective-permute-start | bytes 12296 | tf_op jit(solution)/shard_map/ppermute | solution.py:242
  12.3 4.2 %collective-permute-start.1 = (f32[1024]{0:T(1024)S(1)}, f32[1024]{0:T(1024)S(1)}, u32[]{:S(2)}, u32[]{:S(2)}) collective-permute-start(f32[1024]{0:T(1024)S(1)} %add.100), channel_id=1, source_target_pairs={{0,2},{1,3},{2,0},{3,1},{4,6},{5,7},{6,4},{7,5},{8,10},{9,11},{10,... | collective-permute-start | bytes 12296 | tf_op jit(solution)/shard_map/ppermute | solution.py:242
  16.5 3.7 %collective-permute-start.2 = (f32[1024]{0:T(1024)S(1)}, f32[1024]{0:T(1024)S(1)}, u32[]{:S(2)}, u32[]{:S(2)}) collective-permute-start(f32[1024]{0:T(1024)S(1)} %add.101), channel_id=1, source_target_pairs={{0,4},{1,5},{2,6},{3,7},{4,0},{5,1},{6,2},{7,3},{8,12},{9,13},{10,... | collective-permute-start | bytes 12296 | tf_op jit(solution)/shard_map/ppermute | solution.py:242
  20.2 4.6 %collective-permute-start.3 = (f32[1024]{0:T(1024)S(1)}, f32[1024]{0:T(1024)S(1)}, u32[]{:S(2)}, u32[]{:S(2)}) collective-permute-start(f32[1024]{0:T(1024)S(1)} %add.102), channel_id=1, source_target_pairs={{0,8},{1,9},{2,10},{3,11},{4,12},{5,13},{6,14},{7,15},{8,0},{9,1},... | collective-permute-start | bytes 12296 | tf_op jit(solution)/shard_map/ppermute | solution.py:242
  24.8 1.4 %copy-start.1 = (bf16[2,3,320,320]{3,2,1,0:T(8,128)(2,1)S(1)}, bf16[2,3,320,320]{3,2,1,0:T(8,128)(2,1)}, u32[]{:S(2)}) copy-start(bf16[2,3,320,320]{3,2,1,0:T(8,128)(2,1)} %wt_hbm.1) | copy-start | bytes 3686404
  26.2 33.9 %copy-start.8 = (f32[1,4,4,2,128]{4,3,2,1,0:T(2,128)S(1)}, f32[1,4,4,2,128]{4,3,2,1,0:T(2,128)}, u32[]{:S(2)}) copy-start(f32[1,4,4,2,128]{4,3,2,1,0:T(2,128)} %param.18) | copy-start | bytes 49156
  26.2 47.6 %copy-start.9 = (f32[4,4,2,128]{3,2,1,0:T(2,128)S(1)}, f32[4,4,2,128]{3,2,1,0:T(2,128)}, u32[]{:S(2)}) copy-start(f32[4,4,2,128]{3,2,1,0:T(2,128)} %param.16) | copy-start | bytes 49156
  60.2 1.2 %collective-permute-start.4 = (f32[4,4,2,128]{3,2,1,0:T(2,128)S(1)}, f32[4,4,2,128]{3,2,1,0:T(2,128)S(1)}, u32[]{:S(2)}, u32[]{:S(2)}) collective-permute-start(f32[4,4,2,128]{3,2,1,0:T(2,128)S(1)} %fusion.7), channel_id=1, source_target_pairs={{0,1},{1,0},{2,3},{3,2},{4,5},{5,4},{6,7},{7,6},{8,9},{9,8},{10,11... | collective-permute-start | bytes 49160 | tf_op jit(solution)/shard_map/ppermute | solution.py:256
  61.4 3.8 %collective-permute-start.5 = (f32[4,4,2,128]{3,2,1,0:T(2,128)S(1)}, f32[4,4,2,128]{3,2,1,0:T(2,128)S(1)}, u32[]{:S(2)}, u32[]{:S(2)}) collective-permute-start(f32[4,4,2,128]{3,2,1,0:T(2,128)S(1)} %add.107), channel_id=1, source_target_pairs={{0,2},{1,3},{2,0},{3,1},{4,6},{5,7},{6,4},{7,5},{8,10},{9,11},{10,... | collective-permute-start | bytes 49160 | tf_op jit(solution)/shard_map/ppermute | solution.py:256
  65.3 3.8 %collective-permute-start.6 = (f32[4,4,2,128]{3,2,1,0:T(2,128)S(1)}, f32[4,4,2,128]{3,2,1,0:T(2,128)S(1)}, u32[]{:S(2)}, u32[]{:S(2)}) collective-permute-start(f32[4,4,2,128]{3,2,1,0:T(2,128)S(1)} %add.109), channel_id=1, source_target_pairs={{0,4},{1,5},{2,6},{3,7},{4,0},{5,1},{6,2},{7,3},{8,12},{9,13},{10,... | collective-permute-start | bytes 49160 | tf_op jit(solution)/shard_map/ppermute | solution.py:256
  69.1 4.7 %collective-permute-start.7 = (f32[4,4,2,128]{3,2,1,0:T(2,128)S(1)}, f32[4,4,2,128]{3,2,1,0:T(2,128)S(1)}, u32[]{:S(2)}, u32[]{:S(2)}) collective-permute-start(f32[4,4,2,128]{3,2,1,0:T(2,128)S(1)} %add.111), channel_id=1, source_target_pairs={{0,8},{1,9},{2,10},{3,11},{4,12},{5,13},{6,14},{7,15},{8,0},{9,1},... | collective-permute-start | bytes 49160 | tf_op jit(solution)/shard_map/ppermute | solution.py:256

commit v9 on v4

--- a/solution.py
+++ b/solution.py
@@ -237,10 +237,10 @@
     peers = lax.axis_size(axis)
     if peers & (peers - 1):
         return jnp.sum(lax.all_gather(x, axis), axis=0)
-    k = 1
-    while k < peers:
+    k = peers // 2
+    while k:
         x = x + lax.ppermute(x, axis, [(i, i ^ k) for i in range(peers)])
-        k *= 2
+        k //= 2
     return x
 
 

time: 74.3 us -> 74.1 us (level)
  starting transfers between devices: 15.1 us -> 11.1 us
  waiting for transfers between devices: 10 us -> 13.9 us
    ppermute x4, waiting for transfers between devices: 6.6 us -> 9.83 us  [butterfly_scan(): got = lax.ppermute(total, axis, [(i, i ^ k) for i in range(peers)])]
    ppermute x4, starting transfers between devices: 6.96 us -> 3.88 us  [butterfly_scan(): got = lax.ppermute(total, axis, [(i, i ^ k) for i in range(peers)])]
    ppermute x4, starting transfers between devices: 8.16 us -> 7.21 us  [butterfly_sum(): x = x + lax.ppermute(x, axis, [(i, i ^ k) for i in range(peers)])]
  transfers between devices with their start and end apart: 8 -> 8, of which waited for: 7 -> 6; matrix products, arithmetic and copies ran while one was open for 6% -> 6% of each run, Pallas kernels for 0% -> 0%
where the time goes in v9:
time: 74.1 us; the launch traced here: 73.9 us
  Pallas kernels  33.8 us (46%)
  waiting for transfers between devices  13.9 us (19%)
  starting transfers between devices  11.1 us (15%)
  matrix products  6.2 us (8%)
  between operations  3.44 us (5%)
  other arithmetic  3.28 us (4%)
  local copies, waits for them, and re-layouts  2.15 us (3%)
    pallas_call x1, Pallas kernels, unet(): pl.pallas_call(functools.partial(unet_body, count=float(count)), out_shap...  33.8 us
    ppermute x4, waiting for transfers between devices, butterfly_scan(): got = lax.ppermute(total, axis, [(i, i ^ k) for i in range(peers)])  9.83 us
    ppermute x4, starting transfers between devices, butterfly_sum(): x = x + lax.ppermute(x, axis, [(i, i ^ k) for i in range(peers)])  7.21 us
    ppermute x4, waiting for transfers between devices, butterfly_sum(): x = x + lax.ppermute(x, axis, [(i, i ^ k) for i in range(peers)])  4.04 us
    ppermute x4, starting transfers between devices, butterfly_scan(): got = lax.ppermute(total, axis, [(i, i ^ k) for i in range(peers)])  3.88 us
    dot_general x1, matrix products, local(): jnp.dot(counts, token_table, preferred_element_type=jnp.float32)[0]  3.73 us
    unnamed x22, local copies, waits for them, and re-layouts  1.77 us
    dot_general x1, matrix products, conv_lifted(): lax.dot_general(windows, stacked, (((0,), (1,)), ((), ())), preferred_ele...  1.56 us
  transfers between devices with their start and end apart: 8, of which 6 were waited for; matrix products, arithmetic and copies ran while one was open for 6% of the time, Pallas kernels for 0%

profile of v9, /device:TPU:0, one launch (start us, length us, event | category | flops | bytes accessed | tf_op | source)
XLA Modules:
  0.0 73.9 jit_solution(2744289352647064180)
XLA Ops:
  0.7 0.8 %broadcast_subtract_fusion = s32[77]{0:T(128)S(1)} fusion(s32[77]{0:T(128)} %param.15, s32[]{:T(128)S(6)} %mul.88), kind=kLoop, calls=%fused_computation.51 | loop fusion | flops 77 | bytes 620 | tf_op jit(solution)/shard_map/sub | solution.py:281
  1.5 0.2 convert_reduce_fusion
  1.7 3.7 %fusion.14 = f32[1,1024]{1,0:T(1,128)S(1)} fusion(bf16[3088,1]{0,1:T(2,128)(2,1)S(1)} %reshape.106, bf16[3088,1024]{1,0:T(8,128)(2,1)} %param.19), kind=kOutput, calls=%fused_computation.53 | convolution fusion | flops 6324224 | bytes 6334496 | tf_op jit(solution)/shard_map/dot_general | solution.py:284
  5.5 4.0 %collective-permute-start = (f32[1024]{0:T(1024)S(1)}, f32[1024]{0:T(1024)S(1)}, u32[]{:S(2)}, u32[]{:S(2)}) collective-permute-start(f32[1024]{0:T(1024)S(1)} %bitcast.54), channel_id=1, source_target_pairs={{0,8},{1,9},{2,10},{3,11},{4,12},{5,13},{6,14},{7,15},{8,0},{9,1},... | collective-permute-start | bytes 12296 | tf_op jit(solution)/shard_map/ppermute | solution.py:242
  9.5 0.1 pad_slice_fusion
  10.3 0.1 sine_convert_fusion
  10.4 0.1 pad_maximum_fusion
  10.5 0.2 convolution_reduce_fusion
  10.8 0.6 reduce_sum.27
  12.0 0.6 multiply_reduce_fusion
  13.3 0.1 compare_convert_fusion.same_ref
  13.4 0.2 concatenate.11
  13.6 1.6 %convolution_bitcast_fusion.first_ref = f32[2,4,128,320]{3,2,1,0:T(8,128)} fusion(bf16[320,36,1,1]{0,1,2,3:T(8,128)(2,1)S(1)} %reshape.99, bf16[36,4,2,128]{3,0,2,1:T(8,128)(2,1)S(1)} %concatenate.11), kind=kOutput, calls=%fused_computation | convolution fusion | flops 23592960 | bytes 1407488 | tf_op jit(solution)/shard_map/dot_general | solution.py:73
  15.1 0.3 fusion.13
  15.5 1.6 %collective-permute-start.1 = (f32[1024]{0:T(1024)S(1)}, f32[1024]{0:T(1024)S(1)}, u32[]{:S(2)}, u32[]{:S(2)}) collective-permute-start(f32[1024]{0:T(1024)S(1)} %add.100), channel_id=1, source_target_pairs={{0,4},{1,5},{2,6},{3,7},{4,0},{5,1},{6,2},{7,3},{8,12},{9,13},{10,... | collective-permute-start | bytes 12296 | tf_op jit(solution)/shard_map/ppermute | solution.py:242
  17.2 2.0 %collective-permute-done.1 = f32[1024]{0:T(1024)S(1)} collective-permute-done((f32[1024]{0:T(1024)S(1)}, f32[1024]{0:T(1024)S(1)}, u32[]{:S(2)}, u32[]{:S(2)}) %collective-permute-start.1) | collective-permute-done | bytes 4128 | tf_op jit(solution)/shard_map/ppermute | solution.py:242
  19.2 1.5 %collective-permute-start.2 = (f32[1024]{0:T(1024)S(1)}, f32[1024]{0:T(1024)S(1)}, u32[]{:S(2)}, u32[]{:S(2)}) collective-permute-start(f32[1024]{0:T(1024)S(1)} %add.101), channel_id=1, source_target_pairs={{0,2},{1,3},{2,0},{3,1},{4,6},{5,7},{6,4},{7,5},{8,10},{9,11},{10,... | collective-permute-start | bytes 12296 | tf_op jit(solution)/shard_map/ppermute | solution.py:242
  20.7 0.1 compare_convert_fusion.1.batch_ref
  20.8 2.0 %collective-permute-done.2 = f32[1024]{0:T(1024)S(1)} collective-permute-done((f32[1024]{0:T(1024)S(1)}, f32[1024]{0:T(1024)S(1)}, u32[]{:S(2)}, u32[]{:S(2)}) %collective-permute-start.2) | collective-permute-done | bytes 4128 | tf_op jit(solution)/shard_map/ppermute | solution.py:242
  22.8 0.3 convolution_reduce_fusion.1
  23.1 0.4 copy.22.tproj_ref
  24.1 1.4 %copy-done.1 = bf16[2,3,320,320]{3,2,1,0:T(8,128)(2,1)S(1)} copy-done((bf16[2,3,320,320]{3,2,1,0:T(8,128)(2,1)S(1)}, bf16[2,3,320,320]{3,2,1,0:T(8,128)(2,1)}, u32[]{:S(2)}) %copy-start.1) | copy-done | bytes 1228824
  25.5 33.8 %shard_map.149 = f32[2,16,1024]{2,1,0:T(8,128)S(1)} custom-call(f32[2,4,128,320]{3,2,1,0:T(8,128)} %convolution_bitcast_fusion.first_ref, f32[1,320]{1,0:T(1,128)S(1)} %add.99.emb_u_ref, f32[1,320]{1,0:T(1,128)S(1)} %get-tuple-element.13.time_ref, f32[1,1024]{1,0:T(1,128)S(1)} %bitcast.49, bf16[1024,320]{1,0:T(8,128)(2,1)S(1)} %copy.22.tproj_ref, ...), custom_call_target="tpu_custom_call" | custom-call | flops 7549747200 | bytes 6225920 | tf_op jit(solution)/shard_map/pallas_call | solution.py:217
  59.5 0.6 collective-permute-start.4
  60.0 0.8 %collective-permute-done.4 = f32[4,4,2,128]{3,2,1,0:T(2,128)S(1)} collective-permute-done((f32[4,4,2,128]{3,2,1,0:T(2,128)S(1)}, f32[4,4,2,128]{3,2,1,0:T(2,128)S(1)}, u32[]{:S(2)}, u32[]{:S(2)}) %collective-permute-start.4) | collective-permute-done | bytes 16416 | tf_op jit(solution)/shard_map/ppermute | solution.py:256
  60.9 1.6 %collective-permute-start.5 = (f32[4,4,2,128]{3,2,1,0:T(2,128)S(1)}, f32[4,4,2,128]{3,2,1,0:T(2,128)S(1)}, u32[]{:S(2)}, u32[]{:S(2)}) collective-permute-start(f32[4,4,2,128]{3,2,1,0:T(2,128)S(1)} %add.107), channel_id=1, source_target_pairs={{0,2},{1,3},{2,0},{3,1},{4,6},{5,7},{6,4},{7,5},{8,10},{9,11},{10,... | collective-permute-start | bytes 49160 | tf_op jit(solution)/shard_map/ppermute | solution.py:256
  62.5 2.2 %collective-permute-done.5 = f32[4,4,2,128]{3,2,1,0:T(2,128)S(1)} collective-permute-done((f32[4,4,2,128]{3,2,1,0:T(2,128)S(1)}, f32[4,4,2,128]{3,2,1,0:T(2,128)S(1)}, u32[]{:S(2)}, u32[]{:S(2)}) %collective-permute-start.5) | collective-permute-done | bytes 16416 | tf_op jit(solution)/shard_map/ppermute | solution.py:256
  64.7 1.6 %collective-permute-start.6 = (f32[4,4,2,128]{3,2,1,0:T(2,128)S(1)}, f32[4,4,2,128]{3,2,1,0:T(2,128)S(1)}, u32[]{:S(2)}, u32[]{:S(2)}) collective-permute-start(f32[4,4,2,128]{3,2,1,0:T(2,128)S(1)} %add.109), channel_id=1, source_target_pairs={{0,4},{1,5},{2,6},{3,7},{4,0},{5,1},{6,2},{7,3},{8,12},{9,13},{10,... | collective-permute-start | bytes 49160 | tf_op jit(solution)/shard_map/ppermute | solution.py:256
  66.3 2.2 %collective-permute-done.6 = f32[4,4,2,128]{3,2,1,0:T(2,128)S(1)} collective-permute-done((f32[4,4,2,128]{3,2,1,0:T(2,128)S(1)}, f32[4,4,2,128]{3,2,1,0:T(2,128)S(1)}, u32[]{:S(2)}, u32[]{:S(2)}) %collective-permute-start.6) | collective-permute-done | bytes 16416 | tf_op jit(solution)/shard_map/ppermute | solution.py:256
  68.5 0.1 collective-permute-start.7
  68.6 4.6 %collective-permute-done.7 = f32[4,4,2,128]{3,2,1,0:T(2,128)S(1)} collective-permute-done((f32[4,4,2,128]{3,2,1,0:T(2,128)S(1)}, f32[4,4,2,128]{3,2,1,0:T(2,128)S(1)}, u32[]{:S(2)}, u32[]{:S(2)}) %collective-permute-start.7) | collective-permute-done | bytes 16416 | tf_op jit(solution)/shard_map/ppermute | solution.py:256
  73.2 0.6 add_add_fusion
  (46 shorter events, 0.3 us)
Async XLA Ops:
  0.6 9.8 %copy-start = (bf16[320,1280]{1,0:T(8,128)(2,1)S(1)}, bf16[320,1280]{1,0:T(8,128)(2,1)}, u32[]{:S(2)}) copy-start(bf16[320,1280]{1,0:T(8,128)(2,1)} %param.21) | copy-start | bytes 2457604
  0.6 8.9 %copy-start.4 = (f32[1,4,4,2,128]{4,3,2,1,0:T(2,128)S(1)}, f32[1,4,4,2,128]{4,3,2,1,0:T(2,128)}, u32[]{:S(2)}) copy-start(f32[1,4,4,2,128]{4,3,2,1,0:T(2,128)} %param.17) | copy-start | bytes 49156
  0.7 9.0 %copy-start.6 = (bf16[9,320,4]{1,2,0:T(4,128)(2,1)S(1)}, bf16[9,320,4]{1,2,0:T(4,128)(2,1)}, u32[]{:S(2)}) copy-start(bf16[9,320,4]{1,2,0:T(4,128)(2,1)} %param.24) | copy-start | bytes 69124
  0.7 10.1 %copy-start.5 = (f32[1024]{0:T(1024)S(1)}, f32[1024]{0:T(1024)}, u32[]{:S(2)}) copy-start(f32[1024]{0:T(1024)} %param.20) | copy-start | bytes 12292
  0.7 14.5 %copy-start.3 = (bf16[1280,320]{0,1:T(8,128)(2,1)S(1)}, bf16[1280,320]{0,1:T(8,128)(2,1)}, u32[]{:S(2)}) copy-start(bf16[1280,320]{0,1:T(8,128)(2,1)} %param.22) | copy-start | bytes 2457604
  0.7 22.1 %copy-start.2 = (bf16[1024,320]{0,1:T(8,128)(2,1)S(1)}, bf16[1024,320]{0,1:T(8,128)(2,1)}, u32[]{:S(2)}) copy-start(bf16[1024,320]{0,1:T(8,128)(2,1)} %param.23) | copy-start | bytes 1966084
  1.7 22.3 %copy-start.7 = (bf16[9,4,320]{2,1,0:T(4,128)(2,1)S(1)}, bf16[9,4,320]{2,1,0:T(4,128)(2,1)}, u32[]{:S(2)}) copy-start(bf16[9,4,320]{2,1,0:T(4,128)(2,1)} %param.27) | copy-start | bytes 69124
  5.5 10.0 %collective-permute-start = (f32[1024]{0:T(1024)S(1)}, f32[1024]{0:T(1024)S(1)}, u32[]{:S(2)}, u32[]{:S(2)}) collective-permute-start(f32[1024]{0:T(1024)S(1)} %bitcast.54), channel_id=1, source_target_pairs={{0,8},{1,9},{2,10},{3,11},{4,12},{5,13},{6,14},{7,15},{8,0},{9,1},... | collective-permute-start | bytes 12296 | tf_op jit(solution)/shard_map/ppermute | solution.py:242
  15.5 3.7 %collective-permute-start.1 = (f32[1024]{0:T(1024)S(1)}, f32[1024]{0:T(1024)S(1)}, u32[]{:S(2)}, u32[]{:S(2)}) collective-permute-start(f32[1024]{0:T(1024)S(1)} %add.100), channel_id=1, source_target_pairs={{0,4},{1,5},{2,6},{3,7},{4,0},{5,1},{6,2},{7,3},{8,12},{9,13},{10,... | collective-permute-start | bytes 12296 | tf_op jit(solution)/shard_map/ppermute | solution.py:242
  19.2 3.6 %collective-permute-start.2 = (f32[1024]{0:T(1024)S(1)}, f32[1024]{0:T(1024)S(1)}, u32[]{:S(2)}, u32[]{:S(2)}) collective-permute-start(f32[1024]{0:T(1024)S(1)} %add.101), channel_id=1, source_target_pairs={{0,2},{1,3},{2,0},{3,1},{4,6},{5,7},{6,4},{7,5},{8,10},{9,11},{10,... | collective-permute-start | bytes 12296 | tf_op jit(solution)/shard_map/ppermute | solution.py:242
  22.8 1.3 %collective-permute-start.3 = (f32[1024]{0:T(1024)S(1)}, f32[1024]{0:T(1024)S(1)}, u32[]{:S(2)}, u32[]{:S(2)}) collective-permute-start(f32[1024]{0:T(1024)S(1)} %add.102), channel_id=1, source_target_pairs={{0,1},{1,0},{2,3},{3,2},{4,5},{5,4},{6,7},{7,6},{8,9},{9,8},{10,11... | collective-permute-start | bytes 12296 | tf_op jit(solution)/shard_map/ppermute | solution.py:242
  24.1 1.4 %copy-start.1 = (bf16[2,3,320,320]{3,2,1,0:T(8,128)(2,1)S(1)}, bf16[2,3,320,320]{3,2,1,0:T(8,128)(2,1)}, u32[]{:S(2)}) copy-start(bf16[2,3,320,320]{3,2,1,0:T(8,128)(2,1)} %wt_hbm.1) | copy-start | bytes 3686404
  25.5 33.9 %copy-start.8 = (f32[1,4,4,2,128]{4,3,2,1,0:T(2,128)S(1)}, f32[1,4,4,2,128]{4,3,2,1,0:T(2,128)}, u32[]{:S(2)}) copy-start(f32[1,4,4,2,128]{4,3,2,1,0:T(2,128)} %param.18) | copy-start | bytes 49156
  25.5 47.7 %copy-start.9 = (f32[4,4,2,128]{3,2,1,0:T(2,128)S(1)}, f32[4,4,2,128]{3,2,1,0:T(2,128)}, u32[]{:S(2)}) copy-start(f32[4,4,2,128]{3,2,1,0:T(2,128)} %param.16) | copy-start | bytes 49156
  59.5 1.4 %collective-permute-start.4 = (f32[4,4,2,128]{3,2,1,0:T(2,128)S(1)}, f32[4,4,2,128]{3,2,1,0:T(2,128)S(1)}, u32[]{:S(2)}, u32[]{:S(2)}) collective-permute-start(f32[4,4,2,128]{3,2,1,0:T(2,128)S(1)} %fusion.7), channel_id=1, source_target_pairs={{0,1},{1,0},{2,3},{3,2},{4,5},{5,4},{6,7},{7,6},{8,9},{9,8},{10,11... | collective-permute-start | bytes 49160 | tf_op jit(solution)/shard_map/ppermute | solution.py:256
  60.9 3.8 %collective-permute-start.5 = (f32[4,4,2,128]{3,2,1,0:T(2,128)S(1)}, f32[4,4,2,128]{3,2,1,0:T(2,128)S(1)}, u32[]{:S(2)}, u32[]{:S(2)}) collective-permute-start(f32[4,4,2,128]{3,2,1,0:T(2,128)S(1)} %add.107), channel_id=1, source_target_pairs={{0,2},{1,3},{2,0},{3,1},{4,6},{5,7},{6,4},{7,5},{8,10},{9,11},{10,... | collective-permute-start | bytes 49160 | tf_op jit(solution)/shard_map/ppermute | solution.py:256
  64.7 3.8 %collective-permute-start.6 = (f32[4,4,2,128]{3,2,1,0:T(2,128)S(1)}, f32[4,4,2,128]{3,2,1,0:T(2,128)S(1)}, u32[]{:S(2)}, u32[]{:S(2)}) collective-permute-start(f32[4,4,2,128]{3,2,1,0:T(2,128)S(1)} %add.109), channel_id=1, source_target_pairs={{0,4},{1,5},{2,6},{3,7},{4,0},{5,1},{6,2},{7,3},{8,12},{9,13},{10,... | collective-permute-start | bytes 49160 | tf_op jit(solution)/shard_map/ppermute | solution.py:256
  68.5 4.7 %collective-permute-start.7 = (f32[4,4,2,128]{3,2,1,0:T(2,128)S(1)}, f32[4,4,2,128]{3,2,1,0:T(2,128)S(1)}, u32[]{:S(2)}, u32[]{:S(2)}) collective-permute-start(f32[4,4,2,128]{3,2,1,0:T(2,128)S(1)} %add.111), channel_id=1, source_target_pairs={{0,8},{1,9},{2,10},{3,11},{4,12},{5,13},{6,14},{7,15},{8,0},{9,1},... | collective-permute-start | bytes 49160 | tf_op jit(solution)/shard_map/ppermute | solution.py:256

commit v10 on v9

--- a/solution.py
+++ b/solution.py
@@ -99,7 +99,7 @@
     copy_tm.start()
     same = same_ref[...]
     batch_mix = batch_ref[...]
-    hi = lax.Precision.HIGHEST
+    hi = lax.Precision.HIGH
 
     pooled = pooled_ref[...] / count
     average = jnp.mean(pooled, axis=1, keepdims=True)

time: 74.1 us -> 72.9 us (0.984)
  Pallas kernels: 33.8 us -> 32.6 us
    pallas_call x1, Pallas kernels: 33.8 us -> 32.6 us  [unet(): pl.pallas_call(functools.partial(unet_body, count=float(count)), out_shap...]
where the time goes in v10:
time: 72.9 us; the launch traced here: 72.6 us
  Pallas kernels  32.6 us (45%)
  waiting for transfers between devices  13.9 us (19%)
  starting transfers between devices  11.1 us (15%)
  matrix products  6.2 us (9%)
  between operations  3.43 us (5%)
  other arithmetic  3.28 us (4%)
  local copies, waits for them, and re-layouts  2.15 us (3%)
    pallas_call x1, Pallas kernels, unet(): pl.pallas_call(functools.partial(unet_body, count=float(count)), out_shap...  32.6 us
    ppermute x4, waiting for transfers between devices, butterfly_scan(): got = lax.ppermute(total, axis, [(i, i ^ k) for i in range(peers)])  9.82 us
    ppermute x4, starting transfers between devices, butterfly_sum(): x = x + lax.ppermute(x, axis, [(i, i ^ k) for i in range(peers)])  7.21 us
    ppermute x4, waiting for transfers between devices, butterfly_sum(): x = x + lax.ppermute(x, axis, [(i, i ^ k) for i in range(peers)])  4.04 us
    ppermute x4, starting transfers between devices, butterfly_scan(): got = lax.ppermute(total, axis, [(i, i ^ k) for i in range(peers)])  3.89 us
    dot_general x1, matrix products, local(): jnp.dot(counts, token_table, preferred_element_type=jnp.float32)[0]  3.73 us
    unnamed x22, local copies, waits for them, and re-layouts  1.77 us
    dot_general x1, matrix products, conv_lifted(): lax.dot_general(windows, stacked, (((0,), (1,)), ((), ())), preferred_ele...  1.56 us
  transfers between devices with their start and end apart: 8, of which 6 were waited for; matrix products, arithmetic and copies ran while one was open for 6% of the time, Pallas kernels for 0%

profile of v10, /device:TPU:0, one launch (start us, length us, event | category | flops | bytes accessed | tf_op | source)
XLA Modules:
  0.0 72.6 jit_solution(4509499237800505533)
XLA Ops:
  0.7 0.8 %broadcast_subtract_fusion = s32[77]{0:T(128)S(1)} fusion(s32[77]{0:T(128)} %param.15, s32[]{:T(128)S(6)} %mul.88), kind=kLoop, calls=%fused_computation.51 | loop fusion | flops 77 | bytes 620 | tf_op jit(solution)/shard_map/sub | solution.py:281
  1.5 0.2 convert_reduce_fusion
  1.7 3.7 %fusion.14 = f32[1,1024]{1,0:T(1,128)S(1)} fusion(bf16[3088,1]{0,1:T(2,128)(2,1)S(1)} %reshape.106, bf16[3088,1024]{1,0:T(8,128)(2,1)} %param.19), kind=kOutput, calls=%fused_computation.53 | convolution fusion | flops 6324224 | bytes 6334496 | tf_op jit(solution)/shard_map/dot_general | solution.py:284
  5.5 4.0 %collective-permute-start = (f32[1024]{0:T(1024)S(1)}, f32[1024]{0:T(1024)S(1)}, u32[]{:S(2)}, u32[]{:S(2)}) collective-permute-start(f32[1024]{0:T(1024)S(1)} %bitcast.54), channel_id=1, source_target_pairs={{0,8},{1,9},{2,10},{3,11},{4,12},{5,13},{6,14},{7,15},{8,0},{9,1},... | collective-permute-start | bytes 12296 | tf_op jit(solution)/shard_map/ppermute | solution.py:242
  9.5 0.1 pad_slice_fusion
  10.3 0.1 sine_convert_fusion
  10.4 0.1 pad_maximum_fusion
  10.5 0.2 convolution_reduce_fusion
  10.8 0.6 reduce_sum.27
  12.0 0.6 multiply_reduce_fusion
  13.3 0.1 compare_convert_fusion.same_ref
  13.4 0.2 concatenate.11
  13.6 1.6 %convolution_bitcast_fusion.first_ref = f32[2,4,128,320]{3,2,1,0:T(8,128)} fusion(bf16[320,36,1,1]{0,1,2,3:T(8,128)(2,1)S(1)} %reshape.99, bf16[36,4,2,128]{3,0,2,1:T(8,128)(2,1)S(1)} %concatenate.11), kind=kOutput, calls=%fused_computation | convolution fusion | flops 23592960 | bytes 1407488 | tf_op jit(solution)/shard_map/dot_general | solution.py:73
  15.1 0.3 fusion.13
  15.5 1.6 %collective-permute-start.1 = (f32[1024]{0:T(1024)S(1)}, f32[1024]{0:T(1024)S(1)}, u32[]{:S(2)}, u32[]{:S(2)}) collective-permute-start(f32[1024]{0:T(1024)S(1)} %add.100), channel_id=1, source_target_pairs={{0,4},{1,5},{2,6},{3,7},{4,0},{5,1},{6,2},{7,3},{8,12},{9,13},{10,... | collective-permute-start | bytes 12296 | tf_op jit(solution)/shard_map/ppermute | solution.py:242
  17.2 2.0 %collective-permute-done.1 = f32[1024]{0:T(1024)S(1)} collective-permute-done((f32[1024]{0:T(1024)S(1)}, f32[1024]{0:T(1024)S(1)}, u32[]{:S(2)}, u32[]{:S(2)}) %collective-permute-start.1) | collective-permute-done | bytes 4128 | tf_op jit(solution)/shard_map/ppermute | solution.py:242
  19.2 1.5 %collective-permute-start.2 = (f32[1024]{0:T(1024)S(1)}, f32[1024]{0:T(1024)S(1)}, u32[]{:S(2)}, u32[]{:S(2)}) collective-permute-start(f32[1024]{0:T(1024)S(1)} %add.101), channel_id=1, source_target_pairs={{0,2},{1,3},{2,0},{3,1},{4,6},{5,7},{6,4},{7,5},{8,10},{9,11},{10,... | collective-permute-start | bytes 12296 | tf_op jit(solution)/shard_map/ppermute | solution.py:242
  20.7 0.1 compare_convert_fusion.1.batch_ref
  20.8 2.0 %collective-permute-done.2 = f32[1024]{0:T(1024)S(1)} collective-permute-done((f32[1024]{0:T(1024)S(1)}, f32[1024]{0:T(1024)S(1)}, u32[]{:S(2)}, u32[]{:S(2)}) %collective-permute-start.2) | collective-permute-done | bytes 4128 | tf_op jit(solution)/shard_map/ppermute | solution.py:242
  22.8 0.3 convolution_reduce_fusion.1
  23.1 0.4 copy.22.tproj_ref
  24.1 1.4 %copy-done.1 = bf16[2,3,320,320]{3,2,1,0:T(8,128)(2,1)S(1)} copy-done((bf16[2,3,320,320]{3,2,1,0:T(8,128)(2,1)S(1)}, bf16[2,3,320,320]{3,2,1,0:T(8,128)(2,1)}, u32[]{:S(2)}) %copy-start.1) | copy-done | bytes 1228824
  25.5 32.6 %shard_map.149 = f32[2,16,1024]{2,1,0:T(8,128)S(1)} custom-call(f32[2,4,128,320]{3,2,1,0:T(8,128)} %convolution_bitcast_fusion.first_ref, f32[1,320]{1,0:T(1,128)S(1)} %add.99.emb_u_ref, f32[1,320]{1,0:T(1,128)S(1)} %get-tuple-element.13.time_ref, f32[1,1024]{1,0:T(1,128)S(1)} %bitcast.49, bf16[1024,320]{1,0:T(8,128)(2,1)S(1)} %copy.22.tproj_ref, ...), custom_call_target="tpu_custom_call" | custom-call | flops 7549747200 | bytes 6225920 | tf_op jit(solution)/shard_map/pallas_call | solution.py:217
  58.2 0.6 collective-permute-start.4
  58.8 0.8 %collective-permute-done.4 = f32[4,4,2,128]{3,2,1,0:T(2,128)S(1)} collective-permute-done((f32[4,4,2,128]{3,2,1,0:T(2,128)S(1)}, f32[4,4,2,128]{3,2,1,0:T(2,128)S(1)}, u32[]{:S(2)}, u32[]{:S(2)}) %collective-permute-start.4) | collective-permute-done | bytes 16416 | tf_op jit(solution)/shard_map/ppermute | solution.py:256
  59.6 1.6 %collective-permute-start.5 = (f32[4,4,2,128]{3,2,1,0:T(2,128)S(1)}, f32[4,4,2,128]{3,2,1,0:T(2,128)S(1)}, u32[]{:S(2)}, u32[]{:S(2)}) collective-permute-start(f32[4,4,2,128]{3,2,1,0:T(2,128)S(1)} %add.107), channel_id=1, source_target_pairs={{0,2},{1,3},{2,0},{3,1},{4,6},{5,7},{6,4},{7,5},{8,10},{9,11},{10,... | collective-permute-start | bytes 49160 | tf_op jit(solution)/shard_map/ppermute | solution.py:256
  61.2 2.2 %collective-permute-done.5 = f32[4,4,2,128]{3,2,1,0:T(2,128)S(1)} collective-permute-done((f32[4,4,2,128]{3,2,1,0:T(2,128)S(1)}, f32[4,4,2,128]{3,2,1,0:T(2,128)S(1)}, u32[]{:S(2)}, u32[]{:S(2)}) %collective-permute-start.5) | collective-permute-done | bytes 16416 | tf_op jit(solution)/shard_map/ppermute | solution.py:256
  63.5 1.6 %collective-permute-start.6 = (f32[4,4,2,128]{3,2,1,0:T(2,128)S(1)}, f32[4,4,2,128]{3,2,1,0:T(2,128)S(1)}, u32[]{:S(2)}, u32[]{:S(2)}) collective-permute-start(f32[4,4,2,128]{3,2,1,0:T(2,128)S(1)} %add.109), channel_id=1, source_target_pairs={{0,4},{1,5},{2,6},{3,7},{4,0},{5,1},{6,2},{7,3},{8,12},{9,13},{10,... | collective-permute-start | bytes 49160 | tf_op jit(solution)/shard_map/ppermute | solution.py:256
  65.1 2.2 %collective-permute-done.6 = f32[4,4,2,128]{3,2,1,0:T(2,128)S(1)} collective-permute-done((f32[4,4,2,128]{3,2,1,0:T(2,128)S(1)}, f32[4,4,2,128]{3,2,1,0:T(2,128)S(1)}, u32[]{:S(2)}, u32[]{:S(2)}) %collective-permute-start.6) | collective-permute-done | bytes 16416 | tf_op jit(solution)/shard_map/ppermute | solution.py:256
  67.3 0.1 collective-permute-start.7
  67.4 4.6 %collective-permute-done.7 = f32[4,4,2,128]{3,2,1,0:T(2,128)S(1)} collective-permute-done((f32[4,4,2,128]{3,2,1,0:T(2,128)S(1)}, f32[4,4,2,128]{3,2,1,0:T(2,128)S(1)}, u32[]{:S(2)}, u32[]{:S(2)}) %collective-permute-start.7) | collective-permute-done | bytes 16416 | tf_op jit(solution)/shard_map/ppermute | solution.py:256
  72.0 0.6 add_add_fusion
  (46 shorter events, 0.3 us)
Async XLA Ops:
  0.6 9.8 %copy-start = (bf16[320,1280]{1,0:T(8,128)(2,1)S(1)}, bf16[320,1280]{1,0:T(8,128)(2,1)}, u32[]{:S(2)}) copy-start(bf16[320,1280]{1,0:T(8,128)(2,1)} %param.21) | copy-start | bytes 2457604
  0.6 8.9 %copy-start.4 = (f32[1,4,4,2,128]{4,3,2,1,0:T(2,128)S(1)}, f32[1,4,4,2,128]{4,3,2,1,0:T(2,128)}, u32[]{:S(2)}) copy-start(f32[1,4,4,2,128]{4,3,2,1,0:T(2,128)} %param.17) | copy-start | bytes 49156
  0.7 9.0 %copy-start.6 = (bf16[9,320,4]{1,2,0:T(4,128)(2,1)S(1)}, bf16[9,320,4]{1,2,0:T(4,128)(2,1)}, u32[]{:S(2)}) copy-start(bf16[9,320,4]{1,2,0:T(4,128)(2,1)} %param.24) | copy-start | bytes 69124
  0.7 10.1 %copy-start.5 = (f32[1024]{0:T(1024)S(1)}, f32[1024]{0:T(1024)}, u32[]{:S(2)}) copy-start(f32[1024]{0:T(1024)} %param.20) | copy-start | bytes 12292
  0.7 14.5 %copy-start.3 = (bf16[1280,320]{0,1:T(8,128)(2,1)S(1)}, bf16[1280,320]{0,1:T(8,128)(2,1)}, u32[]{:S(2)}) copy-start(bf16[1280,320]{0,1:T(8,128)(2,1)} %param.22) | copy-start | bytes 2457604
  0.7 22.1 %copy-start.2 = (bf16[1024,320]{0,1:T(8,128)(2,1)S(1)}, bf16[1024,320]{0,1:T(8,128)(2,1)}, u32[]{:S(2)}) copy-start(bf16[1024,320]{0,1:T(8,128)(2,1)} %param.23) | copy-start | bytes 1966084
  1.7 22.3 %copy-start.7 = (bf16[9,4,320]{2,1,0:T(4,128)(2,1)S(1)}, bf16[9,4,320]{2,1,0:T(4,128)(2,1)}, u32[]{:S(2)}) copy-start(bf16[9,4,320]{2,1,0:T(4,128)(2,1)} %param.27) | copy-start | bytes 69124
  5.5 10.0 %collective-permute-start = (f32[1024]{0:T(1024)S(1)}, f32[1024]{0:T(1024)S(1)}, u32[]{:S(2)}, u32[]{:S(2)}) collective-permute-start(f32[1024]{0:T(1024)S(1)} %bitcast.54), channel_id=1, source_target_pairs={{0,8},{1,9},{2,10},{3,11},{4,12},{5,13},{6,14},{7,15},{8,0},{9,1},... | collective-permute-start | bytes 12296 | tf_op jit(solution)/shard_map/ppermute | solution.py:242
  15.5 3.7 %collective-permute-start.1 = (f32[1024]{0:T(1024)S(1)}, f32[1024]{0:T(1024)S(1)}, u32[]{:S(2)}, u32[]{:S(2)}) collective-permute-start(f32[1024]{0:T(1024)S(1)} %add.100), channel_id=1, source_target_pairs={{0,4},{1,5},{2,6},{3,7},{4,0},{5,1},{6,2},{7,3},{8,12},{9,13},{10,... | collective-permute-start | bytes 12296 | tf_op jit(solution)/shard_map/ppermute | solution.py:242
  19.2 3.6 %collective-permute-start.2 = (f32[1024]{0:T(1024)S(1)}, f32[1024]{0:T(1024)S(1)}, u32[]{:S(2)}, u32[]{:S(2)}) collective-permute-start(f32[1024]{0:T(1024)S(1)} %add.101), channel_id=1, source_target_pairs={{0,2},{1,3},{2,0},{3,1},{4,6},{5,7},{6,4},{7,5},{8,10},{9,11},{10,... | collective-permute-start | bytes 12296 | tf_op jit(solution)/shard_map/ppermute | solution.py:242
  22.8 1.3 %collective-permute-start.3 = (f32[1024]{0:T(1024)S(1)}, f32[1024]{0:T(1024)S(1)}, u32[]{:S(2)}, u32[]{:S(2)}) collective-permute-start(f32[1024]{0:T(1024)S(1)} %add.102), channel_id=1, source_target_pairs={{0,1},{1,0},{2,3},{3,2},{4,5},{5,4},{6,7},{7,6},{8,9},{9,8},{10,11... | collective-permute-start | bytes 12296 | tf_op jit(solution)/shard_map/ppermute | solution.py:242
  24.1 1.4 %copy-start.1 = (bf16[2,3,320,320]{3,2,1,0:T(8,128)(2,1)S(1)}, bf16[2,3,320,320]{3,2,1,0:T(8,128)(2,1)}, u32[]{:S(2)}) copy-start(bf16[2,3,320,320]{3,2,1,0:T(8,128)(2,1)} %wt_hbm.1) | copy-start | bytes 3686404
  25.5 32.7 %copy-start.8 = (f32[1,4,4,2,128]{4,3,2,1,0:T(2,128)S(1)}, f32[1,4,4,2,128]{4,3,2,1,0:T(2,128)}, u32[]{:S(2)}) copy-start(f32[1,4,4,2,128]{4,3,2,1,0:T(2,128)} %param.18) | copy-start | bytes 49156
  25.5 46.5 %copy-start.9 = (f32[4,4,2,128]{3,2,1,0:T(2,128)S(1)}, f32[4,4,2,128]{3,2,1,0:T(2,128)}, u32[]{:S(2)}) copy-start(f32[4,4,2,128]{3,2,1,0:T(2,128)} %param.16) | copy-start | bytes 49156
  58.2 1.4 %collective-permute-start.4 = (f32[4,4,2,128]{3,2,1,0:T(2,128)S(1)}, f32[4,4,2,128]{3,2,1,0:T(2,128)S(1)}, u32[]{:S(2)}, u32[]{:S(2)}) collective-permute-start(f32[4,4,2,128]{3,2,1,0:T(2,128)S(1)} %fusion.7), channel_id=1, source_target_pairs={{0,1},{1,0},{2,3},{3,2},{4,5},{5,4},{6,7},{7,6},{8,9},{9,8},{10,11... | collective-permute-start | bytes 49160 | tf_op jit(solution)/shard_map/ppermute | solution.py:256
  59.6 3.8 %collective-permute-start.5 = (f32[4,4,2,128]{3,2,1,0:T(2,128)S(1)}, f32[4,4,2,128]{3,2,1,0:T(2,128)S(1)}, u32[]{:S(2)}, u32[]{:S(2)}) collective-permute-start(f32[4,4,2,128]{3,2,1,0:T(2,128)S(1)} %add.107), channel_id=1, source_target_pairs={{0,2},{1,3},{2,0},{3,1},{4,6},{5,7},{6,4},{7,5},{8,10},{9,11},{10,... | collective-permute-start | bytes 49160 | tf_op jit(solution)/shard_map/ppermute | solution.py:256
  63.5 3.8 %collective-permute-start.6 = (f32[4,4,2,128]{3,2,1,0:T(2,128)S(1)}, f32[4,4,2,128]{3,2,1,0:T(2,128)S(1)}, u32[]{:S(2)}, u32[]{:S(2)}) collective-permute-start(f32[4,4,2,128]{3,2,1,0:T(2,128)S(1)} %add.109), channel_id=1, source_target_pairs={{0,4},{1,5},{2,6},{3,7},{4,0},{5,1},{6,2},{7,3},{8,12},{9,13},{10,... | collective-permute-start | bytes 49160 | tf_op jit(solution)/shard_map/ppermute | solution.py:256
  67.3 4.7 %collective-permute-start.7 = (f32[4,4,2,128]{3,2,1,0:T(2,128)S(1)}, f32[4,4,2,128]{3,2,1,0:T(2,128)S(1)}, u32[]{:S(2)}, u32[]{:S(2)}) collective-permute-start(f32[4,4,2,128]{3,2,1,0:T(2,128)S(1)} %add.111), channel_id=1, source_target_pairs={{0,8},{1,9},{2,10},{3,11},{4,12},{5,13},{6,14},{7,15},{8,0},{9,1},... | collective-permute-start | bytes 49160 | tf_op jit(solution)/shard_map/ppermute | solution.py:256

commit v11 on v10

--- a/solution.py
+++ b/solution.py
@@ -282,7 +282,6 @@
     hits = local_ids[:, None] == jnp.arange(shard_rows, dtype=jnp.int32)[None, :]
     counts = jnp.sum(hits.astype(jnp.float32), axis=0).astype(jnp.bfloat16)[None]
     partial = jnp.dot(counts, token_table, preferred_element_type=jnp.float32)[0]
-    pooled = butterfly_sum(partial, "slot")[None]
     text_uncond = layer_norm(empty_text).astype(jnp.bfloat16)[None]
     vector_uncond = jnp.dot(text_uncond, text_proj, preferred_element_type=jnp.float32)
     half_width = time_in.shape[0] // 2
@@ -296,6 +295,10 @@
     time_vector = jnp.dot(hidden, time_out, preferred_element_type=jnp.float32)
     latent = iterate[0]
     first = conv_lifted(latent.astype(jnp.bfloat16), conv_first)
+    partial, first, vector_uncond, time_vector = lax.optimization_barrier(
+        (partial, first, vector_uncond, time_vector)
+    )
+    pooled = butterfly_sum(partial, "slot")[None]
     rows, frames, cols, chans = first.shape
     predicted = unet(
         first, vector_uncond + time_vector, time_vector, pooled, text_proj,

time: 72.9 us -> 79.1 us (1.085)
  starting transfers between devices: 11.1 us -> 15.1 us
  waiting for transfers between devices: 13.9 us -> 11.4 us
  other arithmetic: 3.28 us -> 5.2 us
  local copies, waits for them, and re-layouts: 2.15 us -> 3.7 us
  matrix products: 6.2 us -> 7.27 us
    ppermute x4, waiting for transfers between devices: 9.82 us -> 6.3 us  [butterfly_scan(): got = lax.ppermute(total, axis, [(i, i ^ k) for i in range(peers)])]
    ppermute x4, starting transfers between devices: 3.89 us -> 7.26 us  [butterfly_scan(): got = lax.ppermute(total, axis, [(i, i ^ k) for i in range(peers)])]
    dot_general x1, matrix products: 0.34 us -> 1.42 us  [local(): time_vector = jnp.dot(hidden, time_out, preferred_element_type=jnp.float32)]
    ppermute x4, waiting for transfers between devices: 4.04 us -> 5.09 us  [butterfly_sum(): x = x + lax.ppermute(x, axis, [(i, i ^ k) for i in range(peers)])]
    unnamed x22 -> x16, local copies, waits for them, and re-layouts: 1.77 us -> 2.59 us
  transfers between devices with their start and end apart: 8 -> 8, of which waited for: 6 -> 8; matrix products, arithmetic and copies ran while one was open for 6% -> 1% of each run, Pallas kernels for 0% -> 0%
where the time goes in v11:
time: 79.1 us; the launch traced here: 78.6 us
  Pallas kernels  32.6 us (41%)
  starting transfers between devices  15.1 us (19%)
  waiting for transfers between devices  11.4 us (14%)
  matrix products  7.27 us (9%)
  other arithmetic  5.2 us (7%)
  local copies, waits for them, and re-layouts  3.7 us (5%)
  between operations  3.32 us (4%)
    pallas_call x1, Pallas kernels, unet(): pl.pallas_call(functools.partial(unet_body, count=float(count)), out_shap...  32.6 us
    ppermute x4, starting transfers between devices, butterfly_sum(): x = x + lax.ppermute(x, axis, [(i, i ^ k) for i in range(peers)])  7.83 us
    ppermute x4, starting transfers between devices, butterfly_scan(): got = lax.ppermute(total, axis, [(i, i ^ k) for i in range(peers)])  7.26 us
    ppermute x4, waiting for transfers between devices, butterfly_scan(): got = lax.ppermute(total, axis, [(i, i ^ k) for i in range(peers)])  6.3 us
    ppermute x4, waiting for transfers between devices, butterfly_sum(): x = x + lax.ppermute(x, axis, [(i, i ^ k) for i in range(peers)])  5.09 us
    dot_general x1, matrix products, local(): jnp.dot(counts, token_table, preferred_element_type=jnp.float32)[0]  3.77 us
    unnamed x16, local copies, waits for them, and re-layouts  2.59 us
  transfers between devices with their start and end apart: 8, of which 8 were waited for; matrix products, arithmetic and copies ran while one was open for 1% of the time, Pallas kernels for 0%

profile of v11, /device:TPU:0, one launch (start us, length us, event | category | flops | bytes accessed | tf_op | source)
XLA Modules:
  0.0 78.6 jit_solution(3300134189926460394)
XLA Ops:
  0.7 0.8 %copy.33 = bf16[1,4,4,2,128]{4,1,3,2,0:T(4,128)(2,1)S(1)} copy(f32[1,4,4,2,128]{4,3,2,1,0:T(2,128)} %param.17) | data formatting | bytes 24576 | tf_op args[3]
  1.6 0.8 reshape.99
  3.2 0.2 convolution_reduce_fusion
  3.4 0.7 broadcast_subtract_fusion
  4.1 0.2 convert_reduce_fusion
  4.3 1.3 %reduce_sum.28 = f32[]{:T(128)} reduce(f32[1024]{0:T(1024)} %param.20, f32[]{:T(128)} %constant.72.clone.1), dimensions={0}, to_apply=%region_1.0 | reduce | flops 1023 | bytes 4104 | tf_op jit(solution)/shard_map/reduce_sum | solution.py:25
  6.3 1.3 %multiply_reduce_fusion = f32[]{:T(128)} fusion(f32[1024]{0:T(1024)} %param.20, f32[]{:T(128)S(6)} %div.65), kind=kLoop, calls=%fused_computation.36 | loop fusion | flops 3071 | bytes 4104 | tf_op jit(solution)/shard_map/reduce_sum | solution.py:26
  8.2 0.7 multiply_convert_fusion.1
  9.0 0.1 concatenate.11
  9.1 1.6 %convolution_bitcast_fusion.first_ref = f32[2,4,128,320]{3,2,1,0:T(8,128)} fusion(bf16[320,36,1,1]{0,1,2,3:T(8,128)(2,1)S(1)} %reshape.99, bf16[36,4,2,128]{3,0,2,1:T(8,128)(2,1)S(1)} %concatenate.11), kind=kOutput, calls=%fused_computation | convolution fusion | flops 23592960 | bytes 1407488 | tf_op jit(solution)/shard_map/dot_general | solution.py:73
  10.7 1.4 %fusion.15.time_ref = f32[1,320]{1,0:T(1,128)S(1)} fusion(bf16[1280,1]{0,1:T(2,128)(2,1)S(1)} %reshape.104, bf16[1280,320]{0,1:T(8,128)(2,1)} %param.22), kind=kOutput, calls=%fused_computation.53 | convolution fusion | flops 819200 | bytes 823040 | tf_op jit(solution)/shard_map/dot_general | solution.py:295
  12.1 3.8 %fusion.13 = f32[1,1024]{1,0:T(1,128)S(1)} fusion(bf16[3088,1]{0,1:T(2,128)(2,1)S(1)} %reshape.97, bf16[3088,1024]{1,0:T(8,128)(2,1)} %param.19), kind=kOutput, calls=%fused_computation.51 | convolution fusion | flops 6324224 | bytes 6334496 | tf_op jit(solution)/shard_map/dot_general | solution.py:284
  15.9 0.3 fusion.14
  16.2 4.1 %collective-permute-start = (f32[1024]{0:T(1024)S(1)}, f32[1024]{0:T(1024)S(1)}, u32[]{:S(2)}, u32[]{:S(2)}) collective-permute-start(f32[1024]{0:T(1024)S(1)} %bitcast.54), channel_id=1, source_target_pairs={{0,8},{1,9},{2,10},{3,11},{4,12},{5,13},{6,14},{7,15},{8,0},{9,1},... | collective-permute-start | bytes 12296 | tf_op jit(solution)/shard_map/ppermute | solution.py:242
  20.2 1.6 %collective-permute-done = f32[1024]{0:T(1024)S(1)} collective-permute-done((f32[1024]{0:T(1024)S(1)}, f32[1024]{0:T(1024)S(1)}, u32[]{:S(2)}, u32[]{:S(2)}) %collective-permute-start) | collective-permute-done | bytes 4128 | tf_op jit(solution)/shard_map/ppermute | solution.py:242
  21.8 1.9 %collective-permute-start.1 = (f32[1024]{0:T(1024)S(1)}, f32[1024]{0:T(1024)S(1)}, u32[]{:S(2)}, u32[]{:S(2)}) collective-permute-start(f32[1024]{0:T(1024)S(1)} %add.97), channel_id=1, source_target_pairs={{0,4},{1,5},{2,6},{3,7},{4,0},{5,1},{6,2},{7,3},{8,12},{9,13},{10,... | collective-permute-start | bytes 12296 | tf_op jit(solution)/shard_map/ppermute | solution.py:242
  23.8 1.6 %collective-permute-done.1 = f32[1024]{0:T(1024)S(1)} collective-permute-done((f32[1024]{0:T(1024)S(1)}, f32[1024]{0:T(1024)S(1)}, u32[]{:S(2)}, u32[]{:S(2)}) %collective-permute-start.1) | collective-permute-done | bytes 4128 | tf_op jit(solution)/shard_map/ppermute | solution.py:242
  25.4 1.9 %collective-permute-start.2 = (f32[1024]{0:T(1024)S(1)}, f32[1024]{0:T(1024)S(1)}, u32[]{:S(2)}, u32[]{:S(2)}) collective-permute-start(f32[1024]{0:T(1024)S(1)} %add.98), channel_id=1, source_target_pairs={{0,2},{1,3},{2,0},{3,1},{4,6},{5,7},{6,4},{7,5},{8,10},{9,11},{10,... | collective-permute-start | bytes 12296 | tf_op jit(solution)/shard_map/ppermute | solution.py:242
  27.3 1.8 %collective-permute-done.2 = f32[1024]{0:T(1024)S(1)} collective-permute-done((f32[1024]{0:T(1024)S(1)}, f32[1024]{0:T(1024)S(1)}, u32[]{:S(2)}, u32[]{:S(2)}) %collective-permute-start.2) | collective-permute-done | bytes 4128 | tf_op jit(solution)/shard_map/ppermute | solution.py:242
  29.1 0.4 copy.22.tproj_ref
  30.0 0.2 collective-permute-done.3
  30.2 1.4 %copy-done.1 = bf16[2,3,320,320]{3,2,1,0:T(8,128)(2,1)S(1)} copy-done((bf16[2,3,320,320]{3,2,1,0:T(8,128)(2,1)S(1)}, bf16[2,3,320,320]{3,2,1,0:T(8,128)(2,1)}, u32[]{:S(2)}) %copy-start.1) | copy-done | bytes 1228824
  31.6 32.6 %shard_map.149 = f32[2,16,1024]{2,1,0:T(8,128)S(1)} custom-call(f32[2,4,128,320]{3,2,1,0:T(8,128)} %convolution_bitcast_fusion.first_ref, f32[1,320]{1,0:T(1,128)S(1)} %add.96.emb_u_ref, f32[1,320]{1,0:T(1,128)S(1)} %fusion.15.time_ref, f32[1,1024]{1,0:T(1,128)S(1)} %bitcast.49, bf16[1024,320]{1,0:T(8,128)(2,1)S(1)} %copy.22.tproj_ref, ...), custom_call_target="tpu_custom_call" | custom-call | flops 7549747200 | bytes 6225920 | tf_op jit(solution)/shard_map/pallas_call | solution.py:217
  64.4 0.4 collective-permute-start.4
  64.8 0.8 %collective-permute-done.4 = f32[4,4,2,128]{3,2,1,0:T(2,128)S(1)} collective-permute-done((f32[4,4,2,128]{3,2,1,0:T(2,128)S(1)}, f32[4,4,2,128]{3,2,1,0:T(2,128)S(1)}, u32[]{:S(2)}, u32[]{:S(2)}) %collective-permute-start.4) | collective-permute-done | bytes 16416 | tf_op jit(solution)/shard_map/ppermute | solution.py:256
  65.6 1.9 %collective-permute-start.5 = (f32[4,4,2,128]{3,2,1,0:T(2,128)S(1)}, f32[4,4,2,128]{3,2,1,0:T(2,128)S(1)}, u32[]{:S(2)}, u32[]{:S(2)}) collective-permute-start(f32[4,4,2,128]{3,2,1,0:T(2,128)S(1)} %add.104), channel_id=1, source_target_pairs={{0,2},{1,3},{2,0},{3,1},{4,6},{5,7},{6,4},{7,5},{8,10},{9,11},{10,... | collective-permute-start | bytes 49160 | tf_op jit(solution)/shard_map/ppermute | solution.py:256
  67.5 1.9 %collective-permute-done.5 = f32[4,4,2,128]{3,2,1,0:T(2,128)S(1)} collective-permute-done((f32[4,4,2,128]{3,2,1,0:T(2,128)S(1)}, f32[4,4,2,128]{3,2,1,0:T(2,128)S(1)}, u32[]{:S(2)}, u32[]{:S(2)}) %collective-permute-start.5) | collective-permute-done | bytes 16416 | tf_op jit(solution)/shard_map/ppermute | solution.py:256
  69.4 2.0 %collective-permute-start.6 = (f32[4,4,2,128]{3,2,1,0:T(2,128)S(1)}, f32[4,4,2,128]{3,2,1,0:T(2,128)S(1)}, u32[]{:S(2)}, u32[]{:S(2)}) collective-permute-start(f32[4,4,2,128]{3,2,1,0:T(2,128)S(1)} %add.106), channel_id=1, source_target_pairs={{0,4},{1,5},{2,6},{3,7},{4,0},{5,1},{6,2},{7,3},{8,12},{9,13},{10,... | collective-permute-start | bytes 49160 | tf_op jit(solution)/shard_map/ppermute | solution.py:256
  71.4 1.8 %collective-permute-done.6 = f32[4,4,2,128]{3,2,1,0:T(2,128)S(1)} collective-permute-done((f32[4,4,2,128]{3,2,1,0:T(2,128)S(1)}, f32[4,4,2,128]{3,2,1,0:T(2,128)S(1)}, u32[]{:S(2)}, u32[]{:S(2)}) %collective-permute-start.6) | collective-permute-done | bytes 16416 | tf_op jit(solution)/shard_map/ppermute | solution.py:256
  73.3 3.0 %collective-permute-start.7 = (f32[4,4,2,128]{3,2,1,0:T(2,128)S(1)}, f32[4,4,2,128]{3,2,1,0:T(2,128)S(1)}, u32[]{:S(2)}, u32[]{:S(2)}) collective-permute-start(f32[4,4,2,128]{3,2,1,0:T(2,128)S(1)} %add.108), channel_id=1, source_target_pairs={{0,8},{1,9},{2,10},{3,11},{4,12},{5,13},{6,14},{7,15},{8,0},{9,1},... | collective-permute-start | bytes 49160 | tf_op jit(solution)/shard_map/ppermute | solution.py:256
  76.2 1.7 %collective-permute-done.7 = f32[4,4,2,128]{3,2,1,0:T(2,128)S(1)} collective-permute-done((f32[4,4,2,128]{3,2,1,0:T(2,128)S(1)}, f32[4,4,2,128]{3,2,1,0:T(2,128)S(1)}, u32[]{:S(2)}, u32[]{:S(2)}) %collective-permute-start.7) | collective-permute-done | bytes 16416 | tf_op jit(solution)/shard_map/ppermute | solution.py:256
  78.0 0.6 add_add_fusion
  (39 shorter events, 0.6 us)
Async XLA Ops:
  0.6 2.5 %copy-start = (bf16[320,1280]{1,0:T(8,128)(2,1)S(1)}, bf16[320,1280]{1,0:T(8,128)(2,1)}, u32[]{:S(2)}) copy-start(bf16[320,1280]{1,0:T(8,128)(2,1)} %param.21) | copy-start | bytes 2457604
  0.6 15.2 %copy-start.2 = (bf16[1024,320]{0,1:T(8,128)(2,1)S(1)}, bf16[1024,320]{0,1:T(8,128)(2,1)}, u32[]{:S(2)}) copy-start(bf16[1024,320]{0,1:T(8,128)(2,1)} %param.23) | copy-start | bytes 1966084
  3.1 26.8 %copy-start.4 = (bf16[9,4,320]{2,1,0:T(4,128)(2,1)S(1)}, bf16[9,4,320]{2,1,0:T(4,128)(2,1)}, u32[]{:S(2)}) copy-start(bf16[9,4,320]{2,1,0:T(4,128)(2,1)} %param.27) | copy-start | bytes 69124
  16.2 5.7 %collective-permute-start = (f32[1024]{0:T(1024)S(1)}, f32[1024]{0:T(1024)S(1)}, u32[]{:S(2)}, u32[]{:S(2)}) collective-permute-start(f32[1024]{0:T(1024)S(1)} %bitcast.54), channel_id=1, source_target_pairs={{0,8},{1,9},{2,10},{3,11},{4,12},{5,13},{6,14},{7,15},{8,0},{9,1},... | collective-permute-start | bytes 12296 | tf_op jit(solution)/shard_map/ppermute | solution.py:242
  21.8 3.6 %collective-permute-start.1 = (f32[1024]{0:T(1024)S(1)}, f32[1024]{0:T(1024)S(1)}, u32[]{:S(2)}, u32[]{:S(2)}) collective-permute-start(f32[1024]{0:T(1024)S(1)} %add.97), channel_id=1, source_target_pairs={{0,4},{1,5},{2,6},{3,7},{4,0},{5,1},{6,2},{7,3},{8,12},{9,13},{10,... | collective-permute-start | bytes 12296 | tf_op jit(solution)/shard_map/ppermute | solution.py:242
  25.4 3.6 %collective-permute-start.2 = (f32[1024]{0:T(1024)S(1)}, f32[1024]{0:T(1024)S(1)}, u32[]{:S(2)}, u32[]{:S(2)}) collective-permute-start(f32[1024]{0:T(1024)S(1)} %add.98), channel_id=1, source_target_pairs={{0,2},{1,3},{2,0},{3,1},{4,6},{5,7},{6,4},{7,5},{8,10},{9,11},{10,... | collective-permute-start | bytes 12296 | tf_op jit(solution)/shard_map/ppermute | solution.py:242
  29.0 1.2 %collective-permute-start.3 = (f32[1024]{0:T(1024)S(1)}, f32[1024]{0:T(1024)S(1)}, u32[]{:S(2)}, u32[]{:S(2)}) collective-permute-start(f32[1024]{0:T(1024)S(1)} %add.99), channel_id=1, source_target_pairs={{0,1},{1,0},{2,3},{3,2},{4,5},{5,4},{6,7},{7,6},{8,9},{9,8},{10,11... | collective-permute-start | bytes 12296 | tf_op jit(solution)/shard_map/ppermute | solution.py:242
  30.2 1.4 %copy-start.1 = (bf16[2,3,320,320]{3,2,1,0:T(8,128)(2,1)S(1)}, bf16[2,3,320,320]{3,2,1,0:T(8,128)(2,1)}, u32[]{:S(2)}) copy-start(bf16[2,3,320,320]{3,2,1,0:T(8,128)(2,1)} %wt_hbm.1) | copy-start | bytes 3686404
  31.6 32.7 %copy-start.3 = (f32[1,4,4,2,128]{4,3,2,1,0:T(2,128)S(1)}, f32[1,4,4,2,128]{4,3,2,1,0:T(2,128)}, u32[]{:S(2)}) copy-start(f32[1,4,4,2,128]{4,3,2,1,0:T(2,128)} %param.17) | copy-start | bytes 49156
  31.6 32.7 %copy-start.5 = (f32[1,4,4,2,128]{4,3,2,1,0:T(2,128)S(1)}, f32[1,4,4,2,128]{4,3,2,1,0:T(2,128)}, u32[]{:S(2)}) copy-start(f32[1,4,4,2,128]{4,3,2,1,0:T(2,128)} %param.18) | copy-start | bytes 49156
  31.6 46.4 %copy-start.6 = (f32[4,4,2,128]{3,2,1,0:T(2,128)S(1)}, f32[4,4,2,128]{3,2,1,0:T(2,128)}, u32[]{:S(2)}) copy-start(f32[4,4,2,128]{3,2,1,0:T(2,128)} %param.16) | copy-start | bytes 49156
  64.4 1.2 %collective-permute-start.4 = (f32[4,4,2,128]{3,2,1,0:T(2,128)S(1)}, f32[4,4,2,128]{3,2,1,0:T(2,128)S(1)}, u32[]{:S(2)}, u32[]{:S(2)}) collective-permute-start(f32[4,4,2,128]{3,2,1,0:T(2,128)S(1)} %fusion.7), channel_id=1, source_target_pairs={{0,1},{1,0},{2,3},{3,2},{4,5},{5,4},{6,7},{7,6},{8,9},{9,8},{10,11... | collective-permute-start | bytes 49160 | tf_op jit(solution)/shard_map/ppermute | solution.py:256
  65.6 3.8 %collective-permute-start.5 = (f32[4,4,2,128]{3,2,1,0:T(2,128)S(1)}, f32[4,4,2,128]{3,2,1,0:T(2,128)S(1)}, u32[]{:S(2)}, u32[]{:S(2)}) collective-permute-start(f32[4,4,2,128]{3,2,1,0:T(2,128)S(1)} %add.104), channel_id=1, source_target_pairs={{0,2},{1,3},{2,0},{3,1},{4,6},{5,7},{6,4},{7,5},{8,10},{9,11},{10,... | collective-permute-start | bytes 49160 | tf_op jit(solution)/shard_map/ppermute | solution.py:256
  69.4 3.8 %collective-permute-start.6 = (f32[4,4,2,128]{3,2,1,0:T(2,128)S(1)}, f32[4,4,2,128]{3,2,1,0:T(2,128)S(1)}, u32[]{:S(2)}, u32[]{:S(2)}) collective-permute-start(f32[4,4,2,128]{3,2,1,0:T(2,128)S(1)} %add.106), channel_id=1, source_target_pairs={{0,4},{1,5},{2,6},{3,7},{4,0},{5,1},{6,2},{7,3},{8,12},{9,13},{10,... | collective-permute-start | bytes 49160 | tf_op jit(solution)/shard_map/ppermute | solution.py:256
  73.3 4.7 %collective-permute-start.7 = (f32[4,4,2,128]{3,2,1,0:T(2,128)S(1)}, f32[4,4,2,128]{3,2,1,0:T(2,128)S(1)}, u32[]{:S(2)}, u32[]{:S(2)}) collective-permute-start(f32[4,4,2,128]{3,2,1,0:T(2,128)S(1)} %add.108), channel_id=1, source_target_pairs={{0,8},{1,9},{2,10},{3,11},{4,12},{5,13},{6,14},{7,15},{8,0},{9,1},... | collective-permute-start | bytes 49160 | tf_op jit(solution)/shard_map/ppermute | solution.py:256

commit v12 on v10

--- a/solution.py
+++ b/solution.py
@@ -89,14 +89,12 @@
 
 def unet_body(
     first_ref, emb_u_ref, time_ref, pooled_ref, tproj_ref, wl_ref, same_ref, batch_ref,
-    wsp_hbm, wt_hbm, out_ref, wsp_ref, wt_ref, sems, *, count
+    wsp_hbm, wt_ref, out_ref, wsp_ref, sems, *, count
 ):
     rows, frames, cols, chans = first_ref.shape
     blocks = 2 * frames
     copy_sp = pltpu.make_async_copy(wsp_hbm, wsp_ref, sems.at[0])
     copy_sp.start()
-    copy_tm = pltpu.make_async_copy(wt_hbm, wt_ref, sems.at[1])
-    copy_tm.start()
     same = same_ref[...]
     batch_mix = batch_ref[...]
     hi = lax.Precision.HIGH
@@ -173,8 +171,6 @@
         state = (x + conv_sp(normed, section)).astype(jnp.bfloat16)
         x = state.astype(jnp.float32)
         normed = norm_silu(x, batch_mix, per_sample)
-        if section == 0:
-            copy_tm.wait()
         state = (x + conv_tm(normed, section)).astype(jnp.bfloat16)
     last = norm_silu(state.astype(jnp.float32), None, per_frame)
     x0 = last[0].reshape(blocks * cols, chans)
@@ -217,12 +213,11 @@
     return pl.pallas_call(
         functools.partial(unet_body, count=float(count)),
         out_shape=jax.ShapeDtypeStruct((rows, padded, blocks * cols), jnp.float32),
-        in_specs=[vmem] * 8 + [anywhere, anywhere],
+        in_specs=[vmem] * 8 + [anywhere, vmem],
         out_specs=vmem,
         scratch_shapes=[
             pltpu.VMEM(spatial_weights.shape, spatial_weights.dtype),
-            pltpu.VMEM(temporal_weights.shape, temporal_weights.dtype),
-            pltpu.SemaphoreType.DMA((2,)),
+            pltpu.SemaphoreType.DMA((1,)),
         ],
         compiler_params=pltpu.CompilerParams(vmem_limit_bytes=100 * 1024 * 1024 // 2),
         cost_estimate=pl.CostEstimate(

time: 72.9 us -> 71.1 us (0.975)
  Pallas kernels: 32.6 us -> 30.8 us
    pallas_call x1, Pallas kernels: 32.6 us -> 30.8 us  [unet(): pl.pallas_call(functools.partial(unet_body, count=float(count)), out_shap...]
  transfers between devices with their start and end apart: 8 -> 8, of which waited for: 6 -> 6; matrix products, arithmetic and copies ran while one was open for 6% -> 7% of each run, Pallas kernels for 0% -> 0%
where the time goes in v12:
time: 71.1 us; the launch traced here: 70.9 us
  Pallas kernels  30.8 us (43%)
  waiting for transfers between devices  13.9 us (20%)
  starting transfers between devices  11.1 us (16%)
  matrix products  6.2 us (9%)
  between operations  3.44 us (5%)
  other arithmetic  3.28 us (5%)
  local copies, waits for them, and re-layouts  2.15 us (3%)
    pallas_call x1, Pallas kernels, unet(): pl.pallas_call(functools.partial(unet_body, count=float(count)), out_shap...  30.8 us
    ppermute x4, waiting for transfers between devices, butterfly_scan(): got = lax.ppermute(total, axis, [(i, i ^ k) for i in range(peers)])  9.83 us
    ppermute x4, starting transfers between devices, butterfly_sum(): x = x + lax.ppermute(x, axis, [(i, i ^ k) for i in range(peers)])  7.21 us
    ppermute x4, waiting for transfers between devices, butterfly_sum(): x = x + lax.ppermute(x, axis, [(i, i ^ k) for i in range(peers)])  4.04 us
    ppermute x4, starting transfers between devices, butterfly_scan(): got = lax.ppermute(total, axis, [(i, i ^ k) for i in range(peers)])  3.88 us
    dot_general x1, matrix products, local(): jnp.dot(counts, token_table, preferred_element_type=jnp.float32)[0]  3.73 us
    unnamed x22, local copies, waits for them, and re-layouts  1.77 us
    dot_general x1, matrix products, conv_lifted(): lax.dot_general(windows, stacked, (((0,), (1,)), ((), ())), preferred_ele...  1.56 us
  transfers between devices with their start and end apart: 8, of which 6 were waited for; matrix products, arithmetic and copies ran while one was open for 7% of the time, Pallas kernels for 0%

profile of v12, /device:TPU:0, one launch (start us, length us, event | category | flops | bytes accessed | tf_op | source)
XLA Modules:
  0.0 70.9 jit_solution(5710994868611526511)
XLA Ops:
  0.7 0.8 %broadcast_subtract_fusion = s32[77]{0:T(128)S(1)} fusion(s32[77]{0:T(128)} %param.15, s32[]{:T(128)S(6)} %mul.88), kind=kLoop, calls=%fused_computation.51 | loop fusion | flops 77 | bytes 620 | tf_op jit(solution)/shard_map/sub | solution.py:276
  1.5 0.2 convert_reduce_fusion
  1.7 3.7 %fusion.14 = f32[1,1024]{1,0:T(1,128)S(1)} fusion(bf16[3088,1]{0,1:T(2,128)(2,1)S(1)} %reshape.106, bf16[3088,1024]{1,0:T(8,128)(2,1)} %param.19), kind=kOutput, calls=%fused_computation.53 | convolution fusion | flops 6324224 | bytes 6334496 | tf_op jit(solution)/shard_map/dot_general | solution.py:279
  5.5 4.0 %collective-permute-start = (f32[1024]{0:T(1024)S(1)}, f32[1024]{0:T(1024)S(1)}, u32[]{:S(2)}, u32[]{:S(2)}) collective-permute-start(f32[1024]{0:T(1024)S(1)} %bitcast.54), channel_id=1, source_target_pairs={{0,8},{1,9},{2,10},{3,11},{4,12},{5,13},{6,14},{7,15},{8,0},{9,1},... | collective-permute-start | bytes 12296 | tf_op jit(solution)/shard_map/ppermute | solution.py:237
  9.5 0.1 pad_slice_fusion
  10.3 0.1 sine_convert_fusion
  10.4 0.1 pad_maximum_fusion
  10.5 0.2 convolution_reduce_fusion
  10.8 0.6 reduce_sum.27
  12.0 0.6 multiply_reduce_fusion
  13.3 0.1 compare_convert_fusion.same_ref
  13.4 0.2 concatenate.11
  13.6 1.6 %convolution_bitcast_fusion.first_ref = f32[2,4,128,320]{3,2,1,0:T(8,128)} fusion(bf16[320,36,1,1]{0,1,2,3:T(8,128)(2,1)S(1)} %reshape.99, bf16[36,4,2,128]{3,0,2,1:T(8,128)(2,1)S(1)} %concatenate.11), kind=kOutput, calls=%fused_computation | convolution fusion | flops 23592960 | bytes 1407488 | tf_op jit(solution)/shard_map/dot_general | solution.py:73
  15.1 0.3 fusion.13
  15.5 1.6 %collective-permute-start.1 = (f32[1024]{0:T(1024)S(1)}, f32[1024]{0:T(1024)S(1)}, u32[]{:S(2)}, u32[]{:S(2)}) collective-permute-start(f32[1024]{0:T(1024)S(1)} %add.100), channel_id=1, source_target_pairs={{0,4},{1,5},{2,6},{3,7},{4,0},{5,1},{6,2},{7,3},{8,12},{9,13},{10,... | collective-permute-start | bytes 12296 | tf_op jit(solution)/shard_map/ppermute | solution.py:237
  17.2 2.0 %collective-permute-done.1 = f32[1024]{0:T(1024)S(1)} collective-permute-done((f32[1024]{0:T(1024)S(1)}, f32[1024]{0:T(1024)S(1)}, u32[]{:S(2)}, u32[]{:S(2)}) %collective-permute-start.1) | collective-permute-done | bytes 4128 | tf_op jit(solution)/shard_map/ppermute | solution.py:237
  19.2 1.5 %collective-permute-start.2 = (f32[1024]{0:T(1024)S(1)}, f32[1024]{0:T(1024)S(1)}, u32[]{:S(2)}, u32[]{:S(2)}) collective-permute-start(f32[1024]{0:T(1024)S(1)} %add.101), channel_id=1, source_target_pairs={{0,2},{1,3},{2,0},{3,1},{4,6},{5,7},{6,4},{7,5},{8,10},{9,11},{10,... | collective-permute-start | bytes 12296 | tf_op jit(solution)/shard_map/ppermute | solution.py:237
  20.7 0.1 compare_convert_fusion.1.batch_ref
  20.8 2.0 %collective-permute-done.2 = f32[1024]{0:T(1024)S(1)} collective-permute-done((f32[1024]{0:T(1024)S(1)}, f32[1024]{0:T(1024)S(1)}, u32[]{:S(2)}, u32[]{:S(2)}) %collective-permute-start.2) | collective-permute-done | bytes 4128 | tf_op jit(solution)/shard_map/ppermute | solution.py:237
  22.8 0.3 convolution_reduce_fusion.1
  23.1 0.4 copy.22.tproj_ref
  24.1 1.4 %copy-done.1 = bf16[2,3,320,320]{3,2,1,0:T(8,128)(2,1)S(1)} copy-done((bf16[2,3,320,320]{3,2,1,0:T(8,128)(2,1)S(1)}, bf16[2,3,320,320]{3,2,1,0:T(8,128)(2,1)}, u32[]{:S(2)}) %copy-start.1) | copy-done | bytes 1228824
  25.5 30.8 %shard_map.149 = f32[2,16,1024]{2,1,0:T(8,128)S(1)} custom-call(f32[2,4,128,320]{3,2,1,0:T(8,128)} %convolution_bitcast_fusion.first_ref, f32[1,320]{1,0:T(1,128)S(1)} %add.99.emb_u_ref, f32[1,320]{1,0:T(1,128)S(1)} %get-tuple-element.13.time_ref, f32[1,1024]{1,0:T(1,128)S(1)} %bitcast.49, bf16[1024,320]{1,0:T(8,128)(2,1)S(1)} %copy.22.tproj_ref, ...), custom_call_target="tpu_custom_call" | custom-call | flops 7549747200 | bytes 6225920 | tf_op jit(solution)/shard_map/pallas_call | solution.py:213
  56.5 0.6 collective-permute-start.4
  57.0 0.8 %collective-permute-done.4 = f32[4,4,2,128]{3,2,1,0:T(2,128)S(1)} collective-permute-done((f32[4,4,2,128]{3,2,1,0:T(2,128)S(1)}, f32[4,4,2,128]{3,2,1,0:T(2,128)S(1)}, u32[]{:S(2)}, u32[]{:S(2)}) %collective-permute-start.4) | collective-permute-done | bytes 16416 | tf_op jit(solution)/shard_map/ppermute | solution.py:251
  57.9 1.6 %collective-permute-start.5 = (f32[4,4,2,128]{3,2,1,0:T(2,128)S(1)}, f32[4,4,2,128]{3,2,1,0:T(2,128)S(1)}, u32[]{:S(2)}, u32[]{:S(2)}) collective-permute-start(f32[4,4,2,128]{3,2,1,0:T(2,128)S(1)} %add.107), channel_id=1, source_target_pairs={{0,2},{1,3},{2,0},{3,1},{4,6},{5,7},{6,4},{7,5},{8,10},{9,11},{10,... | collective-permute-start | bytes 49160 | tf_op jit(solution)/shard_map/ppermute | solution.py:251
  59.5 2.2 %collective-permute-done.5 = f32[4,4,2,128]{3,2,1,0:T(2,128)S(1)} collective-permute-done((f32[4,4,2,128]{3,2,1,0:T(2,128)S(1)}, f32[4,4,2,128]{3,2,1,0:T(2,128)S(1)}, u32[]{:S(2)}, u32[]{:S(2)}) %collective-permute-start.5) | collective-permute-done | bytes 16416 | tf_op jit(solution)/shard_map/ppermute | solution.py:251
  61.7 1.6 %collective-permute-start.6 = (f32[4,4,2,128]{3,2,1,0:T(2,128)S(1)}, f32[4,4,2,128]{3,2,1,0:T(2,128)S(1)}, u32[]{:S(2)}, u32[]{:S(2)}) collective-permute-start(f32[4,4,2,128]{3,2,1,0:T(2,128)S(1)} %add.109), channel_id=1, source_target_pairs={{0,4},{1,5},{2,6},{3,7},{4,0},{5,1},{6,2},{7,3},{8,12},{9,13},{10,... | collective-permute-start | bytes 49160 | tf_op jit(solution)/shard_map/ppermute | solution.py:251
  63.3 2.2 %collective-permute-done.6 = f32[4,4,2,128]{3,2,1,0:T(2,128)S(1)} collective-permute-done((f32[4,4,2,128]{3,2,1,0:T(2,128)S(1)}, f32[4,4,2,128]{3,2,1,0:T(2,128)S(1)}, u32[]{:S(2)}, u32[]{:S(2)}) %collective-permute-start.6) | collective-permute-done | bytes 16416 | tf_op jit(solution)/shard_map/ppermute | solution.py:251
  65.5 0.1 collective-permute-start.7
  65.6 4.6 %collective-permute-done.7 = f32[4,4,2,128]{3,2,1,0:T(2,128)S(1)} collective-permute-done((f32[4,4,2,128]{3,2,1,0:T(2,128)S(1)}, f32[4,4,2,128]{3,2,1,0:T(2,128)S(1)}, u32[]{:S(2)}, u32[]{:S(2)}) %collective-permute-start.7) | collective-permute-done | bytes 16416 | tf_op jit(solution)/shard_map/ppermute | solution.py:251
  70.2 0.6 add_add_fusion
  (46 shorter events, 0.3 us)
Async XLA Ops:
  0.6 9.8 %copy-start = (bf16[320,1280]{1,0:T(8,128)(2,1)S(1)}, bf16[320,1280]{1,0:T(8,128)(2,1)}, u32[]{:S(2)}) copy-start(bf16[320,1280]{1,0:T(8,128)(2,1)} %param.21) | copy-start | bytes 2457604
  0.6 8.9 %copy-start.4 = (f32[1,4,4,2,128]{4,3,2,1,0:T(2,128)S(1)}, f32[1,4,4,2,128]{4,3,2,1,0:T(2,128)}, u32[]{:S(2)}) copy-start(f32[1,4,4,2,128]{4,3,2,1,0:T(2,128)} %param.17) | copy-start | bytes 49156
  0.7 9.0 %copy-start.6 = (bf16[9,320,4]{1,2,0:T(4,128)(2,1)S(1)}, bf16[9,320,4]{1,2,0:T(4,128)(2,1)}, u32[]{:S(2)}) copy-start(bf16[9,320,4]{1,2,0:T(4,128)(2,1)} %param.24) | copy-start | bytes 69124
  0.7 10.1 %copy-start.5 = (f32[1024]{0:T(1024)S(1)}, f32[1024]{0:T(1024)}, u32[]{:S(2)}) copy-start(f32[1024]{0:T(1024)} %param.20) | copy-start | bytes 12292
  0.7 14.5 %copy-start.3 = (bf16[1280,320]{0,1:T(8,128)(2,1)S(1)}, bf16[1280,320]{0,1:T(8,128)(2,1)}, u32[]{:S(2)}) copy-start(bf16[1280,320]{0,1:T(8,128)(2,1)} %param.22) | copy-start | bytes 2457604
  0.7 22.1 %copy-start.2 = (bf16[1024,320]{0,1:T(8,128)(2,1)S(1)}, bf16[1024,320]{0,1:T(8,128)(2,1)}, u32[]{:S(2)}) copy-start(bf16[1024,320]{0,1:T(8,128)(2,1)} %param.23) | copy-start | bytes 1966084
  1.7 22.3 %copy-start.7 = (bf16[9,4,320]{2,1,0:T(4,128)(2,1)S(1)}, bf16[9,4,320]{2,1,0:T(4,128)(2,1)}, u32[]{:S(2)}) copy-start(bf16[9,4,320]{2,1,0:T(4,128)(2,1)} %param.27) | copy-start | bytes 69124
  5.5 10.0 %collective-permute-start = (f32[1024]{0:T(1024)S(1)}, f32[1024]{0:T(1024)S(1)}, u32[]{:S(2)}, u32[]{:S(2)}) collective-permute-start(f32[1024]{0:T(1024)S(1)} %bitcast.54), channel_id=1, source_target_pairs={{0,8},{1,9},{2,10},{3,11},{4,12},{5,13},{6,14},{7,15},{8,0},{9,1},... | collective-permute-start | bytes 12296 | tf_op jit(solution)/shard_map/ppermute | solution.py:237
  15.5 3.7 %collective-permute-start.1 = (f32[1024]{0:T(1024)S(1)}, f32[1024]{0:T(1024)S(1)}, u32[]{:S(2)}, u32[]{:S(2)}) collective-permute-start(f32[1024]{0:T(1024)S(1)} %add.100), channel_id=1, source_target_pairs={{0,4},{1,5},{2,6},{3,7},{4,0},{5,1},{6,2},{7,3},{8,12},{9,13},{10,... | collective-permute-start | bytes 12296 | tf_op jit(solution)/shard_map/ppermute | solution.py:237
  19.2 3.6 %collective-permute-start.2 = (f32[1024]{0:T(1024)S(1)}, f32[1024]{0:T(1024)S(1)}, u32[]{:S(2)}, u32[]{:S(2)}) collective-permute-start(f32[1024]{0:T(1024)S(1)} %add.101), channel_id=1, source_target_pairs={{0,2},{1,3},{2,0},{3,1},{4,6},{5,7},{6,4},{7,5},{8,10},{9,11},{10,... | collective-permute-start | bytes 12296 | tf_op jit(solution)/shard_map/ppermute | solution.py:237
  22.8 1.3 %collective-permute-start.3 = (f32[1024]{0:T(1024)S(1)}, f32[1024]{0:T(1024)S(1)}, u32[]{:S(2)}, u32[]{:S(2)}) collective-permute-start(f32[1024]{0:T(1024)S(1)} %add.102), channel_id=1, source_target_pairs={{0,1},{1,0},{2,3},{3,2},{4,5},{5,4},{6,7},{7,6},{8,9},{9,8},{10,11... | collective-permute-start | bytes 12296 | tf_op jit(solution)/shard_map/ppermute | solution.py:237
  24.1 1.4 %copy-start.1 = (bf16[2,3,320,320]{3,2,1,0:T(8,128)(2,1)S(1)}, bf16[2,3,320,320]{3,2,1,0:T(8,128)(2,1)}, u32[]{:S(2)}) copy-start(bf16[2,3,320,320]{3,2,1,0:T(8,128)(2,1)} %wt_ref.1) | copy-start | bytes 3686404
  25.5 30.9 %copy-start.8 = (f32[1,4,4,2,128]{4,3,2,1,0:T(2,128)S(1)}, f32[1,4,4,2,128]{4,3,2,1,0:T(2,128)}, u32[]{:S(2)}) copy-start(f32[1,4,4,2,128]{4,3,2,1,0:T(2,128)} %param.18) | copy-start | bytes 49156
  25.5 44.7 %copy-start.9 = (f32[4,4,2,128]{3,2,1,0:T(2,128)S(1)}, f32[4,4,2,128]{3,2,1,0:T(2,128)}, u32[]{:S(2)}) copy-start(f32[4,4,2,128]{3,2,1,0:T(2,128)} %param.16) | copy-start | bytes 49156
  56.5 1.4 %collective-permute-start.4 = (f32[4,4,2,128]{3,2,1,0:T(2,128)S(1)}, f32[4,4,2,128]{3,2,1,0:T(2,128)S(1)}, u32[]{:S(2)}, u32[]{:S(2)}) collective-permute-start(f32[4,4,2,128]{3,2,1,0:T(2,128)S(1)} %fusion.7), channel_id=1, source_target_pairs={{0,1},{1,0},{2,3},{3,2},{4,5},{5,4},{6,7},{7,6},{8,9},{9,8},{10,11... | collective-permute-start | bytes 49160 | tf_op jit(solution)/shard_map/ppermute | solution.py:251
  57.9 3.8 %collective-permute-start.5 = (f32[4,4,2,128]{3,2,1,0:T(2,128)S(1)}, f32[4,4,2,128]{3,2,1,0:T(2,128)S(1)}, u32[]{:S(2)}, u32[]{:S(2)}) collective-permute-start(f32[4,4,2,128]{3,2,1,0:T(2,128)S(1)} %add.107), channel_id=1, source_target_pairs={{0,2},{1,3},{2,0},{3,1},{4,6},{5,7},{6,4},{7,5},{8,10},{9,11},{10,... | collective-permute-start | bytes 49160 | tf_op jit(solution)/shard_map/ppermute | solution.py:251
  61.7 3.8 %collective-permute-start.6 = (f32[4,4,2,128]{3,2,1,0:T(2,128)S(1)}, f32[4,4,2,128]{3,2,1,0:T(2,128)S(1)}, u32[]{:S(2)}, u32[]{:S(2)}) collective-permute-start(f32[4,4,2,128]{3,2,1,0:T(2,128)S(1)} %add.109), channel_id=1, source_target_pairs={{0,4},{1,5},{2,6},{3,7},{4,0},{5,1},{6,2},{7,3},{8,12},{9,13},{10,... | collective-permute-start | bytes 49160 | tf_op jit(solution)/shard_map/ppermute | solution.py:251
  65.5 4.7 %collective-permute-start.7 = (f32[4,4,2,128]{3,2,1,0:T(2,128)S(1)}, f32[4,4,2,128]{3,2,1,0:T(2,128)S(1)}, u32[]{:S(2)}, u32[]{:S(2)}) collective-permute-start(f32[4,4,2,128]{3,2,1,0:T(2,128)S(1)} %add.111), channel_id=1, source_target_pairs={{0,8},{1,9},{2,10},{3,11},{4,12},{5,13},{6,14},{7,15},{8,0},{9,1},... | collective-permute-start | bytes 49160 | tf_op jit(solution)/shard_map/ppermute | solution.py:251
